TPU v7x, 32 devices: a whole 2x2x4 slice. The times are simulated.
32 devices in a mesh: strip: 8 (over z, y), blk: 2 (over x), dp: 2 (over core).
Axes of the slice: x: 2, y: 2, z: 4, core: 2. Of those that a mesh axis runs over, the one named last changes fastest.
Arguments:
- fields: bfloat16 [4, 256, 128, 128], P('dp', 'blk', 'strip'), may hold values from -6 to 6
- cotangent: bfloat16 [4, 256, 128, 128], P('dp', 'blk', 'strip'), may hold values from -6 to 6
- kernel_one: float32 [9, 128], replicated, may hold values from -2 to 2
- weight_one: bfloat16 [128, 128], replicated, may hold values from -0.5 to 0.5
- kernel_two: float32 [9, 128], replicated, may hold values from -2 to 2
- weight_two: bfloat16 [128, 128], replicated, may hold values from -0.5 to 0.5
- seam_flags: int32 [2, 8], replicated, may hold values from 0 to 1, as said below
Outputs:
- grad_fields: bfloat16 [4, 256, 128, 128], P('dp', 'blk', 'strip')
- grad_kernel_one: float32 [9, 128], replicated
- grad_weight_one: float32 [128, 128], replicated
- grad_kernel_two: float32 [9, 128], replicated
- grad_weight_two: float32 [128, 128], replicated
Inputs may be any that keep to these rules, and one draw needn't show every extreme that they name: seam_flags[q, s] is 0 unless s is a multiple of 2 (a seam between two faces); at such a seam it is 1 where the row order reverses.
All inputs are finite; a program needn't handle non-finite values.
Results may differ from a plain program's by a relative error of at most 0.0056.
Values may be sent and summed in bfloat16 or wider, within the bound.
No kernel may reach another device: no remote copies, remote signals or barrier semaphores. Data moves between devices by JAX's collectives and lax.ppermute only.
A program may use at most 128 MiB of HBM per device.

v0:
```python
import jax
import jax.numpy as jnp
from jax import lax
from jax.sharding import PartitionSpec as P

COL_DEV = 16


def with_halo(shard, sides, width, wrap):
    for axis, dim in sides:
        count, length = (lax.axis_size(axis), shard.shape[dim])
        up = [(i, (i + 1) % count) for i in range(count if wrap else count - 1)]
        down = [(j, i) for i, j in up]
        last = lax.slice_in_dim(shard, length - width, length, axis=dim)
        first = lax.slice_in_dim(shard, 0, width, axis=dim)
        before = lax.ppermute(last, axis, up)
        after = lax.ppermute(first, axis, down)
        shard = jnp.concatenate([before, shard, after], axis=dim)
    return shard


def seam_bits(seam_flags, local_strips):
    circle_idx = lax.axis_index("blk")
    strip_idx = lax.axis_index("strip")
    strip_total = seam_flags.shape[1]
    circle_flags = lax.dynamic_index_in_dim(seam_flags, circle_idx, 0, keepdims=False)
    global_strip = strip_idx * local_strips + jnp.arange(local_strips, dtype=jnp.int32)
    next_strip = (global_strip + 1) % strip_total
    left_flip = jnp.take(circle_flags, global_strip) == 1
    right_flip = jnp.take(circle_flags, next_strip) == 1
    return (left_flip[None, None, :, None, None], right_flip[None, None, :, None, None])


def extend(values, margin, seams):
    batch_size, row_count, col_total, channels = values.shape
    local_strips = col_total // COL_DEV
    strips = values.reshape(batch_size, row_count, local_strips, COL_DEV, channels)
    rim_cols = jnp.concatenate(
        [strips[:, :, 0, :margin], strips[:, :, local_strips - 1, COL_DEV - margin :]], axis=2
    )
    padded = with_halo(rim_cols, (("strip", 2),), margin, True)
    halo_left = padded[:, :, :margin][:, :, None]
    halo_right = padded[:, :, 3 * margin :][:, :, None]
    from_left = jnp.concatenate(
        [halo_left, strips[:, :, : local_strips - 1, COL_DEV - margin :]], axis=2
    )
    from_right = jnp.concatenate([strips[:, :, 1:, :margin], halo_right], axis=2)
    from_left = jnp.where(seams[0], from_left[:, ::-1], from_left)
    from_right = jnp.where(seams[1], from_right[:, ::-1], from_right)
    widened = jnp.concatenate([from_left, strips, from_right], axis=3)
    rim_rows = jnp.concatenate([widened[:, :margin], widened[:, row_count - margin :]], axis=1)
    padded_rows = with_halo(rim_rows, (("blk", 1),), margin, False)
    return jnp.concatenate([padded_rows[:, :margin], widened, padded_rows[:, 3 * margin :]], axis=1)


def depthwise(widened, kernel, margin, row_count):
    batch_size, unused_rows, local_strips, unused_cols, channels = widened.shape
    summed = jnp.zeros((batch_size, row_count, local_strips, COL_DEV, channels), jnp.float32)
    for tap_row in range(3):
        for tap_col in range(3):
            tap_slice = widened[
                :,
                tap_row * margin : tap_row * margin + row_count,
                :,
                tap_col * margin : tap_col * margin + COL_DEV,
            ]
            summed = summed + tap_slice * kernel[3 * tap_row + tap_col]
    return summed.reshape(batch_size, row_count, local_strips * COL_DEV, channels)


def conv_back(widened, kernel, grad_pre, margin):
    batch_size, row_count, col_total, channels = grad_pre.shape
    local_strips = col_total // COL_DEV
    grad_strips = grad_pre.reshape(batch_size, row_count, local_strips, COL_DEV, channels)
    grad_wide = jnp.zeros(widened.shape, jnp.float32)
    tap_sums = []
    for tap_row in range(3):
        for tap_col in range(3):
            row_start = tap_row * margin
            col_start = tap_col * margin
            tap_slice = widened[
                :, row_start : row_start + row_count, :, col_start : col_start + COL_DEV
            ]
            tap_sums.append(jnp.sum(tap_slice * grad_strips, axis=(0, 1, 2, 3)))
            placed = jnp.pad(
                kernel[3 * tap_row + tap_col] * grad_strips,
                (
                    (0, 0),
                    (row_start, 2 * margin - row_start),
                    (0, 0),
                    (col_start, 2 * margin - col_start),
                    (0, 0),
                ),
            )
            grad_wide = grad_wide + placed
    return (jnp.stack(tap_sums), grad_wide)


def fold_back(grad_wide, margin, seams):
    batch_size, wide_rows, local_strips, wide_cols, channels = grad_wide.shape
    row_count = wide_rows - 2 * margin
    rim_rows = jnp.concatenate([grad_wide[:, :margin], grad_wide[:, wide_rows - margin :]], axis=1)
    padded = with_halo(rim_rows.astype(jnp.bfloat16), (("blk", 1),), margin, False).astype(
        rim_rows.dtype
    )
    core_rows = grad_wide[:, margin : wide_rows - margin]
    no_pad = (0, 0)
    core_rows = core_rows + jnp.pad(
        padded[:, :margin], (no_pad, (0, row_count - margin), no_pad, no_pad, no_pad)
    )
    core_rows = core_rows + jnp.pad(
        padded[:, 3 * margin :], (no_pad, (row_count - margin, 0), no_pad, no_pad, no_pad)
    )
    left_part = core_rows[:, :, :, :margin]
    right_part = core_rows[:, :, :, wide_cols - margin :]
    left_part = jnp.where(seams[0], left_part[:, ::-1], left_part)
    right_part = jnp.where(seams[1], right_part[:, ::-1], right_part)
    rim_cols = jnp.concatenate([left_part[:, :, 0], right_part[:, :, local_strips - 1]], axis=2)
    padded_cols = with_halo(rim_cols.astype(jnp.bfloat16), (("strip", 2),), margin, True).astype(
        rim_cols.dtype
    )
    from_left_dev = padded_cols[:, :, :margin][:, :, None]
    from_right_dev = padded_cols[:, :, 3 * margin :][:, :, None]
    add_first = jnp.concatenate([from_left_dev, right_part[:, :, : local_strips - 1]], axis=2)
    add_last = jnp.concatenate([left_part[:, :, 1:], from_right_dev], axis=2)
    inner_cols = core_rows[:, :, :, margin : wide_cols - margin]
    inner_cols = inner_cols + jnp.pad(
        add_first, (no_pad, no_pad, no_pad, (0, COL_DEV - margin), no_pad)
    )
    inner_cols = inner_cols + jnp.pad(
        add_last, (no_pad, no_pad, no_pad, (COL_DEV - margin, 0), no_pad)
    )
    return inner_cols.reshape(batch_size, row_count, local_strips * COL_DEV, channels)


def pointwise(act, weight):
    channels = act.shape[-1]
    flat_act = act.reshape(-1, channels)
    return jnp.dot(flat_act, weight, preferred_element_type=jnp.float32).reshape(act.shape)


def block_back(widened, pre_val, act, grad_out, kernel, weight, margin, seams):
    channels = act.shape[-1]
    flat_grad = grad_out.reshape(-1, channels)
    d_weight = lax.dot_general(
        act.reshape(-1, channels),
        flat_grad,
        (((0,), (0,)), ((), ())),
        preferred_element_type=jnp.float32,
    )
    d_act = lax.dot_general(
        flat_grad, weight, (((1,), (1,)), ((), ())), preferred_element_type=jnp.float32
    ).reshape(pre_val.shape)
    logistic = jax.nn.sigmoid(pre_val)
    d_pre = d_act * logistic * (1.0 + pre_val * (1.0 - logistic))
    d_kernel, grad_wide = conv_back(widened, kernel, d_pre, margin)
    d_values = fold_back(grad_wide, margin, seams)
    grad_in = (grad_out.astype(jnp.float32) + d_values).astype(jnp.bfloat16)
    return (grad_in, d_kernel, d_weight)


def shards(fields, cotangent, kernel_one, weight_one, kernel_two, weight_two, seam_flags):
    batch_size, row_count, col_count, channels = fields.shape
    seams = seam_bits(seam_flags, col_count // COL_DEV)
    cells_all = (
        batch_size
        * row_count
        * col_count
        * lax.axis_size("strip")
        * lax.axis_size("blk")
        * lax.axis_size("dp")
    )
    factor = float(cells_all) ** (-0.5)
    wide_one = extend(fields, 1, seams)
    pre_one = depthwise(wide_one, kernel_one, 1, row_count)
    act_one = jax.nn.silu(pre_one).astype(jnp.bfloat16)
    hidden = (fields.astype(jnp.float32) + pointwise(act_one, weight_one)).astype(jnp.bfloat16)
    wide_two = extend(hidden, 2, seams)
    pre_two = depthwise(wide_two, kernel_two, 2, row_count)
    act_two = jax.nn.silu(pre_two).astype(jnp.bfloat16)
    grad_hidden, dk_two, dw_two = block_back(
        wide_two, pre_two, act_two, cotangent, kernel_two, weight_two, 2, seams
    )
    grad_fields, dk_one, dw_one = block_back(
        wide_one, pre_one, act_one, grad_hidden, kernel_one, weight_one, 1, seams
    )
    dk_one, dw_one, dk_two, dw_two = lax.psum(
        (dk_one, dw_one, dk_two, dw_two), ("strip", "blk", "dp")
    )
    return (grad_fields, dk_one * factor, dw_one * factor, dk_two * factor, dw_two * factor)


def solution(mesh):
    return jax.shard_map(
        shards,
        mesh=mesh,
        in_specs=(
            P("dp", "blk", "strip", None),
            P("dp", "blk", "strip", None),
            P(),
            P(),
            P(),
            P(),
            P(),
        ),
        out_specs=(P("dp", "blk", "strip", None), P(), P(), P(), P()),
        check_vma=False,
    )
```

profile of v0, /device:TPU:0, one launch (start us, length us, event | category | flops | bytes accessed | tf_op | source)
XLA Modules:
  0.0 263.6 jit_solution(16309442129639962826)
XLA Ops:
  7.2 1.5 copy.110
  8.8 3.0 %collective-permute-start = (bf16[2,128,1,128]{3,1,0,2:T(8,128)(2,1)S(1)}, bf16[2,128,1,128]{3,1,0,2:T(8,128)(2,1)S(1)}, u32[]{:S(2)}, u32[]{:S(2)}) collective-permute-start(bf16[2,128,1,128]{3,1,0,2:T(8,128)(2,1)S(1)} %get-tuple-element.116), channel_id=1, source_target_pairs={{0,4},{4,8},{8,12},{12,16},{16,20},{20,24},{24,28},{28,0},{1,5},{5... | collective-permute-start | bytes 196616 | tf_op jit(solution)/shard_map/ppermute | solution.py:16
  11.8 3.1 %collective-permute-start.1 = (bf16[2,128,1,128]{3,1,0,2:T(8,128)(2,1)S(1)}, bf16[2,128,1,128]{3,1,0,2:T(8,128)(2,1)S(1)}, u32[]{:S(2)}, u32[]{:S(2)}) collective-permute-start(bf16[2,128,1,128]{3,1,0,2:T(8,128)(2,1)S(1)} %get-tuple-element.117), channel_id=1, source_target_pairs={{4,0},{8,4},{12,8},{16,12},{20,16},{24,20},{28,24},{0,28},{5,1},{9... | collective-permute-start | bytes 196616 | tf_op jit(solution)/shard_map/ppermute | solution.py:17
  17.6 3.5 %collective-permute-start.2 = (bf16[2,1,1,18,128]{4,1,3,0,2:T(2,128)(2,1)S(1)}, bf16[2,1,1,18,128]{4,1,3,0,2:T(2,128)(2,1)S(1)}, u32[]{:S(2)}, u32[]{:S(2)}) collective-permute-start(bf16[2,1,1,18,128]{4,1,3,0,2:T(2,128)(2,1)S(1)} %get-tuple-element.112), channel_id=1, source_target_pairs={{0,2},{1,3},{4,6},{5,7},{8,10},{9,11},{12,14},{13,15},{16,18},{17,... | collective-permute-start | bytes 27656 | tf_op jit(solution)/shard_map/ppermute | solution.py:16
  21.2 1.3 collective-permute-start.3
  22.6 4.2 %collective-permute-done.3 = bf16[2,1,1,18,128]{4,1,3,0,2:T(2,128)(2,1)S(1)} collective-permute-done((bf16[2,1,1,18,128]{4,1,3,0,2:T(2,128)(2,1)S(1)}, bf16[2,1,1,18,128]{4,1,3,0,2:T(2,128)(2,1)S(1)}, u32[]{:S(2)}, u32[]{:S(2)}) %collective-permute-start.3) | collective-permute-done | bytes 9248 | tf_op jit(solution)/shard_map/ppermute | solution.py:17
  27.6 3.9 %multiply_convert_fusion.1 = (bf16[2,128,16,128]{3,1,2,0:T(8,128)(2,1)S(1)}, f32[2,128,16,128]{3,1,2,0:T(8,128)}) fusion(f32[128]{0:T(128)S(1)} %get-tuple-element.142, bf16[2,129,1,18,128]{4,1,3,0,2:T(8,128)(2,1)S(1)} %get-tuple-element.111, f32[128]{0:T(128)S(1)} %get-tuple-element.143, f32[128]{0:T(128)S(1)} %get-tuple-element.136, ...), kind=kLoop, calls=%fused_computation.114 | loop fusion | flops 17301504 | bytes 11670016 | tf_op jit(solution)/shard_map/convert_element_type | solution.py:176
  31.5 1.0 copy-done.9
  33.7 1.0 collective-permute-start.4
  34.7 3.7 %collective-permute-start.5 = (bf16[2,128,2,128]{3,1,2,0:T(8,128)(2,1)}, bf16[2,128,2,128]{3,1,2,0:T(8,128)(2,1)}, u32[]{:S(2)}, u32[]{:S(2)}) collective-permute-start(bf16[2,128,2,128]{3,1,2,0:T(8,128)(2,1)} %get-tuple-element.115), channel_id=1, source_target_pairs={{4,0},{8,4},{12,8},{16,12},{20,16},{24,20},{28,24},{0,28},{5,1},{9... | collective-permute-start | bytes 393224 | tf_op jit(solution)/shard_map/ppermute | solution.py:17
  38.4 2.9 %collective-permute-done.4 = bf16[2,128,2,128]{3,1,2,0:T(8,128)(2,1)S(1)} collective-permute-done((bf16[2,128,2,128]{3,1,2,0:T(8,128)(2,1)S(1)}, bf16[2,128,2,128]{3,1,2,0:T(8,128)(2,1)S(1)}, u32[]{:S(2)}, u32[]{:S(2)}) %collective-permute-start.4) | collective-permute-done | bytes 131104 | tf_op jit(solution)/shard_map/ppermute | solution.py:16
  42.0 1.3 reverse.14
  44.2 2.8 %reverse.15 = bf16[2,128,2,128]{3,1,2,0:T(8,128)(2,1)} reverse(bf16[2,128,2,128]{3,1,2,0:T(8,128)(2,1)} %collective-permute-done.5), dimensions={1} | reverse | bytes 262144 | tf_op jit(solution)/shard_map/reverse.3
  48.0 1.6 collective-permute-start.6
  49.6 1.3 collective-permute-start.7
  50.9 1.0 slice_bitcast_fusion.21
  51.9 3.4 %collective-permute-done.7 = bf16[2,2,1,20,128]{4,1,3,0,2:T(2,128)(2,1)S(1)} collective-permute-done((bf16[2,2,1,20,128]{4,1,3,0,2:T(2,128)(2,1)S(1)}, bf16[2,2,1,20,128]{4,1,3,0,2:T(2,128)(2,1)S(1)}, u32[]{:S(2)}, u32[]{:S(2)}) %collective-permute-start.7) | collective-permute-done | bytes 20512 | tf_op jit(solution)/shard_map/ppermute | solution.py:17
  55.9 2.5 fusion.27
  58.5 4.4 %fusion.37 = (f32[128]{0:T(128)S(1)}, f32[128]{0:T(128)S(1)}, f32[128]{0:T(128)S(1)}, f32[128]{0:T(128)S(1)}, f32[128]{0:T(128)S(1)}, /*index=5*/f32[128]{0:T(12...) fusion(bf16[2,130,1,20,128]{4,1,3,0,2:T(8,128)(2,1)S(1)} %get-tuple-element.107, ...), kind=kOutput, calls=%fused_computation.78 | convolution fusion | flops 152042496 | bytes 12881920 | tf_op jit(solution)/shard_map/dot_general | solution.py:151
  62.9 5.9 %fusion.33 = (f32[128]{0:T(128)S(1)}, f32[2,128,1,16,128]{4,1,3,0,2:T(8,128)S(1)}, f32[2,128,1,16,128]{4,1,3,0,2:T(8,128)S(1)}, f32[2,128,1,16,128]{4,1,3,0,2:T(...) fusion(f32[2,128,16,128]{3,1,2,0:T(8,128)} %get-tuple-element.1, ...), kind=kLoop, calls=%fused_computation.74 | loop fusion | flops 6291328 | bytes 22025216 | tf_op jit(solution)/shard_map/reduce_sum | solution.py:84
  68.8 5.2 %pad_add_fusion = f32[2,132,1,20,128]{4,1,3,0,2:T(8,128)S(1)} fusion(f32[2,128,1,16,128]{4,1,3,0,2:T(8,128)S(1)} %get-tuple-element.87, f32[2,128,1,16,128]{4,1,3,0,2:T(8,128)S(1)} %get-tuple-element.88, f32[2,128,1,16,128]{4,1,3,0,2:T(8,128)S(1)} %get-tuple-element.89, f32[2,128,1,16,128]{4,1,3,0,2:T(8,128)S(1)} %get-tuple-element.90, ...), kind=kLoop, calls=%fused_computation.3 | loop fusion | flops 5406720 | bytes 21577728 | tf_op jit(solution)/shard_map/add | solution.py:95
  74.1 1.6 collective-permute-start.8
  75.7 1.3 collective-permute-start.9
  77.2 4.2 %collective-permute-done.9 = bf16[2,2,1,20,128]{4,1,3,0,2:T(2,128)(2,1)S(1)} collective-permute-done((bf16[2,2,1,20,128]{4,1,3,0,2:T(2,128)(2,1)S(1)}, bf16[2,2,1,20,128]{4,1,3,0,2:T(2,128)(2,1)S(1)}, u32[]{:S(2)}, u32[]{:S(2)}) %collective-permute-start.9) | collective-permute-done | bytes 20512 | tf_op jit(solution)/shard_map/ppermute | solution.py:17
  81.9 1.6 copy-done.5
  84.2 1.6 rev.16
  85.8 2.8 %rev.17 = bf16[2,128,1,2,128]{4,1,3,0,2:T(8,128)(2,1)} reverse(bf16[2,128,1,2,128]{4,1,3,0,2:T(8,128)(2,1)} %get-tuple-element.79), dimensions={1} | reverse | bytes 262144 | tf_op jit(solution)/shard_map/rev | solution.py:116
  88.6 1.8 fusion.51
  90.4 4.7 %collective-permute-start.11 = (bf16[2,128,2,128]{3,1,2,0:T(8,128)(2,1)}, bf16[2,128,2,128]{3,1,2,0:T(8,128)(2,1)}, u32[]{:S(2)}, u32[]{:S(2)}) collective-permute-start(bf16[2,128,2,128]{3,1,2,0:T(8,128)(2,1)} %get-tuple-element.77), channel_id=1, source_target_pairs={{4,0},{8,4},{12,8},{16,12},{20,16},{24,20},{28,24},{0,28},{5,1},{9... | collective-permute-start | bytes 393224 | tf_op jit(solution)/shard_map/ppermute | solution.py:17
  95.1 3.0 %convolution_bitcast_fusion = f32[128,128]{1,0:T(8,128)} fusion(f32[2,128,16,128]{3,1,2,0:T(8,128)} %copy-done.11, bf16[2,128,16,128]{3,2,1,0:T(8,128)(2,1)S(1)} %copy-done.13), kind=kOutput, calls=%fused_computation.120 | convolution fusion | flops 136839168 | bytes 3211264 | tf_op jit(solution)/shard_map/dot_general | solution.py:145
  98.3 0.9 convert_bitcast_fusion
  99.2 2.4 fusion.48
  101.6 1.0 copy-done.7
  102.6 1.1 convolution_bitcast_fusion.1
  103.9 7.9 %fusion.18 = (f32[128]{0:T(128)}, f32[128]{0:T(128)}, f32[128]{0:T(128)}, f32[128]{0:T(128)}, f32[128]{0:T(128)}, /*index=5*/f32[128]{0:T(128)}, f32[128]{0:T(128)}, f32[128]{0:T(128)}, f32[2,128,16,128]{3,1,2,0:T(8,128)}) fusion(bf16[2,129,1,18,128]{4,1,3,0,2:T(8,128)(2,1)} %copy-done.4, bf16[2,129,1,18,128]{4,1,3,0,2:T(8,128)(2,1)S(1)} %copy-done.3, ...), kind=kOutput, calls=%fused_computation.59 | convolution fusion | flops 152042496 | bytes 12750848 | tf_op jit(solution)/shard_map/dot_general | solution.py:151
  111.8 6.0 %fusion.40 = (f32[128]{0:T(128)S(1)}, f32[2,128,1,16,128]{4,1,3,0,2:T(8,128)S(1)}, f32[2,128,1,16,128]{4,1,3,0,2:T(8,128)S(1)}, f32[2,128,1,16,128]{4,1,3,0,2:T(...) fusion(f32[2,128,16,128]{3,1,2,0:T(8,128)} %get-tuple-element.1, ...), kind=kLoop, calls=%fused_computation.81 | loop fusion | flops 6291328 | bytes 22025216 | tf_op jit(solution)/shard_map/reduce_sum | solution.py:84
  117.9 5.0 %pad_add_fusion.1 = f32[2,130,1,18,128]{4,1,3,0,2:T(8,128)S(1)} fusion(f32[2,128,1,16,128]{4,1,3,0,2:T(8,128)S(1)} %get-tuple-element.97, f32[2,128,1,16,128]{4,1,3,0,2:T(8,128)S(1)} %get-tuple-element.98, f32[2,128,1,16,128]{4,1,3,0,2:T(8,128)S(1)} %get-tuple-element.99, f32[2,128,1,16,128]{4,1,3,0,2:T(8,128)S(1)} %get-tuple-element.100, ...), kind=kLoop, calls=%fused_computation.40 | loop fusion | flops 4792320 | bytes 21270528 | tf_op jit(solution)/shard_map/add | solution.py:95
  122.9 1.6 collective-permute-start.12
  124.5 1.3 collective-permute-start.13
  126.0 41.5 %all-reduce.26 = (f32[9,128]{1,0:T(8,128)S(1)}, f32[9,128]{1,0:T(8,128)S(1)}) all-reduce(f32[9,128]{1,0:T(8,128)S(1)} %stack.69, f32[9,128]{1,0:T(8,128)S(1)} %stack.79), channel_id=1, replica_groups=mesh['strip'=8,'blk'=2,'dp'=2] {'strip','blk','dp'}, use_global_device_ids=true, to_apply=%region_9.10 | all-reduce | flops 2304 | bytes 18432 | tf_op jit(solution)/shard_map/psum | solution.py:187
  168.7 1.4 copy-done.6
  170.4 1.1 fusion.53
  171.5 2.4 collective-permute-start.14
  173.8 2.4 collective-permute-start.15
  176.2 75.4 %all-reduce.30.cloned.1.call-done = (f32[128,128]{1,0:T(8,128)}, f32[128,128]{1,0:T(8,128)}) async-done(((f32[128,128]{1,0:T(8,128)}, f32[128,128]{1,0:T(8,128)}), (f32[128,128]{1,0:T(8,128)}, f32[128,128]{1,0:T(8,128)})) %all-reduce.30.cloned.1.call-update) | async-done | bytes 131088 | tf_op jit(solution)/shard_map/psum | solution.py:187
  251.6 1.5 broadcast_multiply_fusion
  253.2 1.9 fusion.44
  255.1 1.6 copy.87
  (101 shorter events, 9.8 us)
Async XLA Ops:
  7.2 25.3 %copy-start = (bf16[128,128]{1,0:T(8,128)(2,1)S(1)}, bf16[128,128]{1,0:T(8,128)(2,1)}, u32[]{:S(2)}) copy-start(bf16[128,128]{1,0:T(8,128)(2,1)} %param.10) | copy-start | bytes 98308
  7.2 7.7 %copy-start.18 = (s32[2,8]{1,0:T(2,128)S(1)}, s32[2,8]{1,0:T(2,128)}, u32[]{:S(2)}) copy-start(s32[2,8]{1,0:T(2,128)} %param.13) | copy-start | bytes 196
  7.2 15.3 %copy-start.17 = (f32[9,128]{1,0:T(8,128)S(1)}, f32[9,128]{1,0:T(8,128)}, u32[]{:S(2)}) copy-start(f32[9,128]{1,0:T(8,128)} %param.9) | copy-start | bytes 13828
  7.2 244.4 %all-reduce.30.cloned.1.call-start = ((), (), s32[]{:S(2)}) async-start(), calls=%async_computation | async-start | bytes 262144 | tf_op jit(solution)/shard_map/psum | solution.py:187
  8.8 8.4 %collective-permute-start = (bf16[2,128,1,128]{3,1,0,2:T(8,128)(2,1)S(1)}, bf16[2,128,1,128]{3,1,0,2:T(8,128)(2,1)S(1)}, u32[]{:S(2)}, u32[]{:S(2)}) collective-permute-start(bf16[2,128,1,128]{3,1,0,2:T(8,128)(2,1)S(1)} %get-tuple-element.116), channel_id=1, source_target_pairs={{0,4},{4,8},{8,12},{12,16},{16,20},{20,24},{24,28},{28,0},{1,5},{5... | collective-permute-start | bytes 196616 | tf_op jit(solution)/shard_map/ppermute | solution.py:16
  11.8 5.7 %collective-permute-start.1 = (bf16[2,128,1,128]{3,1,0,2:T(8,128)(2,1)S(1)}, bf16[2,128,1,128]{3,1,0,2:T(8,128)(2,1)S(1)}, u32[]{:S(2)}, u32[]{:S(2)}) collective-permute-start(bf16[2,128,1,128]{3,1,0,2:T(8,128)(2,1)S(1)} %get-tuple-element.117), channel_id=1, source_target_pairs={{4,0},{8,4},{12,8},{16,12},{20,16},{24,20},{28,24},{0,28},{5,1},{9... | collective-permute-start | bytes 196616 | tf_op jit(solution)/shard_map/ppermute | solution.py:17
  17.6 9.9 %copy-start.1 = (bf16[2,128,16,128]{3,2,1,0:T(8,128)(2,1)S(1)}, bf16[2,128,16,128]{3,2,1,0:T(8,128)(2,1)}, u32[]{:S(2)}) copy-start(bf16[2,128,16,128]{3,2,1,0:T(8,128)(2,1)} %param.7) | copy-start | bytes 3145732
  17.6 5.0 %collective-permute-start.2 = (bf16[2,1,1,18,128]{4,1,3,0,2:T(2,128)(2,1)S(1)}, bf16[2,1,1,18,128]{4,1,3,0,2:T(2,128)(2,1)S(1)}, u32[]{:S(2)}, u32[]{:S(2)}) collective-permute-start(bf16[2,1,1,18,128]{4,1,3,0,2:T(2,128)(2,1)S(1)} %get-tuple-element.112), channel_id=1, source_target_pairs={{0,2},{1,3},{4,6},{5,7},{8,10},{9,11},{12,14},{13,15},{16,18},{17,... | collective-permute-start | bytes 27656 | tf_op jit(solution)/shard_map/ppermute | solution.py:16
  21.2 5.7 %collective-permute-start.3 = (bf16[2,1,1,18,128]{4,1,3,0,2:T(2,128)(2,1)S(1)}, bf16[2,1,1,18,128]{4,1,3,0,2:T(2,128)(2,1)S(1)}, u32[]{:S(2)}, u32[]{:S(2)}) collective-permute-start(bf16[2,1,1,18,128]{4,1,3,0,2:T(2,128)(2,1)S(1)} %get-tuple-element.113), channel_id=1, source_target_pairs={{2,0},{3,1},{6,4},{7,5},{10,8},{11,9},{14,12},{15,13},{18,16},{19,... | collective-permute-start | bytes 27656 | tf_op jit(solution)/shard_map/ppermute | solution.py:17
  22.5 9.0 %copy-start.15 = (f32[128]{0:T(128)}, f32[128]{0:T(128)S(1)}, u32[]{:S(2)}) copy-start(f32[128]{0:T(128)S(1)} %get-tuple-element.143) | copy-start | bytes 1540
  27.5 4.0 %copy-start.2 = (bf16[2,129,1,18,128]{4,1,3,0,2:T(8,128)(2,1)}, bf16[2,129,1,18,128]{4,1,3,0,2:T(8,128)(2,1)S(1)}, u32[]{:S(2)}) copy-start(bf16[2,129,1,18,128]{4,1,3,0,2:T(8,128)(2,1)S(1)} %get-tuple-element.110) | copy-start | bytes 3566596
  27.5 4.0 %copy-start.4 = (bf16[2,129,1,18,128]{4,1,3,0,2:T(8,128)(2,1)}, bf16[2,129,1,18,128]{4,1,3,0,2:T(8,128)(2,1)S(1)}, u32[]{:S(2)}) copy-start(bf16[2,129,1,18,128]{4,1,3,0,2:T(8,128)(2,1)S(1)} %get-tuple-element.111) | copy-start | bytes 3566596
  31.5 1.0 copy-start.9
  33.7 7.7 %collective-permute-start.4 = (bf16[2,128,2,128]{3,1,2,0:T(8,128)(2,1)S(1)}, bf16[2,128,2,128]{3,1,2,0:T(8,128)(2,1)S(1)}, u32[]{:S(2)}, u32[]{:S(2)}) collective-permute-start(bf16[2,128,2,128]{3,1,2,0:T(8,128)(2,1)S(1)} %get-tuple-element.114), channel_id=1, source_target_pairs={{0,4},{4,8},{8,12},{12,16},{16,20},{20,24},{24,28},{28,0},{1,5},{5... | collective-permute-start | bytes 393224 | tf_op jit(solution)/shard_map/ppermute | solution.py:16
  34.7 9.5 %collective-permute-start.5 = (bf16[2,128,2,128]{3,1,2,0:T(8,128)(2,1)}, bf16[2,128,2,128]{3,1,2,0:T(8,128)(2,1)}, u32[]{:S(2)}, u32[]{:S(2)}) collective-permute-start(bf16[2,128,2,128]{3,1,2,0:T(8,128)(2,1)} %get-tuple-element.115), channel_id=1, source_target_pairs={{4,0},{8,4},{12,8},{16,12},{20,16},{24,20},{28,24},{0,28},{5,1},{9... | collective-permute-start | bytes 393224 | tf_op jit(solution)/shard_map/ppermute | solution.py:17
  41.3 0.6 copy-start.14
  48.0 3.9 %collective-permute-start.6 = (bf16[2,2,1,20,128]{4,1,3,0,2:T(2,128)(2,1)S(1)}, bf16[2,2,1,20,128]{4,1,3,0,2:T(2,128)(2,1)S(1)}, u32[]{:S(2)}, u32[]{:S(2)}) collective-permute-start(bf16[2,2,1,20,128]{4,1,3,0,2:T(2,128)(2,1)S(1)} %get-tuple-element.108), channel_id=1, source_target_pairs={{0,2},{1,3},{4,6},{5,7},{8,10},{9,11},{12,14},{13,15},{16,18},{17,... | collective-permute-start | bytes 61448 | tf_op jit(solution)/shard_map/ppermute | solution.py:16
  49.6 5.7 %collective-permute-start.7 = (bf16[2,2,1,20,128]{4,1,3,0,2:T(2,128)(2,1)S(1)}, bf16[2,2,1,20,128]{4,1,3,0,2:T(2,128)(2,1)S(1)}, u32[]{:S(2)}, u32[]{:S(2)}) collective-permute-start(bf16[2,2,1,20,128]{4,1,3,0,2:T(2,128)(2,1)S(1)} %get-tuple-element.109), channel_id=1, source_target_pairs={{2,0},{3,1},{6,4},{7,5},{10,8},{11,9},{14,12},{15,13},{18,16},{19,... | collective-permute-start | bytes 61448 | tf_op jit(solution)/shard_map/ppermute | solution.py:17
  55.9 2.5 copy-start.12
  55.9 2.5 copy-start.27
  58.5 4.4 %copy-start.11 = (f32[2,128,16,128]{3,1,2,0:T(8,128)}, f32[2,128,16,128]{3,1,2,0:T(8,128)S(1)}, u32[]{:S(2)}) copy-start(f32[2,128,16,128]{3,1,2,0:T(8,128)S(1)} %fusion.27) | copy-start | bytes 6291460
  74.1 3.1 %collective-permute-start.8 = (bf16[2,2,1,20,128]{4,1,3,0,2:T(2,128)(2,1)S(1)}, bf16[2,2,1,20,128]{4,1,3,0,2:T(2,128)(2,1)S(1)}, u32[]{:S(2)}, u32[]{:S(2)}) collective-permute-start(bf16[2,2,1,20,128]{4,1,3,0,2:T(2,128)(2,1)S(1)} %get-tuple-element.74), channel_id=1, source_target_pairs={{0,2},{1,3},{4,6},{5,7},{8,10},{9,11},{12,14},{13,15},{16,18},{17,... | collective-permute-start | bytes 61448 | tf_op jit(solution)/shard_map/ppermute | solution.py:16
  75.7 5.7 %collective-permute-start.9 = (bf16[2,2,1,20,128]{4,1,3,0,2:T(2,128)(2,1)S(1)}, bf16[2,2,1,20,128]{4,1,3,0,2:T(2,128)(2,1)S(1)}, u32[]{:S(2)}, u32[]{:S(2)}) collective-permute-start(bf16[2,2,1,20,128]{4,1,3,0,2:T(2,128)(2,1)S(1)} %get-tuple-element.75), channel_id=1, source_target_pairs={{2,0},{3,1},{6,4},{7,5},{10,8},{11,9},{14,12},{15,13},{18,16},{19,... | collective-permute-start | bytes 61448 | tf_op jit(solution)/shard_map/ppermute | solution.py:17
  81.5 13.6 %copy-start.13 = (bf16[2,128,16,128]{3,2,1,0:T(8,128)(2,1)S(1)}, bf16[2,128,16,128]{3,2,1,0:T(8,128)(2,1)}, u32[]{:S(2)}) copy-start(bf16[2,128,16,128]{3,2,1,0:T(8,128)(2,1)} %param.8) | copy-start | bytes 3145732
  81.9 1.6 copy-start.5
  90.4 7.9 %collective-permute-start.10 = (bf16[2,128,2,128]{3,1,2,0:T(8,128)(2,1)}, bf16[2,128,2,128]{3,1,2,0:T(8,128)(2,1)S(1)}, u32[]{:S(2)}, u32[]{:S(2)}) collective-permute-start(bf16[2,128,2,128]{3,1,2,0:T(8,128)(2,1)} %get-tuple-element.76), channel_id=1, source_target_pairs={{0,4},{4,8},{8,12},{12,16},{16,20},{20,24},{24,28},{28,0},{1,5},{5... | collective-permute-start | bytes 393224 | tf_op jit(solution)/shard_map/ppermute | solution.py:16
  90.4 7.9 %collective-permute-start.11 = (bf16[2,128,2,128]{3,1,2,0:T(8,128)(2,1)}, bf16[2,128,2,128]{3,1,2,0:T(8,128)(2,1)}, u32[]{:S(2)}, u32[]{:S(2)}) collective-permute-start(bf16[2,128,2,128]{3,1,2,0:T(8,128)(2,1)} %get-tuple-element.77), channel_id=1, source_target_pairs={{4,0},{8,4},{12,8},{16,12},{20,16},{24,20},{28,24},{0,28},{5,1},{9... | collective-permute-start | bytes 393224 | tf_op jit(solution)/shard_map/ppermute | solution.py:17
  99.2 3.3 %copy-start.10 = (bf16[2,128,16,128]{3,1,2,0:T(8,128)(2,1)S(1)}, bf16[2,128,16,128]{3,1,2,0:T(8,128)(2,1)}, u32[]{:S(2)}) copy-start(bf16[2,128,16,128]{3,1,2,0:T(8,128)(2,1)} %copy-done.9) | copy-start | bytes 3145732
  101.6 1.0 copy-start.7
  102.6 1.3 copy-start.3
  103.9 7.9 %copy-start.16 = (f32[128]{0:T(128)S(1)}, f32[128]{0:T(128)}, u32[]{:S(2)}) copy-start(f32[128]{0:T(128)} %copy-done.15) | copy-start | bytes 1540
  117.8 8.1 %copy-start.19 = (f32[128]{0:T(128)S(1)}, f32[128]{0:T(128)}, u32[]{:S(2)}) copy-start(f32[128]{0:T(128)} %get-tuple-element.48) | copy-start | bytes 1540
  117.8 8.1 %copy-start.20 = (f32[128]{0:T(128)S(1)}, f32[128]{0:T(128)}, u32[]{:S(2)}) copy-start(f32[128]{0:T(128)} %get-tuple-element.49) | copy-start | bytes 1540
  117.8 8.1 %copy-start.21 = (f32[128]{0:T(128)S(1)}, f32[128]{0:T(128)}, u32[]{:S(2)}) copy-start(f32[128]{0:T(128)} %get-tuple-element.50) | copy-start | bytes 1540
  117.8 8.1 %copy-start.22 = (f32[128]{0:T(128)S(1)}, f32[128]{0:T(128)}, u32[]{:S(2)}) copy-start(f32[128]{0:T(128)} %get-tuple-element.63) | copy-start | bytes 1540
  117.8 8.1 %copy-start.23 = (f32[128]{0:T(128)S(1)}, f32[128]{0:T(128)}, u32[]{:S(2)}) copy-start(f32[128]{0:T(128)} %get-tuple-element.64) | copy-start | bytes 1540
  117.8 8.1 %copy-start.24 = (f32[128]{0:T(128)S(1)}, f32[128]{0:T(128)}, u32[]{:S(2)}) copy-start(f32[128]{0:T(128)} %get-tuple-element.65) | copy-start | bytes 1540
  117.8 8.1 %copy-start.25 = (f32[128]{0:T(128)S(1)}, f32[128]{0:T(128)}, u32[]{:S(2)}) copy-start(f32[128]{0:T(128)} %get-tuple-element.66) | copy-start | bytes 1540
  117.8 8.1 %copy-start.26 = (f32[128]{0:T(128)S(1)}, f32[128]{0:T(128)}, u32[]{:S(2)}) copy-start(f32[128]{0:T(128)} %get-tuple-element.67) | copy-start | bytes 1540
  122.9 45.4 %collective-permute-start.12 = (bf16[2,1,1,18,128]{4,1,3,0,2:T(2,128)(2,1)S(1)}, bf16[2,1,1,18,128]{4,1,3,0,2:T(2,128)(2,1)S(1)}, u32[]{:S(2)}, u32[]{:S(2)}) collective-permute-start(bf16[2,1,1,18,128]{4,1,3,0,2:T(2,128)(2,1)S(1)} %get-tuple-element.80), channel_id=1, source_target_pairs={{0,2},{1,3},{4,6},{5,7},{8,10},{9,11},{12,14},{13,15},{16,18},{17,... | collective-permute-start | bytes 27656 | tf_op jit(solution)/shard_map/ppermute | solution.py:16
  124.5 43.7 %collective-permute-start.13 = (bf16[2,1,1,18,128]{4,1,3,0,2:T(2,128)(2,1)S(1)}, bf16[2,1,1,18,128]{4,1,3,0,2:T(2,128)(2,1)S(1)}, u32[]{:S(2)}, u32[]{:S(2)}) collective-permute-start(bf16[2,1,1,18,128]{4,1,3,0,2:T(2,128)(2,1)S(1)} %get-tuple-element.81), channel_id=1, source_target_pairs={{2,0},{3,1},{6,4},{7,5},{10,8},{11,9},{14,12},{15,13},{18,16},{19,... | collective-permute-start | bytes 27656 | tf_op jit(solution)/shard_map/ppermute | solution.py:17
  168.7 1.4 copy-start.6
  170.1 83.0 %copy-start.8 = (bf16[2,128,16,128]{3,1,2,0:T(8,128)(2,1)S(1)}, bf16[2,128,16,128]{3,1,2,0:T(8,128)(2,1)}, u32[]{:S(2)}) copy-start(bf16[2,128,16,128]{3,1,2,0:T(8,128)(2,1)} %copy-done.7) | copy-start | bytes 3145732
  171.5 81.7 %collective-permute-start.14 = (bf16[2,128,1,128]{3,1,0,2:T(8,128)(2,1)S(1)}, bf16[2,128,1,128]{3,1,0,2:T(8,128)(2,1)S(1)}, u32[]{:S(2)}, u32[]{:S(2)}) collective-permute-start(bf16[2,128,1,128]{3,1,0,2:T(8,128)(2,1)S(1)} %get-tuple-element.82), channel_id=1, source_target_pairs={{0,4},{4,8},{8,12},{12,16},{16,20},{20,24},{24,28},{28,0},{1,5},{5... | collective-permute-start | bytes 196616 | tf_op jit(solution)/shard_map/ppermute | solution.py:16
  173.8 79.3 %collective-permute-start.15 = (bf16[2,128,1,128]{3,1,0,2:T(8,128)(2,1)S(1)}, bf16[2,128,1,128]{3,1,0,2:T(8,128)(2,1)S(1)}, u32[]{:S(2)}, u32[]{:S(2)}) collective-permute-start(bf16[2,128,1,128]{3,1,0,2:T(8,128)(2,1)S(1)} %get-tuple-element.83), channel_id=1, source_target_pairs={{4,0},{8,4},{12,8},{16,12},{20,16},{24,20},{28,24},{0,28},{5,1},{9... | collective-permute-start | bytes 196616 | tf_op jit(solution)/shard_map/ppermute | solution.py:17
Sparse Core Ops, SparseCore 0:
  126.0 125.5 all-reduce.29
where the time goes:
time: 265 us; the launch traced here: 264 us
  waiting for transfers between devices  91.1 us (34%)
  other arithmetic  43.1 us (16%)
  blocking collectives  41.5 us (16%)
  starting transfers between devices  34 us (13%)
  local copies, waits for them, and re-layouts  21.1 us (8%)
  matrix products  16.9 us (6%)
  between operations  16 us (6%)
    psum x1, waiting for transfers between devices, shards(): lax.psum((dk_one, dw_one, dk_two, dw_two), ('strip', 'blk', 'dp'))  75.4 us
    psum x1, blocking collectives, shards(): lax.psum((dk_one, dw_one, dk_two, dw_two), ('strip', 'blk', 'dp'))  41.5 us
    ppermute x8, starting transfers between devices, with_halo(): after = lax.ppermute(first, axis, down)  19.1 us
    ppermute x8, starting transfers between devices, with_halo(): before = lax.ppermute(last, axis, up)  14.8 us
    dot_general x2, matrix products, block_back(): lax.dot_general(flat_grad, weight, (((1,), (1,)), ((), ())), preferred_el...  12.3 us
    ppermute x8, waiting for transfers between devices, with_halo(): after = lax.ppermute(first, axis, down)  12.1 us
    reduce_sum x2, other arithmetic, conv_back(): tap_sums.append(jnp.sum(tap_slice * grad_strips, axis=(0, 1, 2, 3)))  11.9 us
    add x2, other arithmetic, conv_back(): grad_wide = grad_wide + placed  10.2 us
  transfers between devices with their start and end apart: 17, of which 10 were waited for; matrix products, arithmetic and copies ran while one was open for 4% of the time, Pallas kernels for 0%

commit v1 on v0

--- a/solution.py
+++ b/solution.py
@@ -4,6 +4,31 @@
 from jax.sharding import PartitionSpec as P
 
 COL_DEV = 16
+
+
+def tree_sum(value, axes):
+    sizes = [lax.axis_size(axis) for axis in axes]
+    count = 1
+    for size in sizes:
+        count *= size
+    if count & (count - 1):
+        return lax.psum(value, axes)
+    bit = 1
+    while bit < count:
+        pairs = [(i, i ^ bit) for i in range(count)]
+        value = value + lax.ppermute(value, axes, pairs)
+        bit *= 2
+    return value
+
+
+def packed_sum(parts, axes, reducer):
+    rows = [part.shape[0] for part in parts]
+    summed = reducer(jnp.concatenate(parts, axis=0), axes)
+    out, start = [], 0
+    for count in rows:
+        out.append(summed[start : start + count])
+        start += count
+    return out
 
 
 def with_halo(shard, sides, width, wrap):
@@ -184,8 +209,8 @@
     grad_fields, dk_one, dw_one = block_back(
         wide_one, pre_one, act_one, grad_hidden, kernel_one, weight_one, 1, seams
     )
-    dk_one, dw_one, dk_two, dw_two = lax.psum(
-        (dk_one, dw_one, dk_two, dw_two), ("strip", "blk", "dp")
+    dk_one, dw_one, dk_two, dw_two = packed_sum(
+        (dk_one, dw_one, dk_two, dw_two), ("strip", "blk", "dp"), tree_sum
     )
     return (grad_fields, dk_one * factor, dw_one * factor, dk_two * factor, dw_two * factor)
 

time: 265 us -> 145 us (0.55)
  waiting for transfers between devices: 91.1 us -> 30.3 us
  blocking collectives: 41.5 us -> 0 us
  between operations: 16 us -> 2.66 us
  other arithmetic: 43.1 us -> 38.3 us
  starting transfers between devices: 34 us -> 38.4 us
  matrix products: 16.9 us -> 12.9 us
    psum x1 -> x0, waiting for transfers between devices: 75.4 us -> none  [shards(): lax.psum((dk_one, dw_one, dk_two, dw_two), ('strip', 'blk', 'dp'))]
    psum x1 -> x0, blocking collectives: 41.5 us -> none  [shards(): lax.psum((dk_one, dw_one, dk_two, dw_two), ('strip', 'blk', 'dp'))]
    ppermute x0 -> x5, waiting for transfers between devices: none -> 7.1 us  [tree_sum(): value = value + lax.ppermute(value, axes, pairs)]
    ppermute x8, waiting for transfers between devices: 12.1 us -> 16.5 us  [with_halo(): after = lax.ppermute(first, axis, down)]
    ppermute x0 -> x5, starting transfers between devices: none -> 4.38 us  [tree_sum(): value = value + lax.ppermute(value, axes, pairs)]
    ppermute x8, waiting for transfers between devices: 3.59 us -> 6.74 us  [with_halo(): before = lax.ppermute(last, axis, up)]
    dot_general x2, matrix products: 12.3 us -> 9.38 us  [block_back(): lax.dot_general(flat_grad, weight, (((1,), (1,)), ((), ())), preferred_el...]
    unnamed x58 -> x60, local copies, waits for them, and re-layouts: 9.04 us -> 9.96 us
  transfers between devices with their start and end apart: 17 -> 21, of which waited for: 10 -> 15; matrix products, arithmetic and copies ran while one was open for 4% -> 8% of each run, Pallas kernels for 0% -> 0%
where the time goes in v1:
time: 145 us; the launch traced here: 144 us
  starting transfers between devices  38.4 us (26%)
  other arithmetic  38.3 us (26%)
  waiting for transfers between devices  30.3 us (21%)
  local copies, waits for them, and re-layouts  21.4 us (15%)
  matrix products  12.9 us (9%)
  between operations  2.66 us (2%)
    ppermute x8, starting transfers between devices, with_halo(): after = lax.ppermute(first, axis, down)  19.5 us
    ppermute x8, waiting for transfers between devices, with_halo(): after = lax.ppermute(first, axis, down)  16.5 us
    ppermute x8, starting transfers between devices, with_halo(): before = lax.ppermute(last, axis, up)  14.5 us
    reduce_sum x2, other arithmetic, conv_back(): tap_sums.append(jnp.sum(tap_slice * grad_strips, axis=(0, 1, 2, 3)))  11.9 us
    add x2, other arithmetic, conv_back(): grad_wide = grad_wide + placed  10.2 us
    unnamed x60, local copies, waits for them, and re-layouts  9.96 us
    dot_general x2, matrix products, block_back(): lax.dot_general(flat_grad, weight, (((1,), (1,)), ((), ())), preferred_el...  9.38 us
    ppermute x5, waiting for transfers between devices, tree_sum(): value = value + lax.ppermute(value, axes, pairs)  7.1 us
  transfers between devices with their start and end apart: 21, of which 15 were waited for; matrix products, arithmetic and copies ran while one was open for 8% of the time, Pallas kernels for 0%

profile of v1, /device:TPU:0, one launch (start us, length us, event | category | flops | bytes accessed | tf_op | source)
XLA Modules:
  0.0 143.9 jit_solution(9378646457086837455)
XLA Ops:
  0.7 1.5 %copy.110 = bf16[2,128,16,128]{3,1,2,0:T(8,128)(2,1)S(1)} copy(bf16[2,128,16,128]{3,2,1,0:T(8,128)(2,1)} %param.7) | data formatting | bytes 2097152 | tf_op args[0]
  2.2 3.0 %collective-permute-start = (bf16[2,128,1,128]{3,1,0,2:T(8,128)(2,1)S(1)}, bf16[2,128,1,128]{3,1,0,2:T(8,128)(2,1)S(1)}, u32[]{:S(2)}, u32[]{:S(2)}) collective-permute-start(bf16[2,128,1,128]{3,1,0,2:T(8,128)(2,1)S(1)} %get-tuple-element.112), channel_id=1, source_target_pairs={{0,4},{4,8},{8,12},{12,16},{16,20},{20,24},{24,28},{28,0},{1,5},{5... | collective-permute-start | bytes 196616 | tf_op jit(solution)/shard_map/ppermute | solution.py:41
  5.2 3.1 %collective-permute-start.1 = (bf16[2,128,1,128]{3,1,0,2:T(8,128)(2,1)S(1)}, bf16[2,128,1,128]{3,1,0,2:T(8,128)(2,1)S(1)}, u32[]{:S(2)}, u32[]{:S(2)}) collective-permute-start(bf16[2,128,1,128]{3,1,0,2:T(8,128)(2,1)S(1)} %get-tuple-element.113), channel_id=1, source_target_pairs={{4,0},{8,4},{12,8},{16,12},{20,16},{24,20},{28,24},{0,28},{5,1},{9... | collective-permute-start | bytes 196616 | tf_op jit(solution)/shard_map/ppermute | solution.py:42
  11.1 3.5 %collective-permute-start.2 = (bf16[2,1,1,18,128]{4,1,3,0,2:T(2,128)(2,1)S(1)}, bf16[2,1,1,18,128]{4,1,3,0,2:T(2,128)(2,1)S(1)}, u32[]{:S(2)}, u32[]{:S(2)}) collective-permute-start(bf16[2,1,1,18,128]{4,1,3,0,2:T(2,128)(2,1)S(1)} %get-tuple-element.108), channel_id=1, source_target_pairs={{0,2},{1,3},{4,6},{5,7},{8,10},{9,11},{12,14},{13,15},{16,18},{17,... | collective-permute-start | bytes 27656 | tf_op jit(solution)/shard_map/ppermute | solution.py:41
  14.6 1.3 collective-permute-start.3
  16.0 4.2 %collective-permute-done.3 = bf16[2,1,1,18,128]{4,1,3,0,2:T(2,128)(2,1)S(1)} collective-permute-done((bf16[2,1,1,18,128]{4,1,3,0,2:T(2,128)(2,1)S(1)}, bf16[2,1,1,18,128]{4,1,3,0,2:T(2,128)(2,1)S(1)}, u32[]{:S(2)}, u32[]{:S(2)}) %collective-permute-start.3) | collective-permute-done | bytes 9248 | tf_op jit(solution)/shard_map/ppermute | solution.py:42
  21.0 3.9 %multiply_convert_fusion.1 = (bf16[2,128,16,128]{3,1,2,0:T(8,128)(2,1)S(1)}, f32[2,128,16,128]{3,1,2,0:T(8,128)}) fusion(f32[128]{0:T(128)S(1)} %get-tuple-element.142, bf16[2,129,1,18,128]{4,1,3,0,2:T(8,128)(2,1)S(1)} %get-tuple-element.107, f32[128]{0:T(128)S(1)} %get-tuple-element.143, f32[128]{0:T(128)S(1)} %get-tuple-element.136, ...), kind=kLoop, calls=%fused_computation.114 | loop fusion | flops 17301504 | bytes 11670016 | tf_op jit(solution)/shard_map/convert_element_type | solution.py:201
  24.9 1.0 copy-done.11
  27.1 1.0 collective-permute-start.4
  28.1 3.7 %collective-permute-start.5 = (bf16[2,128,2,128]{3,1,2,0:T(8,128)(2,1)}, bf16[2,128,2,128]{3,1,2,0:T(8,128)(2,1)}, u32[]{:S(2)}, u32[]{:S(2)}) collective-permute-start(bf16[2,128,2,128]{3,1,2,0:T(8,128)(2,1)} %get-tuple-element.111), channel_id=1, source_target_pairs={{4,0},{8,4},{12,8},{16,12},{20,16},{24,20},{28,24},{0,28},{5,1},{9... | collective-permute-start | bytes 393224 | tf_op jit(solution)/shard_map/ppermute | solution.py:42
  31.8 2.9 %collective-permute-done.4 = bf16[2,128,2,128]{3,1,2,0:T(8,128)(2,1)S(1)} collective-permute-done((bf16[2,128,2,128]{3,1,2,0:T(8,128)(2,1)S(1)}, bf16[2,128,2,128]{3,1,2,0:T(8,128)(2,1)S(1)}, u32[]{:S(2)}, u32[]{:S(2)}) %collective-permute-start.4) | collective-permute-done | bytes 131104 | tf_op jit(solution)/shard_map/ppermute | solution.py:41
  35.4 1.3 reverse.14
  36.7 0.9 select_bitcast_fusion.1
  37.6 2.8 %reverse.15 = bf16[2,128,2,128]{3,1,2,0:T(8,128)(2,1)} reverse(bf16[2,128,2,128]{3,1,2,0:T(8,128)(2,1)} %collective-permute-done.5), dimensions={1} | reverse | bytes 262144 | tf_op jit(solution)/shard_map/reverse.3
  40.4 0.9 select_bitcast_fusion
  41.3 1.6 %collective-permute-start.6 = (bf16[2,2,1,20,128]{4,1,3,0,2:T(2,128)(2,1)S(1)}, bf16[2,2,1,20,128]{4,1,3,0,2:T(2,128)(2,1)S(1)}, u32[]{:S(2)}, u32[]{:S(2)}) collective-permute-start(bf16[2,2,1,20,128]{4,1,3,0,2:T(2,128)(2,1)S(1)} %get-tuple-element.104), channel_id=1, source_target_pairs={{0,2},{1,3},{4,6},{5,7},{8,10},{9,11},{12,14},{13,15},{16,18},{17,... | collective-permute-start | bytes 61448 | tf_op jit(solution)/shard_map/ppermute | solution.py:41
  43.0 1.3 collective-permute-start.7
  44.4 4.2 %collective-permute-done.7 = bf16[2,2,1,20,128]{4,1,3,0,2:T(2,128)(2,1)S(1)} collective-permute-done((bf16[2,2,1,20,128]{4,1,3,0,2:T(2,128)(2,1)S(1)}, bf16[2,2,1,20,128]{4,1,3,0,2:T(2,128)(2,1)S(1)}, u32[]{:S(2)}, u32[]{:S(2)}) %collective-permute-start.7) | collective-permute-done | bytes 20512 | tf_op jit(solution)/shard_map/ppermute | solution.py:42
  49.3 2.5 %fusion.27 = f32[2,128,16,128]{3,1,2,0:T(8,128)S(1)} fusion(bf16[2,128,16,128]{3,1,2,0:T(8,128)(2,1)S(1)} %fusion.39, f32[128]{0:T(128)S(1)} %get-tuple-element.133, f32[128]{0:T(128)S(1)} %get-tuple-element.134, f32[128]{0:T(128)S(1)} %get-tuple-element.127, f32[128]{0:T(128)S(1)} %get-tuple-element.128, f32[128]{0:T(128)S(1)} %get-tuple-element.129, ...), kind=kLoop, calls=%fused_computation.68 | loop fusion | flops 14680064 | bytes 10752512 | tf_op jit(solution)/shard_map/reshape | solution.py:93
  51.9 5.1 %fusion.37 = (f32[128]{0:T(128)S(1)}, f32[128]{0:T(128)S(1)}, f32[128]{0:T(128)}, f32[128]{0:T(128)}, f32[128]{0:T(128)}, /*index=5*/f32[128]{0:T(128)}, f32[128]{0:T(128)}, f32[128]{0:T(128)}, f32[2,128,16,128]{3,1,2,0:T(8,128)}) fusion(bf16[2,130,1,20,128]{4,1,3,0,2:T(8,128)(2,1)S(1)} %get-tuple-element.103, ...), kind=kOutput, calls=%fused_computation.78 | convolution fusion | flops 152042496 | bytes 12881920 | tf_op jit(solution)/shard_map/dot_general | solution.py:176
  56.9 5.9 %fusion.33 = (f32[128]{0:T(128)S(1)}, f32[2,128,1,16,128]{4,1,3,0,2:T(8,128)S(1)}, f32[2,128,1,16,128]{4,1,3,0,2:T(8,128)S(1)}, f32[2,128,1,16,128]{4,1,3,0,2:T(...) fusion(f32[2,128,16,128]{3,1,2,0:T(8,128)} %get-tuple-element.1, ...), kind=kLoop, calls=%fused_computation.74 | loop fusion | flops 6291328 | bytes 22025216 | tf_op jit(solution)/shard_map/reduce_sum | solution.py:109
  62.9 5.2 %pad_add_fusion = f32[2,132,1,20,128]{4,1,3,0,2:T(8,128)S(1)} fusion(f32[2,128,1,16,128]{4,1,3,0,2:T(8,128)S(1)} %get-tuple-element.83, f32[2,128,1,16,128]{4,1,3,0,2:T(8,128)S(1)} %get-tuple-element.84, f32[2,128,1,16,128]{4,1,3,0,2:T(8,128)S(1)} %get-tuple-element.85, f32[2,128,1,16,128]{4,1,3,0,2:T(8,128)S(1)} %get-tuple-element.86, ...), kind=kLoop, calls=%fused_computation.3 | loop fusion | flops 5406720 | bytes 21577728 | tf_op jit(solution)/shard_map/add | solution.py:120
  68.1 1.6 %collective-permute-start.8 = (bf16[2,2,1,20,128]{4,1,3,0,2:T(2,128)(2,1)S(1)}, bf16[2,2,1,20,128]{4,1,3,0,2:T(2,128)(2,1)S(1)}, u32[]{:S(2)}, u32[]{:S(2)}) collective-permute-start(bf16[2,2,1,20,128]{4,1,3,0,2:T(2,128)(2,1)S(1)} %get-tuple-element.70), channel_id=1, source_target_pairs={{0,2},{1,3},{4,6},{5,7},{8,10},{9,11},{12,14},{13,15},{16,18},{17,... | collective-permute-start | bytes 61448 | tf_op jit(solution)/shard_map/ppermute | solution.py:41
  69.8 1.3 collective-permute-start.9
  71.2 4.2 %collective-permute-done.9 = bf16[2,2,1,20,128]{4,1,3,0,2:T(2,128)(2,1)S(1)} collective-permute-done((bf16[2,2,1,20,128]{4,1,3,0,2:T(2,128)(2,1)S(1)}, bf16[2,2,1,20,128]{4,1,3,0,2:T(2,128)(2,1)S(1)}, u32[]{:S(2)}, u32[]{:S(2)}) %collective-permute-start.9) | collective-permute-done | bytes 20512 | tf_op jit(solution)/shard_map/ppermute | solution.py:42
  75.9 1.6 %copy-done.6 = f32[2,128,1,20,128]{4,1,3,0,2:T(8,128)} copy-done((f32[2,128,1,20,128]{4,1,3,0,2:T(8,128)}, f32[2,128,1,20,128]{4,1,3,0,2:T(8,128)S(1)}, u32[]{:S(2)}) %copy-start.6) | copy-done | bytes 2621464
  78.2 1.6 %rev.16 = bf16[2,128,1,2,128]{4,1,3,0,2:T(8,128)(2,1)S(1)} reverse(bf16[2,128,1,2,128]{4,1,3,0,2:T(8,128)(2,1)} %get-tuple-element.74), dimensions={1} | reverse | bytes 262144 | tf_op jit(solution)/shard_map/rev | solution.py:142
  79.8 2.8 %rev.17 = bf16[2,128,1,2,128]{4,1,3,0,2:T(8,128)(2,1)} reverse(bf16[2,128,1,2,128]{4,1,3,0,2:T(8,128)(2,1)} %get-tuple-element.75), dimensions={1} | reverse | bytes 262144 | tf_op jit(solution)/shard_map/rev | solution.py:141
  82.6 1.1 fusion.51
  83.8 4.7 %collective-permute-start.11 = (bf16[2,128,2,128]{3,1,2,0:T(8,128)(2,1)S(1)}, bf16[2,128,2,128]{3,1,2,0:T(8,128)(2,1)S(1)}, u32[]{:S(2)}, u32[]{:S(2)}) collective-permute-start(bf16[2,128,2,128]{3,1,2,0:T(8,128)(2,1)S(1)} %get-tuple-element.73), channel_id=1, source_target_pairs={{4,0},{8,4},{12,8},{16,12},{20,16},{24,20},{28,24},{0,28},{5,1},{9... | collective-permute-start | bytes 393224 | tf_op jit(solution)/shard_map/ppermute | solution.py:42
  88.5 2.5 %convolution_bitcast_fusion = f32[128,128]{1,0:T(8,128)S(1)} fusion(f32[2,128,16,128]{3,1,2,0:T(8,128)} %copy-done.13, bf16[2,128,16,128]{3,2,1,0:T(8,128)(2,1)S(1)} %copy-done.16), kind=kOutput, calls=%fused_computation.120 | convolution fusion | flops 136839168 | bytes 3211264 | tf_op jit(solution)/shard_map/dot_general | solution.py:170
  94.7 4.3 %fusion.18 = (f32[128]{0:T(128)S(1)}, f32[128]{0:T(128)S(1)}, f32[128]{0:T(128)S(1)}, f32[128]{0:T(128)S(1)}, f32[128]{0:T(128)S(1)}, /*index=5*/f32[128]{0:T(12...) fusion(bf16[2,129,1,18,128]{4,1,3,0,2:T(8,128)(2,1)S(1)} %copy-done.5, ...), kind=kOutput, calls=%fused_computation.59 | convolution fusion | flops 152042496 | bytes 12750848 | tf_op jit(solution)/shard_map/dot_general | solution.py:176
  99.0 6.0 %fusion.40 = (f32[128]{0:T(128)S(1)}, f32[2,128,1,16,128]{4,1,3,0,2:T(8,128)S(1)}, f32[2,128,1,16,128]{4,1,3,0,2:T(8,128)S(1)}, f32[2,128,1,16,128]{4,1,3,0,2:T(...) fusion(f32[2,128,16,128]{3,1,2,0:T(8,128)} %get-tuple-element.1, ...), kind=kLoop, calls=%fused_computation.81 | loop fusion | flops 6291328 | bytes 22025216 | tf_op jit(solution)/shard_map/reduce_sum | solution.py:109
  105.0 5.0 %pad_add_fusion.1 = f32[2,130,1,18,128]{4,1,3,0,2:T(8,128)S(1)} fusion(f32[2,128,1,16,128]{4,1,3,0,2:T(8,128)S(1)} %get-tuple-element.93, f32[2,128,1,16,128]{4,1,3,0,2:T(8,128)S(1)} %get-tuple-element.94, f32[2,128,1,16,128]{4,1,3,0,2:T(8,128)S(1)} %get-tuple-element.95, f32[2,128,1,16,128]{4,1,3,0,2:T(8,128)S(1)} %get-tuple-element.96, ...), kind=kLoop, calls=%fused_computation.40 | loop fusion | flops 4792320 | bytes 21270528 | tf_op jit(solution)/shard_map/add | solution.py:120
  110.0 1.6 %collective-permute-start.12 = (bf16[2,1,1,18,128]{4,1,3,0,2:T(2,128)(2,1)S(1)}, bf16[2,1,1,18,128]{4,1,3,0,2:T(2,128)(2,1)S(1)}, u32[]{:S(2)}, u32[]{:S(2)}) collective-permute-start(bf16[2,1,1,18,128]{4,1,3,0,2:T(2,128)(2,1)S(1)} %get-tuple-element.76), channel_id=1, source_target_pairs={{0,2},{1,3},{4,6},{5,7},{8,10},{9,11},{12,14},{13,15},{16,18},{17,... | collective-permute-start | bytes 27656 | tf_op jit(solution)/shard_map/ppermute | solution.py:41
  111.7 1.3 collective-permute-start.13
  113.8 3.6 %collective-permute-done.13 = bf16[2,1,1,18,128]{4,1,3,0,2:T(2,128)(2,1)S(1)} collective-permute-done((bf16[2,1,1,18,128]{4,1,3,0,2:T(2,128)(2,1)S(1)}, bf16[2,1,1,18,128]{4,1,3,0,2:T(2,128)(2,1)S(1)}, u32[]{:S(2)}, u32[]{:S(2)}) %collective-permute-start.13) | collective-permute-done | bytes 9248 | tf_op jit(solution)/shard_map/ppermute | solution.py:42
  117.9 1.3 copy-done.8
  119.5 3.5 %collective-permute-done.17 = f32[274,128]{1,0:T(8,128)S(1)} collective-permute-done((f32[274,128]{1,0:T(8,128)S(1)}, f32[274,128]{1,0:T(8,128)S(1)}, u32[]{:S(2)}, u32[]{:S(2)}) %collective-permute-start.17) | collective-permute-done | bytes 140320 | tf_op jit(solution)/shard_map/ppermute | solution.py:19
  123.1 1.0 fusion.53
  124.1 2.1 %collective-permute-start.14 = (bf16[2,128,1,128]{3,1,0,2:T(8,128)(2,1)S(1)}, bf16[2,128,1,128]{3,1,0,2:T(8,128)(2,1)S(1)}, u32[]{:S(2)}, u32[]{:S(2)}) collective-permute-start(bf16[2,128,1,128]{3,1,0,2:T(8,128)(2,1)S(1)} %get-tuple-element.78), channel_id=1, source_target_pairs={{0,4},{4,8},{8,12},{12,16},{16,20},{20,24},{24,28},{28,0},{1,5},{5... | collective-permute-start | bytes 196616 | tf_op jit(solution)/shard_map/ppermute | solution.py:41
  126.1 2.8 %collective-permute-start.15 = (bf16[2,128,1,128]{3,1,0,2:T(8,128)(2,1)S(1)}, bf16[2,128,1,128]{3,1,0,2:T(8,128)(2,1)S(1)}, u32[]{:S(2)}, u32[]{:S(2)}) collective-permute-start(bf16[2,128,1,128]{3,1,0,2:T(8,128)(2,1)S(1)} %get-tuple-element.79), channel_id=1, source_target_pairs={{4,0},{8,4},{12,8},{16,12},{20,16},{24,20},{28,24},{0,28},{5,1},{9... | collective-permute-start | bytes 196616 | tf_op jit(solution)/shard_map/ppermute | solution.py:42
  129.0 2.7 %collective-permute-done.14 = bf16[2,128,1,128]{3,1,0,2:T(8,128)(2,1)S(1)} collective-permute-done((bf16[2,128,1,128]{3,1,0,2:T(8,128)(2,1)S(1)}, bf16[2,128,1,128]{3,1,0,2:T(8,128)(2,1)S(1)}, u32[]{:S(2)}, u32[]{:S(2)}) %collective-permute-start.14) | collective-permute-done | bytes 65568 | tf_op jit(solution)/shard_map/ppermute | solution.py:41
  131.8 2.4 %collective-permute-done.19 = f32[274,128]{1,0:T(8,128)S(1)} collective-permute-done((f32[274,128]{1,0:T(8,128)S(1)}, f32[274,128]{1,0:T(8,128)S(1)}, u32[]{:S(2)}, u32[]{:S(2)}) %collective-permute-start.19) | collective-permute-done | bytes 140320 | tf_op jit(solution)/shard_map/ppermute | solution.py:19
  134.1 4.1 %collective-permute-start.20 = (f32[274,128]{1,0:T(8,128)S(1)}, f32[274,128]{1,0:T(8,128)S(1)}, u32[]{:S(2)}, u32[]{:S(2)}) collective-permute-start(f32[274,128]{1,0:T(8,128)S(1)} %add.292), channel_id=1, source_target_pairs={{0,16},{1,17},{2,18},{3,19},{4,20},{5,21},{6,22},{7,23},{8,24},{9,... | collective-permute-start | bytes 420872 | tf_op jit(solution)/shard_map/ppermute | solution.py:19
  138.2 1.5 %fusion.44 = bf16[2,128,16,128]{3,1,2,0:T(8,128)(2,1)S(1)} fusion(f32[2,128,1,18,128]{4,1,3,0,2:T(8,128)S(1)} %copy-done.9, f32[2,128,1,1,128]{4,1,3,0,2:T(8,128)S(1)} %get-tuple-element.117, f32[2,128,1,1,128]{4,1,3,0,2:T(8,128)S(1)} %get-tuple-element.116, bf16[2,128,16,128]{3,1,2,0:T(8,128)(2,1)} %copy-done.10), kind=kLoop, calls=%fused_computation.86 | loop fusion | flops 2621440 | bytes 4456448 | tf_op jit(solution)/shard_map/convert_element_type | solution.py:183
  139.8 1.6 %copy.87 = bf16[2,128,16,128]{3,2,1,0:T(8,128)(2,1)} copy(bf16[2,128,16,128]{3,1,2,0:T(8,128)(2,1)S(1)} %fusion.44) | data formatting | bytes 2097152
  141.4 1.2 collective-permute-done.20
  (113 shorter events, 13.0 us)
Async XLA Ops:
  0.6 25.3 %copy-start = (bf16[128,128]{1,0:T(8,128)(2,1)S(1)}, bf16[128,128]{1,0:T(8,128)(2,1)}, u32[]{:S(2)}) copy-start(bf16[128,128]{1,0:T(8,128)(2,1)} %param.10) | copy-start | bytes 98308
  0.6 7.7 %copy-start.21 = (s32[2,8]{1,0:T(2,128)S(1)}, s32[2,8]{1,0:T(2,128)}, u32[]{:S(2)}) copy-start(s32[2,8]{1,0:T(2,128)} %param.13) | copy-start | bytes 196
  0.7 15.2 %copy-start.19 = (f32[9,128]{1,0:T(8,128)S(1)}, f32[9,128]{1,0:T(8,128)}, u32[]{:S(2)}) copy-start(f32[9,128]{1,0:T(8,128)} %param.9) | copy-start | bytes 13828
  2.2 8.4 %collective-permute-start = (bf16[2,128,1,128]{3,1,0,2:T(8,128)(2,1)S(1)}, bf16[2,128,1,128]{3,1,0,2:T(8,128)(2,1)S(1)}, u32[]{:S(2)}, u32[]{:S(2)}) collective-permute-start(bf16[2,128,1,128]{3,1,0,2:T(8,128)(2,1)S(1)} %get-tuple-element.112), channel_id=1, source_target_pairs={{0,4},{4,8},{8,12},{12,16},{16,20},{20,24},{24,28},{28,0},{1,5},{5... | collective-permute-start | bytes 196616 | tf_op jit(solution)/shard_map/ppermute | solution.py:41
  5.2 5.7 %collective-permute-start.1 = (bf16[2,128,1,128]{3,1,0,2:T(8,128)(2,1)S(1)}, bf16[2,128,1,128]{3,1,0,2:T(8,128)(2,1)S(1)}, u32[]{:S(2)}, u32[]{:S(2)}) collective-permute-start(bf16[2,128,1,128]{3,1,0,2:T(8,128)(2,1)S(1)} %get-tuple-element.113), channel_id=1, source_target_pairs={{4,0},{8,4},{12,8},{16,12},{20,16},{24,20},{28,24},{0,28},{5,1},{9... | collective-permute-start | bytes 196616 | tf_op jit(solution)/shard_map/ppermute | solution.py:42
  11.1 9.9 %copy-start.1 = (bf16[2,128,16,128]{3,2,1,0:T(8,128)(2,1)S(1)}, bf16[2,128,16,128]{3,2,1,0:T(8,128)(2,1)}, u32[]{:S(2)}) copy-start(bf16[2,128,16,128]{3,2,1,0:T(8,128)(2,1)} %param.7) | copy-start | bytes 3145732
  11.1 5.0 %collective-permute-start.2 = (bf16[2,1,1,18,128]{4,1,3,0,2:T(2,128)(2,1)S(1)}, bf16[2,1,1,18,128]{4,1,3,0,2:T(2,128)(2,1)S(1)}, u32[]{:S(2)}, u32[]{:S(2)}) collective-permute-start(bf16[2,1,1,18,128]{4,1,3,0,2:T(2,128)(2,1)S(1)} %get-tuple-element.108), channel_id=1, source_target_pairs={{0,2},{1,3},{4,6},{5,7},{8,10},{9,11},{12,14},{13,15},{16,18},{17,... | collective-permute-start | bytes 27656 | tf_op jit(solution)/shard_map/ppermute | solution.py:41
  14.6 5.7 %collective-permute-start.3 = (bf16[2,1,1,18,128]{4,1,3,0,2:T(2,128)(2,1)S(1)}, bf16[2,1,1,18,128]{4,1,3,0,2:T(2,128)(2,1)S(1)}, u32[]{:S(2)}, u32[]{:S(2)}) collective-permute-start(bf16[2,1,1,18,128]{4,1,3,0,2:T(2,128)(2,1)S(1)} %get-tuple-element.109), channel_id=1, source_target_pairs={{2,0},{3,1},{6,4},{7,5},{10,8},{11,9},{14,12},{15,13},{18,16},{19,... | collective-permute-start | bytes 27656 | tf_op jit(solution)/shard_map/ppermute | solution.py:42
  21.0 4.0 %copy-start.2 = (bf16[2,129,1,18,128]{4,1,3,0,2:T(8,128)(2,1)}, bf16[2,129,1,18,128]{4,1,3,0,2:T(8,128)(2,1)S(1)}, u32[]{:S(2)}) copy-start(bf16[2,129,1,18,128]{4,1,3,0,2:T(8,128)(2,1)S(1)} %get-tuple-element.106) | copy-start | bytes 3566596
  21.0 3.9 %copy-start.4 = (bf16[2,129,1,18,128]{4,1,3,0,2:T(8,128)(2,1)}, bf16[2,129,1,18,128]{4,1,3,0,2:T(8,128)(2,1)S(1)}, u32[]{:S(2)}) copy-start(bf16[2,129,1,18,128]{4,1,3,0,2:T(8,128)(2,1)S(1)} %get-tuple-element.107) | copy-start | bytes 3566596
  26.4 17.9 %copy-start.20 = (f32[9,128]{1,0:T(8,128)S(1)}, f32[9,128]{1,0:T(8,128)}, u32[]{:S(2)}) copy-start(f32[9,128]{1,0:T(8,128)} %param.11) | copy-start | bytes 13828
  27.1 7.7 %collective-permute-start.4 = (bf16[2,128,2,128]{3,1,2,0:T(8,128)(2,1)S(1)}, bf16[2,128,2,128]{3,1,2,0:T(8,128)(2,1)S(1)}, u32[]{:S(2)}, u32[]{:S(2)}) collective-permute-start(bf16[2,128,2,128]{3,1,2,0:T(8,128)(2,1)S(1)} %get-tuple-element.110), channel_id=1, source_target_pairs={{0,4},{4,8},{8,12},{12,16},{16,20},{20,24},{24,28},{28,0},{1,5},{5... | collective-permute-start | bytes 393224 | tf_op jit(solution)/shard_map/ppermute | solution.py:41
  28.1 9.5 %collective-permute-start.5 = (bf16[2,128,2,128]{3,1,2,0:T(8,128)(2,1)}, bf16[2,128,2,128]{3,1,2,0:T(8,128)(2,1)}, u32[]{:S(2)}, u32[]{:S(2)}) collective-permute-start(bf16[2,128,2,128]{3,1,2,0:T(8,128)(2,1)} %get-tuple-element.111), channel_id=1, source_target_pairs={{4,0},{8,4},{12,8},{16,12},{20,16},{24,20},{28,24},{0,28},{5,1},{9... | collective-permute-start | bytes 393224 | tf_op jit(solution)/shard_map/ppermute | solution.py:42
  41.3 3.1 %collective-permute-start.6 = (bf16[2,2,1,20,128]{4,1,3,0,2:T(2,128)(2,1)S(1)}, bf16[2,2,1,20,128]{4,1,3,0,2:T(2,128)(2,1)S(1)}, u32[]{:S(2)}, u32[]{:S(2)}) collective-permute-start(bf16[2,2,1,20,128]{4,1,3,0,2:T(2,128)(2,1)S(1)} %get-tuple-element.104), channel_id=1, source_target_pairs={{0,2},{1,3},{4,6},{5,7},{8,10},{9,11},{12,14},{13,15},{16,18},{17,... | collective-permute-start | bytes 61448 | tf_op jit(solution)/shard_map/ppermute | solution.py:41
  43.0 5.7 %collective-permute-start.7 = (bf16[2,2,1,20,128]{4,1,3,0,2:T(2,128)(2,1)S(1)}, bf16[2,2,1,20,128]{4,1,3,0,2:T(2,128)(2,1)S(1)}, u32[]{:S(2)}, u32[]{:S(2)}) collective-permute-start(bf16[2,2,1,20,128]{4,1,3,0,2:T(2,128)(2,1)S(1)} %get-tuple-element.105), channel_id=1, source_target_pairs={{2,0},{3,1},{6,4},{7,5},{10,8},{11,9},{14,12},{15,13},{18,16},{19,... | collective-permute-start | bytes 61448 | tf_op jit(solution)/shard_map/ppermute | solution.py:42
  49.3 2.5 %copy-start.15 = (bf16[2,128,16,128]{3,2,1,0:T(8,128)(2,1)S(1)}, bf16[2,128,16,128]{3,2,1,0:T(8,128)(2,1)}, u32[]{:S(2)}) copy-start(bf16[2,128,16,128]{3,2,1,0:T(8,128)(2,1)} %param.8) | copy-start | bytes 3145732
  49.3 2.5 %copy-start.28 = (bf16[128,128]{1,0:T(8,128)(2,1)S(1)}, bf16[128,128]{1,0:T(8,128)(2,1)}, u32[]{:S(2)}) copy-start(bf16[128,128]{1,0:T(8,128)(2,1)} %param.12) | copy-start | bytes 98308
  51.8 5.1 %copy-start.13 = (f32[2,128,16,128]{3,1,2,0:T(8,128)}, f32[2,128,16,128]{3,1,2,0:T(8,128)S(1)}, u32[]{:S(2)}) copy-start(f32[2,128,16,128]{3,1,2,0:T(8,128)S(1)} %fusion.27) | copy-start | bytes 6291460
  68.1 3.1 %collective-permute-start.8 = (bf16[2,2,1,20,128]{4,1,3,0,2:T(2,128)(2,1)S(1)}, bf16[2,2,1,20,128]{4,1,3,0,2:T(2,128)(2,1)S(1)}, u32[]{:S(2)}, u32[]{:S(2)}) collective-permute-start(bf16[2,2,1,20,128]{4,1,3,0,2:T(2,128)(2,1)S(1)} %get-tuple-element.70), channel_id=1, source_target_pairs={{0,2},{1,3},{4,6},{5,7},{8,10},{9,11},{12,14},{13,15},{16,18},{17,... | collective-permute-start | bytes 61448 | tf_op jit(solution)/shard_map/ppermute | solution.py:41
  69.8 5.7 %collective-permute-start.9 = (bf16[2,2,1,20,128]{4,1,3,0,2:T(2,128)(2,1)S(1)}, bf16[2,2,1,20,128]{4,1,3,0,2:T(2,128)(2,1)S(1)}, u32[]{:S(2)}, u32[]{:S(2)}) collective-permute-start(bf16[2,2,1,20,128]{4,1,3,0,2:T(2,128)(2,1)S(1)} %get-tuple-element.71), channel_id=1, source_target_pairs={{2,0},{3,1},{6,4},{7,5},{10,8},{11,9},{14,12},{15,13},{18,16},{19,... | collective-permute-start | bytes 61448 | tf_op jit(solution)/shard_map/ppermute | solution.py:42
  75.5 12.9 %copy-start.16 = (bf16[2,128,16,128]{3,2,1,0:T(8,128)(2,1)S(1)}, bf16[2,128,16,128]{3,2,1,0:T(8,128)(2,1)}, u32[]{:S(2)}) copy-start(bf16[2,128,16,128]{3,2,1,0:T(8,128)(2,1)} %param.8) | copy-start | bytes 3145732
  75.9 1.6 %copy-start.6 = (f32[2,128,1,20,128]{4,1,3,0,2:T(8,128)}, f32[2,128,1,20,128]{4,1,3,0,2:T(8,128)S(1)}, u32[]{:S(2)}) copy-start(f32[2,128,1,20,128]{4,1,3,0,2:T(8,128)S(1)} %fusion) | copy-start | bytes 7864324
  83.7 7.7 %collective-permute-start.10 = (bf16[2,128,2,128]{3,1,2,0:T(8,128)(2,1)S(1)}, bf16[2,128,2,128]{3,1,2,0:T(8,128)(2,1)S(1)}, u32[]{:S(2)}, u32[]{:S(2)}) collective-permute-start(bf16[2,128,2,128]{3,1,2,0:T(8,128)(2,1)S(1)} %get-tuple-element.72), channel_id=1, source_target_pairs={{0,4},{4,8},{8,12},{12,16},{16,20},{20,24},{24,28},{28,0},{1,5},{5... | collective-permute-start | bytes 393224 | tf_op jit(solution)/shard_map/ppermute | solution.py:41
  83.8 7.7 %copy-start.17 = (bf16[2,128,16,128]{3,2,1,0:T(8,128)(2,1)S(1)}, bf16[2,128,16,128]{3,2,1,0:T(8,128)(2,1)}, u32[]{:S(2)}) copy-start(bf16[2,128,16,128]{3,2,1,0:T(8,128)(2,1)} %param.8) | copy-start | bytes 3145732
  83.8 7.6 %collective-permute-start.11 = (bf16[2,128,2,128]{3,1,2,0:T(8,128)(2,1)S(1)}, bf16[2,128,2,128]{3,1,2,0:T(8,128)(2,1)S(1)}, u32[]{:S(2)}, u32[]{:S(2)}) collective-permute-start(bf16[2,128,2,128]{3,1,2,0:T(8,128)(2,1)S(1)} %get-tuple-element.73), channel_id=1, source_target_pairs={{4,0},{8,4},{12,8},{16,12},{20,16},{24,20},{28,24},{0,28},{5,1},{9... | collective-permute-start | bytes 393224 | tf_op jit(solution)/shard_map/ppermute | solution.py:42
  88.5 3.0 %copy-start.7 = (f32[2,128,1,20,128]{4,1,3,0,2:T(8,128)S(1)}, f32[2,128,1,20,128]{4,1,3,0,2:T(8,128)}, u32[]{:S(2)}) copy-start(f32[2,128,1,20,128]{4,1,3,0,2:T(8,128)} %copy-done.6) | copy-start | bytes 7864324
  91.5 1.2 copy-start.12
  91.5 1.7 %copy-start.5 = (bf16[2,129,1,18,128]{4,1,3,0,2:T(8,128)(2,1)S(1)}, bf16[2,129,1,18,128]{4,1,3,0,2:T(8,128)(2,1)}, u32[]{:S(2)}) copy-start(bf16[2,129,1,18,128]{4,1,3,0,2:T(8,128)(2,1)} %copy-done.4) | copy-start | bytes 3566596
  91.5 2.5 %copy-start.14 = (f32[2,128,16,128]{3,1,2,0:T(8,128)S(1)}, f32[2,128,16,128]{3,1,2,0:T(8,128)}, u32[]{:S(2)}) copy-start(f32[2,128,16,128]{3,1,2,0:T(8,128)} %get-tuple-element.69) | copy-start | bytes 6291460
  92.7 6.3 %copy-start.10 = (bf16[2,128,16,128]{3,1,2,0:T(8,128)(2,1)}, bf16[2,128,16,128]{3,1,2,0:T(8,128)(2,1)S(1)}, u32[]{:S(2)}) copy-start(bf16[2,128,16,128]{3,1,2,0:T(8,128)(2,1)S(1)} %fusion.48) | copy-start | bytes 3145732
  92.7 1.9 %copy-start.3 = (bf16[2,129,1,18,128]{4,1,3,0,2:T(8,128)(2,1)S(1)}, bf16[2,129,1,18,128]{4,1,3,0,2:T(8,128)(2,1)}, u32[]{:S(2)}) copy-start(bf16[2,129,1,18,128]{4,1,3,0,2:T(8,128)(2,1)} %copy-done.2) | copy-start | bytes 3566596
  105.0 8.0 %copy-start.22 = (f32[128]{0:T(128)S(1)}, f32[128]{0:T(128)}, u32[]{:S(2)}) copy-start(f32[128]{0:T(128)} %get-tuple-element.44) | copy-start | bytes 1540
  105.0 8.0 %copy-start.23 = (f32[128]{0:T(128)S(1)}, f32[128]{0:T(128)}, u32[]{:S(2)}) copy-start(f32[128]{0:T(128)} %get-tuple-element.58) | copy-start | bytes 1540
  105.0 8.0 %copy-start.24 = (f32[128]{0:T(128)S(1)}, f32[128]{0:T(128)}, u32[]{:S(2)}) copy-start(f32[128]{0:T(128)} %get-tuple-element.59) | copy-start | bytes 1540
  105.0 8.0 %copy-start.25 = (f32[128]{0:T(128)S(1)}, f32[128]{0:T(128)}, u32[]{:S(2)}) copy-start(f32[128]{0:T(128)} %get-tuple-element.60) | copy-start | bytes 1540
  105.0 8.0 %copy-start.26 = (f32[128]{0:T(128)S(1)}, f32[128]{0:T(128)}, u32[]{:S(2)}) copy-start(f32[128]{0:T(128)} %get-tuple-element.61) | copy-start | bytes 1540
  105.0 8.0 %copy-start.27 = (f32[128]{0:T(128)S(1)}, f32[128]{0:T(128)}, u32[]{:S(2)}) copy-start(f32[128]{0:T(128)} %get-tuple-element.62) | copy-start | bytes 1540
  110.0 3.7 %collective-permute-start.12 = (bf16[2,1,1,18,128]{4,1,3,0,2:T(2,128)(2,1)S(1)}, bf16[2,1,1,18,128]{4,1,3,0,2:T(2,128)(2,1)S(1)}, u32[]{:S(2)}, u32[]{:S(2)}) collective-permute-start(bf16[2,1,1,18,128]{4,1,3,0,2:T(2,128)(2,1)S(1)} %get-tuple-element.76), channel_id=1, source_target_pairs={{0,2},{1,3},{4,6},{5,7},{8,10},{9,11},{12,14},{13,15},{16,18},{17,... | collective-permute-start | bytes 27656 | tf_op jit(solution)/shard_map/ppermute | solution.py:41
  111.7 5.7 %collective-permute-start.13 = (bf16[2,1,1,18,128]{4,1,3,0,2:T(2,128)(2,1)S(1)}, bf16[2,1,1,18,128]{4,1,3,0,2:T(2,128)(2,1)S(1)}, u32[]{:S(2)}, u32[]{:S(2)}) collective-permute-start(bf16[2,1,1,18,128]{4,1,3,0,2:T(2,128)(2,1)S(1)} %get-tuple-element.77), channel_id=1, source_target_pairs={{2,0},{3,1},{6,4},{7,5},{10,8},{11,9},{14,12},{15,13},{18,16},{19,... | collective-permute-start | bytes 27656 | tf_op jit(solution)/shard_map/ppermute | solution.py:42
  113.6 4.2 %collective-permute-start.16 = (f32[274,128]{1,0:T(8,128)S(1)}, f32[274,128]{1,0:T(8,128)S(1)}, u32[]{:S(2)}, u32[]{:S(2)}) collective-permute-start(f32[274,128]{1,0:T(8,128)S(1)} %concatenate.151), channel_id=1, source_target_pairs={{0,1},{1,0},{2,3},{3,2},{4,5},{5,4},{6,7},{7,6},{8,9},{9,8},{10,11... | collective-permute-start | bytes 420872 | tf_op jit(solution)/shard_map/ppermute | solution.py:19
  117.8 1.4 %copy-start.8 = (f32[2,128,1,18,128]{4,1,3,0,2:T(8,128)}, f32[2,128,1,18,128]{4,1,3,0,2:T(8,128)S(1)}, u32[]{:S(2)}) copy-start(f32[2,128,1,18,128]{4,1,3,0,2:T(8,128)S(1)} %fusion.1) | copy-start | bytes 7077892
  117.8 5.2 %collective-permute-start.17 = (f32[274,128]{1,0:T(8,128)S(1)}, f32[274,128]{1,0:T(8,128)S(1)}, u32[]{:S(2)}, u32[]{:S(2)}) collective-permute-start(f32[274,128]{1,0:T(8,128)S(1)} %add.289), channel_id=1, source_target_pairs={{0,2},{1,3},{2,0},{3,1},{4,6},{5,7},{6,4},{7,5},{8,10},{9,11},{10,... | collective-permute-start | bytes 420872 | tf_op jit(solution)/shard_map/ppermute | solution.py:19
  119.2 19.0 %copy-start.9 = (f32[2,128,1,18,128]{4,1,3,0,2:T(8,128)S(1)}, f32[2,128,1,18,128]{4,1,3,0,2:T(8,128)}, u32[]{:S(2)}) copy-start(f32[2,128,1,18,128]{4,1,3,0,2:T(8,128)} %copy-done.8) | copy-start | bytes 7077892
  123.0 5.9 %collective-permute-start.18 = (f32[274,128]{1,0:T(8,128)S(1)}, f32[274,128]{1,0:T(8,128)S(1)}, u32[]{:S(2)}, u32[]{:S(2)}) collective-permute-start(f32[274,128]{1,0:T(8,128)S(1)} %add.290), channel_id=1, source_target_pairs={{0,4},{1,5},{2,6},{3,7},{4,0},{5,1},{6,2},{7,3},{8,12},{9,13},{10,... | collective-permute-start | bytes 420872 | tf_op jit(solution)/shard_map/ppermute | solution.py:19
  124.1 7.6 %collective-permute-start.14 = (bf16[2,128,1,128]{3,1,0,2:T(8,128)(2,1)S(1)}, bf16[2,128,1,128]{3,1,0,2:T(8,128)(2,1)S(1)}, u32[]{:S(2)}, u32[]{:S(2)}) collective-permute-start(bf16[2,128,1,128]{3,1,0,2:T(8,128)(2,1)S(1)} %get-tuple-element.78), channel_id=1, source_target_pairs={{0,4},{4,8},{8,12},{12,16},{16,20},{20,24},{24,28},{28,0},{1,5},{5... | collective-permute-start | bytes 196616 | tf_op jit(solution)/shard_map/ppermute | solution.py:41
  126.1 5.6 %collective-permute-start.15 = (bf16[2,128,1,128]{3,1,0,2:T(8,128)(2,1)S(1)}, bf16[2,128,1,128]{3,1,0,2:T(8,128)(2,1)S(1)}, u32[]{:S(2)}, u32[]{:S(2)}) collective-permute-start(bf16[2,128,1,128]{3,1,0,2:T(8,128)(2,1)S(1)} %get-tuple-element.79), channel_id=1, source_target_pairs={{4,0},{8,4},{12,8},{16,12},{20,16},{24,20},{28,24},{0,28},{5,1},{9... | collective-permute-start | bytes 196616 | tf_op jit(solution)/shard_map/ppermute | solution.py:42
  129.0 5.2 %collective-permute-start.19 = (f32[274,128]{1,0:T(8,128)S(1)}, f32[274,128]{1,0:T(8,128)S(1)}, u32[]{:S(2)}, u32[]{:S(2)}) collective-permute-start(f32[274,128]{1,0:T(8,128)S(1)} %add.291), channel_id=1, source_target_pairs={{0,8},{1,9},{2,10},{3,11},{4,12},{5,13},{6,14},{7,15},{8,0},{9,1},... | collective-permute-start | bytes 420872 | tf_op jit(solution)/shard_map/ppermute | solution.py:19
  134.1 8.5 %collective-permute-start.20 = (f32[274,128]{1,0:T(8,128)S(1)}, f32[274,128]{1,0:T(8,128)S(1)}, u32[]{:S(2)}, u32[]{:S(2)}) collective-permute-start(f32[274,128]{1,0:T(8,128)S(1)} %add.292), channel_id=1, source_target_pairs={{0,16},{1,17},{2,18},{3,19},{4,20},{5,21},{6,22},{7,23},{8,24},{9,... | collective-permute-start | bytes 420872 | tf_op jit(solution)/shard_map/ppermute | solution.py:19
  (2 other events, 1.6 us)

commit v2 on v1

--- a/solution.py
+++ b/solution.py
@@ -2,8 +2,81 @@
 import jax.numpy as jnp
 from jax import lax
 from jax.sharding import PartitionSpec as P
+from jax.experimental import pallas as pl
+from jax.experimental.pallas import tpu as pltpu
+import functools
 
 COL_DEV = 16
+ROW_BLOCK = 8
+
+
+def conv_back_body(margin, wide_ref, gpad_ref, k_ref, gw_ref, dk_ref):
+    batch, wide_rows, wide_cols, channels = wide_ref.shape
+    row_count = wide_rows - 2 * margin
+    col_count = wide_cols - 2 * margin
+    taps = [(a, b) for a in range(3) for b in range(3)]
+    kern = k_ref[...]
+    sums = [jnp.zeros((col_count, channels), jnp.float32) for _ in taps]
+    for item in range(batch):
+
+        def tap_step(step, sums):
+            r0 = pl.multiple_of(step * ROW_BLOCK, ROW_BLOCK)
+            grad = gpad_ref[item, pl.ds(r0 + 2 * margin, ROW_BLOCK), pl.ds(2 * margin, col_count), :]
+            out = []
+            for t, (a, b) in enumerate(taps):
+                seen = wide_ref[item, pl.ds(r0 + a * margin, ROW_BLOCK), pl.ds(b * margin, col_count), :]
+                out.append(sums[t] + jnp.sum(seen * grad, axis=0))
+            return out
+
+        sums = lax.fori_loop(0, row_count // ROW_BLOCK, tap_step, sums)
+
+        def wide_step(step, carry):
+            r0 = step * ROW_BLOCK
+            total = jnp.zeros((ROW_BLOCK, wide_cols, channels), jnp.float32)
+            for t, (a, b) in enumerate(taps):
+                part = gpad_ref[
+                    item,
+                    pl.ds(r0 + 2 * margin - a * margin, ROW_BLOCK),
+                    pl.ds(2 * margin - b * margin, wide_cols),
+                    :,
+                ]
+                total = total + part * kern[t][None, None, :]
+            gw_ref[item, pl.ds(r0, ROW_BLOCK), :, :] = total
+            return carry
+
+        full = wide_rows // ROW_BLOCK
+        lax.fori_loop(0, full, wide_step, 0)
+        rest = wide_rows - full * ROW_BLOCK
+        if rest:
+            r0 = full * ROW_BLOCK
+            total = jnp.zeros((rest, wide_cols, channels), jnp.float32)
+            for t, (a, b) in enumerate(taps):
+                part = gpad_ref[
+                    item,
+                    pl.ds(r0 + 2 * margin - a * margin, rest),
+                    pl.ds(2 * margin - b * margin, wide_cols),
+                    :,
+                ]
+                total = total + part * kern[t][None, None, :]
+            gw_ref[item, pl.ds(r0, rest), :, :] = total
+    dk_ref[...] = jnp.concatenate([jnp.sum(s, axis=0, keepdims=True) for s in sums], axis=0)
+
+
+def conv_back_kernel(wide, grad, kernel, margin):
+    batch, wide_rows, wide_cols, channels = wide.shape
+    gpad = jnp.pad(grad, ((0, 0), (2 * margin, 2 * margin), (2 * margin, 2 * margin), (0, 0)))
+    elems = batch * wide_rows * wide_cols * channels
+    return pl.pallas_call(
+        functools.partial(conv_back_body, margin),
+        out_shape=(
+            jax.ShapeDtypeStruct(wide.shape, jnp.float32),
+            jax.ShapeDtypeStruct((9, channels), jnp.float32),
+        ),
+        in_specs=[pl.BlockSpec(memory_space=pltpu.VMEM)] * 3,
+        out_specs=(pl.BlockSpec(memory_space=pltpu.VMEM), pl.BlockSpec(memory_space=pltpu.VMEM)),
+        compiler_params=pltpu.CompilerParams(vmem_limit_bytes=48 * 1024 * 1024),
+        cost_estimate=pl.CostEstimate(flops=36 * elems, bytes_accessed=12 * elems, transcendentals=0),
+    )(wide.astype(jnp.float32), gpad, kernel)
 
 
 def tree_sum(value, axes):
@@ -31,9 +104,24 @@
     return out
 
 
+def swap_halo(shard, axis, dim, width, length):
+    last = lax.slice_in_dim(shard, length - width, length, axis=dim)
+    first = lax.slice_in_dim(shard, 0, width, axis=dim)
+    upper = lax.axis_index(axis) == 0
+    sent = jnp.where(upper, last, first)
+    got = lax.ppermute(sent, axis, [(0, 1), (1, 0)])
+    zeros = jnp.zeros_like(got)
+    before = jnp.where(upper, zeros, got)
+    after = jnp.where(upper, got, zeros)
+    return jnp.concatenate([before, shard, after], axis=dim)
+
+
 def with_halo(shard, sides, width, wrap):
     for axis, dim in sides:
         count, length = (lax.axis_size(axis), shard.shape[dim])
+        if count == 2 and not wrap:
+            shard = swap_halo(shard, axis, dim, width, length)
+            continue
         up = [(i, (i + 1) % count) for i in range(count if wrap else count - 1)]
         down = [(j, i) for i, j in up]
         last = lax.slice_in_dim(shard, length - width, length, axis=dim)
@@ -95,30 +183,13 @@
 
 def conv_back(widened, kernel, grad_pre, margin):
     batch_size, row_count, col_total, channels = grad_pre.shape
-    local_strips = col_total // COL_DEV
+    unused, wide_rows, local_strips, wide_cols, unused_ch = widened.shape
+    flat_wide = jnp.swapaxes(widened, 1, 2).reshape(-1, wide_rows, wide_cols, channels)
     grad_strips = grad_pre.reshape(batch_size, row_count, local_strips, COL_DEV, channels)
-    grad_wide = jnp.zeros(widened.shape, jnp.float32)
-    tap_sums = []
-    for tap_row in range(3):
-        for tap_col in range(3):
-            row_start = tap_row * margin
-            col_start = tap_col * margin
-            tap_slice = widened[
-                :, row_start : row_start + row_count, :, col_start : col_start + COL_DEV
-            ]
-            tap_sums.append(jnp.sum(tap_slice * grad_strips, axis=(0, 1, 2, 3)))
-            placed = jnp.pad(
-                kernel[3 * tap_row + tap_col] * grad_strips,
-                (
-                    (0, 0),
-                    (row_start, 2 * margin - row_start),
-                    (0, 0),
-                    (col_start, 2 * margin - col_start),
-                    (0, 0),
-                ),
-            )
-            grad_wide = grad_wide + placed
-    return (jnp.stack(tap_sums), grad_wide)
+    flat_grad = jnp.swapaxes(grad_strips, 1, 2).reshape(-1, row_count, COL_DEV, channels)
+    grad_wide, tap_sums = conv_back_kernel(flat_wide, flat_grad, kernel, margin)
+    grad_wide = grad_wide.reshape(batch_size, local_strips, wide_rows, wide_cols, channels)
+    return (tap_sums, jnp.swapaxes(grad_wide, 1, 2))
 
 
 def fold_back(grad_wide, margin, seams):

time: 145 us -> 122 us (0.84)
  other arithmetic: 38.3 us -> 22.5 us
  Pallas kernels: 0 us -> 13.5 us
  starting transfers between devices: 38.4 us -> 26.8 us
  matrix products: 12.9 us -> 3.47 us
  waiting for transfers between devices: 30.3 us -> 36 us
  local copies, waits for them, and re-layouts: 21.4 us -> 16.5 us
    ppermute x8 -> x4, waiting for transfers between devices: 16.5 us -> 1.75 us  [with_halo(): after = lax.ppermute(first, axis, down)]
    ppermute x8 -> x4, starting transfers between devices: 14.5 us -> 0.18 us  [with_halo(): before = lax.ppermute(last, axis, up)]
    pallas_call x0 -> x2, Pallas kernels: none -> 13.5 us  [conv_back_kernel(): pl.pallas_call(functools.partial(conv_back_body, margin), out_shape=(jax....]
    reduce_sum x2 -> x0, other arithmetic: 11.9 us -> none  [conv_back(): tap_sums.append(jnp.sum(tap_slice * grad_strips, axis=(0, 1, 2, 3)))]
    ppermute x8 -> x4, waiting for transfers between devices: 6.74 us -> 14.9 us  [with_halo(): before = lax.ppermute(last, axis, up)]
    dot_general x2, matrix products: 9.38 us -> 1.8 us  [block_back(): lax.dot_general(flat_grad, weight, (((1,), (1,)), ((), ())), preferred_el...]
    unnamed x60 -> x22, local copies, waits for them, and re-layouts: 9.96 us -> 2.75 us
    add x2 -> x3, other arithmetic: 10.2 us -> 3.58 us  [the longest x2 3.41 us: depthwise(): summed = summed + tap_slice * kernel[3 * tap_row + tap_col]]
  transfers between devices with their start and end apart: 21 -> 17, of which waited for: 15 -> 11; matrix products, arithmetic and copies ran while one was open for 8% -> 12% of each run, Pallas kernels for 0% -> 0%
where the time goes in v2:
time: 122 us; the launch traced here: 121 us
  waiting for transfers between devices  36 us (30%)
  starting transfers between devices  26.8 us (22%)
  other arithmetic  22.5 us (18%)
  local copies, waits for them, and re-layouts  16.5 us (14%)
  Pallas kernels  13.5 us (11%)
  matrix products  3.47 us (3%)
  between operations  2.48 us (2%)
    ppermute x4, starting transfers between devices, with_halo(): after = lax.ppermute(first, axis, down)  20.6 us
    ppermute x4, waiting for transfers between devices, with_halo(): before = lax.ppermute(last, axis, up)  14.9 us
    pallas_call x2, Pallas kernels, conv_back_kernel(): pl.pallas_call(functools.partial(conv_back_body, margin), out_shape=(jax....  13.5 us
    ppermute x5, waiting for transfers between devices, tree_sum(): value = value + lax.ppermute(value, axes, pairs)  12.9 us
    ppermute x4, waiting for transfers between devices, swap_halo(): got = lax.ppermute(sent, axis, [(0, 1), (1, 0)])  6.36 us
    ppermute x4, starting transfers between devices, swap_halo(): got = lax.ppermute(sent, axis, [(0, 1), (1, 0)])  4.95 us
    convert_element_type x1, other arithmetic, shards(): act_one = jax.nn.silu(pre_one).astype(jnp.bfloat16)  4.19 us
    pad x2, local copies, waits for them, and re-layouts, conv_back_kernel(): jnp.pad(grad, ((0, 0), (2 * margin, 2 * margin), (2 * margin, 2 * margin)...  3.84 us
  transfers between devices with their start and end apart: 17, of which 11 were waited for; matrix products, arithmetic and copies ran while one was open for 12% of the time, Pallas kernels for 0%

profile of v2, /device:TPU:0, one launch (start us, length us, event | category | flops | bytes accessed | tf_op | source)
XLA Modules:
  0.0 121.3 jit_solution(17244710785451116768)
XLA Ops:
  0.7 1.1 slice.311
  1.8 6.1 %collective-permute-start.1 = (bf16[2,128,1,128]{3,1,0,2:T(8,128)(2,1)S(1)}, bf16[2,128,1,128]{3,1,0,2:T(8,128)(2,1)S(1)}, u32[]{:S(2)}, u32[]{:S(2)}) collective-permute-start(bf16[2,128,1,128]{3,1,0,2:T(8,128)(2,1)S(1)} %bitcast.201), channel_id=1, source_target_pairs={{4,0},{8,4},{12,8},{16,12},{20,16},{24,20},{28,24},{0,28},{5,1},{9... | collective-permute-start | bytes 196616 | tf_op jit(solution)/shard_map/ppermute | solution.py:130
  7.9 1.5 %copy.70 = bf16[2,128,1,16,128]{4,1,0,3,2:T(8,128)(2,1)S(1)} copy(bf16[2,128,1,16,128]{4,3,1,0,2:T(8,128)(2,1)} %bitcast.196) | data formatting | bytes 2097152 | tf_op jit(solution)/shard_map/reshape | solution.py:150
  9.5 0.6 fusion.51
  11.5 4.9 %collective-permute-done = bf16[2,128,1,128]{3,1,0,2:T(8,128)(2,1)S(1)} collective-permute-done((bf16[2,128,1,128]{3,1,0,2:T(8,128)(2,1)S(1)}, bf16[2,128,1,128]{3,1,0,2:T(8,128)(2,1)S(1)}, u32[]{:S(2)}, u32[]{:S(2)}) %collective-permute-start) | collective-permute-done | bytes 65568 | tf_op jit(solution)/shard_map/ppermute | solution.py:129
  16.7 1.6 %collective-permute-start.2 = (bf16[2,1,1,18,128]{4,1,0,3,2:T(2,128)(2,1)S(1)}, bf16[2,1,1,18,128]{4,1,0,3,2:T(2,128)(2,1)S(1)}, u32[]{:S(2)}, u32[]{:S(2)}) collective-permute-start(bf16[2,1,1,18,128]{4,1,0,3,2:T(2,128)(2,1)S(1)} %broadcast_select_fusion.7), channel_id=1, source_target_pairs={{0,2},{2,0},{1,3},{3,1},{4,6},{6,4},{5,7},{7,5},{8,10},{10,8},{9,1... | collective-permute-start | bytes 27656 | tf_op jit(solution)/shard_map/ppermute | solution.py:112
  18.3 0.8 copy_dynamic-update-slice_fusion
  19.3 1.2 %collective-permute-done.2 = bf16[2,1,1,18,128]{4,1,0,3,2:T(2,128)(2,1)S(1)} collective-permute-done((bf16[2,1,1,18,128]{4,1,0,3,2:T(2,128)(2,1)S(1)}, bf16[2,1,1,18,128]{4,1,0,3,2:T(2,128)(2,1)S(1)}, u32[]{:S(2)}, u32[]{:S(2)}) %collective-permute-start.2) | collective-permute-done | bytes 9248 | tf_op jit(solution)/shard_map/ppermute | solution.py:112
  21.5 0.8 copy-done.3
  22.3 4.2 %multiply_convert_fusion = (bf16[2,128,16,128]{3,2,1,0:T(8,128)(2,1)S(1)}, f32[2,128,16,128]{3,2,1,0:T(8,128)}) fusion(f32[128]{0:T(128)S(1)} %get-tuple-element.95, bf16[2,129,1,18,128]{4,3,1,0,2:T(8,128)(2,1)S(1)} %copy_dynamic-update-slice_fusion.1, f32[128]{0:T(128)S(1)} %get-tuple-element.88, f32[128]{0:T(128)S(1)} %get-tuple-element.89, ...), kind=kLoop, calls=%fused_computation.40 | loop fusion | flops 15204352 | bytes 10619904 | tf_op jit(solution)/shard_map/convert_element_type | solution.py:272
  27.2 4.9 %collective-permute-start.4 = (bf16[2,128,2,128]{3,2,1,0:T(2,128)(2,1)S(1)}, bf16[2,128,2,128]{3,2,1,0:T(2,128)(2,1)S(1)}, u32[]{:S(2)}, u32[]{:S(2)}) collective-permute-start(bf16[2,128,2,128]{3,2,1,0:T(2,128)(2,1)S(1)} %get-tuple-element.57), channel_id=1, source_target_pairs={{4,0},{8,4},{12,8},{16,12},{20,16},{24,20},{28,24},{0,28},{5,1},{9... | collective-permute-start | bytes 393224 | tf_op jit(solution)/shard_map/ppermute | solution.py:130
  32.1 2.7 %collective-permute-done.3 = bf16[2,128,2,128]{3,2,1,0:T(2,128)(2,1)S(1)} collective-permute-done((bf16[2,128,2,128]{3,2,1,0:T(2,128)(2,1)S(1)}, bf16[2,128,2,128]{3,2,1,0:T(2,128)(2,1)S(1)}, u32[]{:S(2)}, u32[]{:S(2)}) %collective-permute-start.3) | collective-permute-done | bytes 131104 | tf_op jit(solution)/shard_map/ppermute | solution.py:129
  35.2 1.6 %collective-permute-start.5 = (bf16[2,2,1,20,128]{4,3,1,0,2:T(8,128)(2,1)S(1)}, bf16[2,2,1,20,128]{4,3,1,0,2:T(8,128)(2,1)S(1)}, u32[]{:S(2)}, u32[]{:S(2)}) collective-permute-start(bf16[2,2,1,20,128]{4,3,1,0,2:T(8,128)(2,1)S(1)} %fusion.41), channel_id=1, source_target_pairs={{0,2},{2,0},{1,3},{3,1},{4,6},{6,4},{5,7},{7,5},{8,10},{10,8},{9,1... | collective-permute-start | bytes 61448 | tf_op jit(solution)/shard_map/ppermute | solution.py:112
  37.2 2.5 %copy.83.wide_ref = f32[2,130,18,128]{3,2,1,0:T(8,128)} copy(f32[2,130,18,128]{3,1,0,2:T(8,128)S(1)} %fusion.26) | data formatting | bytes 4792320 | tf_op jit(solution)/shard_map/convert_element_type | solution.py:79
  39.7 1.9 %maximum_maximum_fusion = (bf16[2,130,1,20,128]{4,3,1,0,2:T(8,128)(2,1)S(1)}, bf16[2,130,1,20,128]{4,3,1,0,2:T(8,128)(2,1)S(1)}) fusion(bf16[2,128,1,2,128]{4,3,1,0,2:T(2,128)(2,1)S(1)} %fusion.31, bf16[2,128,1,16,128]{4,3,1,0,2:T(8,128)(2,1)S(1)} %bitcast.192, bf16[2,128,1,2,128]{4,3,1,0,2:T(2,128)(2,1)S(1)} %fusion.30, ...), kind=kLoop, calls=%fused_computation.45 | loop fusion | flops 10649600 | bytes 4014080 | tf_op jit(solution)/shard_map/concatenate | solution.py:166
  41.6 2.5 %fusion.25.wide_ref = f32[2,132,20,128]{3,2,1,0:T(8,128)} fusion(bf16[2,2,1,20,128]{4,3,1,0,2:T(8,128)(2,1)S(1)} %get-tuple-element.73, bf16[2,128,1,2,128]{4,3,1,0,2:T(2,128)(2,1)S(1)} %fusion.31, bf16[2,128,1,16,128]{4,3,1,0,2:T(8,128)(2,1)S(1)} %bitcast.193, bf16[2,128,1,2,128]{4,3,1,0,2:T(2,128)(2,1)S(1)} %fusion.30, ...), kind=kLoop, calls=%fused_computation.44 | loop fusion | flops 7434240 | bytes 4055040 | tf_op jit(solution)/shard_map/convert_element_type | solution.py:79
  44.1 3.0 %fusion.24 = f32[2,128,1,16,128]{4,3,1,0,2:T(8,128)S(1)} fusion(bf16[2,128,16,128]{3,2,1,0:T(8,128)(2,1)S(1)} %fusion.9, bf16[2,130,1,20,128]{4,3,1,0,2:T(8,128)(2,1)S(1)} %get-tuple-element.55, bf16[2,128,1,2,128]{4,3,1,0,2:T(2,128)(2,1)S(1)} %fusion.31, bf16[2,128,1,16,128]{4,3,1,0,2:T(8,128)(2,1)S(1)} %bitcast.194, ...), kind=kLoop, calls=%fused_computation.36 | loop fusion | flops 16777216 | bytes 10752512 | tf_op jit(solution)/shard_map/add | solution.py:180
  47.1 0.9 fusion.19
  48.0 1.9 %pad.40.gpad_ref = f32[2,136,24,128]{3,2,1,0:T(8,128)} pad(f32[2,128,16,128]{3,2,1,0:T(8,128)S(1)} %fusion.19, f32[]{:T(128)} %constant.70.clone.1), padding=0_0x4_4x4_4x0_0 | pad | bytes 5439492 | tf_op jit(solution)/shard_map/jit(_pad)/pad | solution.py:67
  49.9 6.9 %shard_map.110 = (f32[2,132,20,128]{3,2,1,0:T(8,128)S(1)}, f32[9,128]{1,0:T(8,128)S(1)}) custom-call(f32[2,132,20,128]{3,2,1,0:T(8,128)} %fusion.25.wide_ref, f32[2,136,24,128]{3,2,1,0:T(8,128)} %pad.40.gpad_ref, f32[9,128]{1,0:T(8,128)S(1)} %copy-done.1), custom_call_target="tpu_custom_call" | custom-call | flops 24330240 | bytes 8110080 | tf_op jit(solution)/shard_map/pallas_call | solution.py:69
  56.9 0.9 collective-permute-start.6
  57.8 3.0 %collective-permute-done.6 = bf16[2,2,1,20,128]{4,3,1,0,2:T(8,128)(2,1)S(1)} collective-permute-done((bf16[2,2,1,20,128]{4,3,1,0,2:T(8,128)(2,1)S(1)}, bf16[2,2,1,20,128]{4,3,1,0,2:T(8,128)(2,1)S(1)}, u32[]{:S(2)}, u32[]{:S(2)}) %collective-permute-start.6) | collective-permute-done | bytes 20512 | tf_op jit(solution)/shard_map/ppermute | solution.py:112
  61.5 4.9 %collective-permute-start.8 = (bf16[2,128,2,128]{3,2,1,0:T(2,128)(2,1)S(1)}, bf16[2,128,2,128]{3,2,1,0:T(2,128)(2,1)S(1)}, u32[]{:S(2)}, u32[]{:S(2)}) collective-permute-start(bf16[2,128,2,128]{3,2,1,0:T(2,128)(2,1)S(1)} %fusion.32), channel_id=1, source_target_pairs={{4,0},{8,4},{12,8},{16,12},{20,16},{24,20},{28,24},{0,28},{5,1},{9... | collective-permute-start | bytes 393224 | tf_op jit(solution)/shard_map/ppermute | solution.py:130
  66.3 0.8 convolution_bitcast_fusion
  67.1 1.7 %collective-permute-done.8 = bf16[2,128,2,128]{3,2,1,0:T(2,128)(2,1)S(1)} collective-permute-done((bf16[2,128,2,128]{3,2,1,0:T(2,128)(2,1)S(1)}, bf16[2,128,2,128]{3,2,1,0:T(2,128)(2,1)S(1)}, u32[]{:S(2)}, u32[]{:S(2)}) %collective-permute-start.8) | collective-permute-done | bytes 131104 | tf_op jit(solution)/shard_map/ppermute | solution.py:130
  68.9 5.1 %collective-permute-done.7 = bf16[2,128,2,128]{3,2,1,0:T(2,128)(2,1)S(1)} collective-permute-done((bf16[2,128,2,128]{3,2,1,0:T(2,128)(2,1)S(1)}, bf16[2,128,2,128]{3,2,1,0:T(2,128)(2,1)S(1)}, u32[]{:S(2)}, u32[]{:S(2)}) %collective-permute-start.7) | collective-permute-done | bytes 131104 | tf_op jit(solution)/shard_map/ppermute | solution.py:129
  74.0 1.0 convert_bitcast_fusion
  76.1 1.1 copy-done.4
  77.2 0.9 add_multiply_fusion
  78.1 1.9 %pad.45.gpad_ref = f32[2,132,20,128]{3,2,1,0:T(8,128)} pad(f32[2,128,16,128]{3,2,1,0:T(8,128)S(1)} %add_multiply_fusion, f32[]{:T(128)} %constant.70.clone.1), padding=0_0x2_2x2_2x0_0 | pad | bytes 4800516 | tf_op jit(solution)/shard_map/jit(_pad)/pad | solution.py:67
  80.0 6.6 %shard_map.111 = (f32[2,130,18,128]{3,2,1,0:T(8,128)S(1)}, f32[9,128]{1,0:T(8,128)S(1)}) custom-call(f32[2,130,18,128]{3,2,1,0:T(8,128)} %copy.83.wide_ref, f32[2,132,20,128]{3,2,1,0:T(8,128)} %pad.45.gpad_ref, f32[9,128]{1,0:T(8,128)S(1)} %copy-done.2), custom_call_target="tpu_custom_call" | custom-call | flops 21565440 | bytes 7188480 | tf_op jit(solution)/shard_map/pallas_call | solution.py:69
  87.2 0.9 collective-permute-start.9
  88.1 0.7 pad_maximum_fusion.6
  88.8 2.2 %collective-permute-done.9 = bf16[2,1,1,18,128]{4,1,0,3,2:T(2,128)(2,1)S(1)} collective-permute-done((bf16[2,1,1,18,128]{4,1,0,3,2:T(2,128)(2,1)S(1)}, bf16[2,1,1,18,128]{4,1,0,3,2:T(2,128)(2,1)S(1)}, u32[]{:S(2)}, u32[]{:S(2)}) %collective-permute-start.9) | collective-permute-done | bytes 9248 | tf_op jit(solution)/shard_map/ppermute | solution.py:112
  91.5 0.7 fusion.50
  92.2 0.8 rev.18
  93.0 1.4 %rev.19 = bf16[2,128,1,1,128]{4,1,0,3,2:T(8,128)(2,1)} reverse(bf16[2,128,1,1,128]{4,1,0,3,2:T(8,128)(2,1)} %get-tuple-element.53), dimensions={1} | reverse | bytes 131072 | tf_op jit(solution)/shard_map/rev | solution.py:212
  94.4 1.0 fusion.58
  95.4 0.9 collective-permute-start.13
  96.3 0.9 fusion.34
  97.2 4.7 %collective-permute-start.11 = (bf16[2,128,1,128]{3,1,0,2:T(8,128)(2,1)S(1)}, bf16[2,128,1,128]{3,1,0,2:T(8,128)(2,1)S(1)}, u32[]{:S(2)}, u32[]{:S(2)}) collective-permute-start(bf16[2,128,1,128]{3,1,0,2:T(8,128)(2,1)S(1)} %get-tuple-element.51), channel_id=1, source_target_pairs={{4,0},{8,4},{12,8},{16,12},{20,16},{24,20},{28,24},{0,28},{5,1},{9... | collective-permute-start | bytes 196616 | tf_op jit(solution)/shard_map/ppermute | solution.py:130
  102.1 2.2 %collective-permute-done.10 = bf16[2,128,1,128]{3,1,0,2:T(8,128)(2,1)S(1)} collective-permute-done((bf16[2,128,1,128]{3,1,0,2:T(8,128)(2,1)S(1)}, bf16[2,128,1,128]{3,1,0,2:T(8,128)(2,1)S(1)}, u32[]{:S(2)}, u32[]{:S(2)}) %collective-permute-start.10) | collective-permute-done | bytes 65568 | tf_op jit(solution)/shard_map/ppermute | solution.py:129
  104.3 2.8 %collective-permute-done.14 = f32[274,128]{1,0:T(8,128)S(1)} collective-permute-done((f32[274,128]{1,0:T(8,128)S(1)}, f32[274,128]{1,0:T(8,128)S(1)}, u32[]{:S(2)}, u32[]{:S(2)}) %collective-permute-start.14) | collective-permute-done | bytes 140320 | tf_op jit(solution)/shard_map/ppermute | solution.py:92
  107.4 4.9 %collective-permute-done.15 = f32[274,128]{1,0:T(8,128)S(1)} collective-permute-done((f32[274,128]{1,0:T(8,128)S(1)}, f32[274,128]{1,0:T(8,128)S(1)}, u32[]{:S(2)}, u32[]{:S(2)}) %collective-permute-start.15) | collective-permute-done | bytes 140320 | tf_op jit(solution)/shard_map/ppermute | solution.py:92
  112.4 2.3 %fusion.14 = bf16[2,128,16,128]{3,2,1,0:T(8,128)(2,1)} fusion(f32[2,128,1,16,128]{4,1,0,3,2:T(8,128)S(1)} %slice_add_fusion.2, f32[2,128,1,1,128]{4,3,1,0,2:T(1,128)S(1)} %bitcast.200, bf16[2,128,16,128]{3,2,1,0:T(8,128)(2,1)S(1)} %fusion.13), kind=kLoop, calls=%fused_computation.22 | loop fusion | flops 2097152 | bytes 4325376 | tf_op jit(solution)/shard_map/convert_element_type | solution.py:254
  114.8 5.2 %collective-permute-done.16 = f32[274,128]{1,0:T(8,128)S(1)} collective-permute-done((f32[274,128]{1,0:T(8,128)S(1)}, f32[274,128]{1,0:T(8,128)S(1)}, u32[]{:S(2)}, u32[]{:S(2)}) %collective-permute-start.16) | collective-permute-done | bytes 140320 | tf_op jit(solution)/shard_map/ppermute | solution.py:92
  120.0 0.6 slice_multiply_fusion.2
  120.6 0.7 slice_multiply_fusion
  (77 shorter events, 6.5 us)
Async XLA Ops:
  0.6 25.8 %copy-start = (bf16[128,128]{1,0:T(8,128)(2,1)S(1)}, bf16[128,128]{1,0:T(8,128)(2,1)}, u32[]{:S(2)}) copy-start(bf16[128,128]{1,0:T(8,128)(2,1)} %param.10) | copy-start | bytes 98308
  0.6 8.8 %copy-start.2 = (f32[9,128]{1,0:T(8,128)S(1)}, f32[9,128]{1,0:T(8,128)}, u32[]{:S(2)}) copy-start(f32[9,128]{1,0:T(8,128)} %k_ref.3) | copy-start | bytes 13828
  0.7 8.9 %copy-start.8 = (s32[2,8]{1,0:T(2,128)S(1)}, s32[2,8]{1,0:T(2,128)}, u32[]{:S(2)}) copy-start(s32[2,8]{1,0:T(2,128)} %param.13) | copy-start | bytes 196
  1.8 9.6 %collective-permute-start.1 = (bf16[2,128,1,128]{3,1,0,2:T(8,128)(2,1)S(1)}, bf16[2,128,1,128]{3,1,0,2:T(8,128)(2,1)S(1)}, u32[]{:S(2)}, u32[]{:S(2)}) collective-permute-start(bf16[2,128,1,128]{3,1,0,2:T(8,128)(2,1)S(1)} %bitcast.201), channel_id=1, source_target_pairs={{4,0},{8,4},{12,8},{16,12},{20,16},{24,20},{28,24},{0,28},{5,1},{9... | collective-permute-start | bytes 196616 | tf_op jit(solution)/shard_map/ppermute | solution.py:130
  9.4 7.0 %collective-permute-start = (bf16[2,128,1,128]{3,1,0,2:T(8,128)(2,1)S(1)}, bf16[2,128,1,128]{3,1,0,2:T(8,128)(2,1)S(1)}, u32[]{:S(2)}, u32[]{:S(2)}) collective-permute-start(bf16[2,128,1,128]{3,1,0,2:T(8,128)(2,1)S(1)} %slice_bitcast_fusion.2), channel_id=1, source_target_pairs={{0,4},{4,8},{8,12},{12,16},{16,20},{20,24},{24,28},{28,0},{1,5},{5... | collective-permute-start | bytes 196616 | tf_op jit(solution)/shard_map/ppermute | solution.py:129
  16.7 3.8 %collective-permute-start.2 = (bf16[2,1,1,18,128]{4,1,0,3,2:T(2,128)(2,1)S(1)}, bf16[2,1,1,18,128]{4,1,0,3,2:T(2,128)(2,1)S(1)}, u32[]{:S(2)}, u32[]{:S(2)}) collective-permute-start(bf16[2,1,1,18,128]{4,1,0,3,2:T(2,128)(2,1)S(1)} %broadcast_select_fusion.7), channel_id=1, source_target_pairs={{0,2},{2,0},{1,3},{3,1},{4,6},{6,4},{5,7},{7,5},{8,10},{10,8},{9,1... | collective-permute-start | bytes 27656 | tf_op jit(solution)/shard_map/ppermute | solution.py:112
  21.1 1.2 %copy-start.3 = (bf16[2,128,16,128]{3,2,1,0:T(8,128)(2,1)S(1)}, bf16[2,128,16,128]{3,2,1,0:T(8,128)(2,1)}, u32[]{:S(2)}) copy-start(bf16[2,128,16,128]{3,2,1,0:T(8,128)(2,1)} %param.7) | copy-start | bytes 3145732
  26.5 0.7 copy-start.1
  27.1 7.7 %collective-permute-start.3 = (bf16[2,128,2,128]{3,2,1,0:T(2,128)(2,1)S(1)}, bf16[2,128,2,128]{3,2,1,0:T(2,128)(2,1)S(1)}, u32[]{:S(2)}, u32[]{:S(2)}) collective-permute-start(bf16[2,128,2,128]{3,2,1,0:T(2,128)(2,1)S(1)} %get-tuple-element.56), channel_id=1, source_target_pairs={{0,4},{4,8},{8,12},{12,16},{16,20},{20,24},{24,28},{28,0},{1,5},{5... | collective-permute-start | bytes 393224 | tf_op jit(solution)/shard_map/ppermute | solution.py:129
  27.2 7.8 %collective-permute-start.4 = (bf16[2,128,2,128]{3,2,1,0:T(2,128)(2,1)S(1)}, bf16[2,128,2,128]{3,2,1,0:T(2,128)(2,1)S(1)}, u32[]{:S(2)}, u32[]{:S(2)}) collective-permute-start(bf16[2,128,2,128]{3,2,1,0:T(2,128)(2,1)S(1)} %get-tuple-element.57), channel_id=1, source_target_pairs={{4,0},{8,4},{12,8},{16,12},{20,16},{24,20},{28,24},{0,28},{5,1},{9... | collective-permute-start | bytes 393224 | tf_op jit(solution)/shard_map/ppermute | solution.py:130
  35.2 4.5 %collective-permute-start.5 = (bf16[2,2,1,20,128]{4,3,1,0,2:T(8,128)(2,1)S(1)}, bf16[2,2,1,20,128]{4,3,1,0,2:T(8,128)(2,1)S(1)}, u32[]{:S(2)}, u32[]{:S(2)}) collective-permute-start(bf16[2,2,1,20,128]{4,3,1,0,2:T(8,128)(2,1)S(1)} %fusion.41), channel_id=1, source_target_pairs={{0,2},{2,0},{1,3},{3,1},{4,6},{6,4},{5,7},{7,5},{8,10},{10,8},{9,1... | collective-permute-start | bytes 61448 | tf_op jit(solution)/shard_map/ppermute | solution.py:112
  44.1 3.0 %copy-start.5 = (bf16[2,128,16,128]{3,2,1,0:T(8,128)(2,1)S(1)}, bf16[2,128,16,128]{3,2,1,0:T(8,128)(2,1)}, u32[]{:S(2)}) copy-start(bf16[2,128,16,128]{3,2,1,0:T(8,128)(2,1)} %param.8) | copy-start | bytes 3145732
  44.1 3.0 %copy-start.9 = (bf16[128,128]{1,0:T(8,128)(2,1)S(1)}, bf16[128,128]{1,0:T(8,128)(2,1)}, u32[]{:S(2)}) copy-start(bf16[128,128]{1,0:T(8,128)(2,1)} %param.12) | copy-start | bytes 98308
  56.9 3.9 %collective-permute-start.6 = (bf16[2,2,1,20,128]{4,3,1,0,2:T(8,128)(2,1)S(1)}, bf16[2,2,1,20,128]{4,3,1,0,2:T(8,128)(2,1)S(1)}, u32[]{:S(2)}, u32[]{:S(2)}) collective-permute-start(bf16[2,2,1,20,128]{4,3,1,0,2:T(8,128)(2,1)S(1)} %get-tuple-element.44), channel_id=1, source_target_pairs={{0,2},{2,0},{1,3},{3,1},{4,6},{6,4},{5,7},{7,5},{8,10},{10,8},{9,1... | collective-permute-start | bytes 61448 | tf_op jit(solution)/shard_map/ppermute | solution.py:112
  61.5 7.4 %collective-permute-start.8 = (bf16[2,128,2,128]{3,2,1,0:T(2,128)(2,1)S(1)}, bf16[2,128,2,128]{3,2,1,0:T(2,128)(2,1)S(1)}, u32[]{:S(2)}, u32[]{:S(2)}) collective-permute-start(bf16[2,128,2,128]{3,2,1,0:T(2,128)(2,1)S(1)} %fusion.32), channel_id=1, source_target_pairs={{4,0},{8,4},{12,8},{16,12},{20,16},{24,20},{28,24},{0,28},{5,1},{9... | collective-permute-start | bytes 393224 | tf_op jit(solution)/shard_map/ppermute | solution.py:130
  66.3 7.7 %collective-permute-start.7 = (bf16[2,128,2,128]{3,2,1,0:T(2,128)(2,1)S(1)}, bf16[2,128,2,128]{3,2,1,0:T(2,128)(2,1)S(1)}, u32[]{:S(2)}, u32[]{:S(2)}) collective-permute-start(bf16[2,128,2,128]{3,2,1,0:T(2,128)(2,1)S(1)} %fusion.33), channel_id=1, source_target_pairs={{0,4},{4,8},{8,12},{12,16},{16,20},{20,24},{24,28},{28,0},{1,5},{5... | collective-permute-start | bytes 393224 | tf_op jit(solution)/shard_map/ppermute | solution.py:129
  67.1 21.0 %copy-start.6 = (f32[128,128]{1,0:T(8,128)}, f32[128,128]{1,0:T(8,128)S(1)}, u32[]{:S(2)}) copy-start(f32[128,128]{1,0:T(8,128)S(1)} %convolution_bitcast_fusion) | copy-start | bytes 196612
  75.6 1.6 %copy-start.4 = (f32[2,128,16,128]{3,2,1,0:T(8,128)S(1)}, f32[2,128,16,128]{3,2,1,0:T(8,128)}, u32[]{:S(2)}) copy-start(f32[2,128,16,128]{3,2,1,0:T(8,128)} %get-tuple-element.41) | copy-start | bytes 6291460
  76.1 12.0 %copy-start.7 = (f32[128,128]{1,0:T(8,128)}, f32[128,128]{1,0:T(8,128)S(1)}, u32[]{:S(2)}) copy-start(f32[128,128]{1,0:T(8,128)S(1)} %convolution_bitcast_fusion.1) | copy-start | bytes 196612
  87.2 3.8 %collective-permute-start.9 = (bf16[2,1,1,18,128]{4,1,0,3,2:T(2,128)(2,1)S(1)}, bf16[2,1,1,18,128]{4,1,0,3,2:T(2,128)(2,1)S(1)}, u32[]{:S(2)}, u32[]{:S(2)}) collective-permute-start(bf16[2,1,1,18,128]{4,1,0,3,2:T(2,128)(2,1)S(1)} %get-tuple-element.49), channel_id=1, source_target_pairs={{0,2},{2,0},{1,3},{3,1},{4,6},{6,4},{5,7},{7,5},{8,10},{10,8},{9,1... | collective-permute-start | bytes 27656 | tf_op jit(solution)/shard_map/ppermute | solution.py:112
  88.8 5.6 %collective-permute-start.12 = (f32[274,128]{1,0:T(8,128)}, f32[274,128]{1,0:T(8,128)}, u32[]{:S(2)}, u32[]{:S(2)}) collective-permute-start(f32[274,128]{1,0:T(8,128)} %pad_maximum_fusion.6), channel_id=1, source_target_pairs={{0,1},{1,0},{2,3},{3,2},{4,5},{5,4},{6,7},{7,6},{8,9},{9,8},{10,11... | collective-permute-start | bytes 420872 | tf_op jit(solution)/shard_map/ppermute | solution.py:92
  95.4 6.6 %collective-permute-start.13 = (f32[274,128]{1,0:T(8,128)S(1)}, f32[274,128]{1,0:T(8,128)S(1)}, u32[]{:S(2)}, u32[]{:S(2)}) collective-permute-start(f32[274,128]{1,0:T(8,128)S(1)} %fusion.58), channel_id=1, source_target_pairs={{0,2},{1,3},{2,0},{3,1},{4,6},{5,7},{6,4},{7,5},{8,10},{9,11},{10,... | collective-permute-start | bytes 420872 | tf_op jit(solution)/shard_map/ppermute | solution.py:92
  97.2 7.1 %collective-permute-start.10 = (bf16[2,128,1,128]{3,1,0,2:T(8,128)(2,1)S(1)}, bf16[2,128,1,128]{3,1,0,2:T(8,128)(2,1)S(1)}, u32[]{:S(2)}, u32[]{:S(2)}) collective-permute-start(bf16[2,128,1,128]{3,1,0,2:T(8,128)(2,1)S(1)} %get-tuple-element.50), channel_id=1, source_target_pairs={{0,4},{4,8},{8,12},{12,16},{16,20},{20,24},{24,28},{28,0},{1,5},{5... | collective-permute-start | bytes 196616 | tf_op jit(solution)/shard_map/ppermute | solution.py:129
  97.2 7.1 %collective-permute-start.11 = (bf16[2,128,1,128]{3,1,0,2:T(8,128)(2,1)S(1)}, bf16[2,128,1,128]{3,1,0,2:T(8,128)(2,1)S(1)}, u32[]{:S(2)}, u32[]{:S(2)}) collective-permute-start(bf16[2,128,1,128]{3,1,0,2:T(8,128)(2,1)S(1)} %get-tuple-element.51), channel_id=1, source_target_pairs={{4,0},{8,4},{12,8},{16,12},{20,16},{24,20},{28,24},{0,28},{5,1},{9... | collective-permute-start | bytes 196616 | tf_op jit(solution)/shard_map/ppermute | solution.py:130
  102.0 5.2 %collective-permute-start.14 = (f32[274,128]{1,0:T(8,128)S(1)}, f32[274,128]{1,0:T(8,128)S(1)}, u32[]{:S(2)}, u32[]{:S(2)}) collective-permute-start(f32[274,128]{1,0:T(8,128)S(1)} %add.194), channel_id=1, source_target_pairs={{0,4},{1,5},{2,6},{3,7},{4,0},{5,1},{6,2},{7,3},{8,12},{9,13},{10,... | collective-permute-start | bytes 420872 | tf_op jit(solution)/shard_map/ppermute | solution.py:92
  107.2 5.2 %collective-permute-start.15 = (f32[274,128]{1,0:T(8,128)S(1)}, f32[274,128]{1,0:T(8,128)S(1)}, u32[]{:S(2)}, u32[]{:S(2)}) collective-permute-start(f32[274,128]{1,0:T(8,128)S(1)} %add.195), channel_id=1, source_target_pairs={{0,8},{1,9},{2,10},{3,11},{4,12},{5,13},{6,14},{7,15},{8,0},{9,1},... | collective-permute-start | bytes 420872 | tf_op jit(solution)/shard_map/ppermute | solution.py:92
  112.4 7.6 %collective-permute-start.16 = (f32[274,128]{1,0:T(8,128)S(1)}, f32[274,128]{1,0:T(8,128)S(1)}, u32[]{:S(2)}, u32[]{:S(2)}) collective-permute-start(f32[274,128]{1,0:T(8,128)S(1)} %add.196), channel_id=1, source_target_pairs={{0,16},{1,17},{2,18},{3,19},{4,20},{5,21},{6,22},{7,23},{8,24},{9,... | collective-permute-start | bytes 420872 | tf_op jit(solution)/shard_map/ppermute | solution.py:92

commit v3 on v2

--- a/solution.py
+++ b/solution.py
@@ -10,7 +10,7 @@
 ROW_BLOCK = 8
 
 
-def conv_back_body(margin, wide_ref, gpad_ref, k_ref, gw_ref, dk_ref):
+def conv_back_body(margin, wide_ref, grad_ref, k_ref, gw_ref, dk_ref, gpad_ref):
     batch, wide_rows, wide_cols, channels = wide_ref.shape
     row_count = wide_rows - 2 * margin
     col_count = wide_cols - 2 * margin
@@ -18,10 +18,20 @@
     kern = k_ref[...]
     sums = [jnp.zeros((col_count, channels), jnp.float32) for _ in taps]
     for item in range(batch):
+        gpad_ref[...] = jnp.zeros(gpad_ref.shape, jnp.float32)
+
+        def fill_step(step, carry):
+            r0 = pl.multiple_of(step * ROW_BLOCK, ROW_BLOCK)
+            gpad_ref[pl.ds(r0 + 2 * margin, ROW_BLOCK), pl.ds(2 * margin, col_count), :] = grad_ref[
+                item, pl.ds(r0, ROW_BLOCK)
+            ]
+            return carry
+
+        lax.fori_loop(0, row_count // ROW_BLOCK, fill_step, 0)
 
         def tap_step(step, sums):
             r0 = pl.multiple_of(step * ROW_BLOCK, ROW_BLOCK)
-            grad = gpad_ref[item, pl.ds(r0 + 2 * margin, ROW_BLOCK), pl.ds(2 * margin, col_count), :]
+            grad = grad_ref[item, pl.ds(r0, ROW_BLOCK)]
             out = []
             for t, (a, b) in enumerate(taps):
                 seen = wide_ref[item, pl.ds(r0 + a * margin, ROW_BLOCK), pl.ds(b * margin, col_count), :]
@@ -35,7 +45,6 @@
             total = jnp.zeros((ROW_BLOCK, wide_cols, channels), jnp.float32)
             for t, (a, b) in enumerate(taps):
                 part = gpad_ref[
-                    item,
                     pl.ds(r0 + 2 * margin - a * margin, ROW_BLOCK),
                     pl.ds(2 * margin - b * margin, wide_cols),
                     :,
@@ -52,7 +61,6 @@
             total = jnp.zeros((rest, wide_cols, channels), jnp.float32)
             for t, (a, b) in enumerate(taps):
                 part = gpad_ref[
-                    item,
                     pl.ds(r0 + 2 * margin - a * margin, rest),
                     pl.ds(2 * margin - b * margin, wide_cols),
                     :,
@@ -64,8 +72,9 @@
 
 def conv_back_kernel(wide, grad, kernel, margin):
     batch, wide_rows, wide_cols, channels = wide.shape
-    gpad = jnp.pad(grad, ((0, 0), (2 * margin, 2 * margin), (2 * margin, 2 * margin), (0, 0)))
     elems = batch * wide_rows * wide_cols * channels
+    pad_rows = grad.shape[1] + 4 * margin
+    pad_cols = -(-(grad.shape[2] + 4 * margin) // 8) * 8
     return pl.pallas_call(
         functools.partial(conv_back_body, margin),
         out_shape=(
@@ -74,9 +83,10 @@
         ),
         in_specs=[pl.BlockSpec(memory_space=pltpu.VMEM)] * 3,
         out_specs=(pl.BlockSpec(memory_space=pltpu.VMEM), pl.BlockSpec(memory_space=pltpu.VMEM)),
+        scratch_shapes=[pltpu.VMEM((pad_rows, pad_cols, channels), jnp.float32)],
         compiler_params=pltpu.CompilerParams(vmem_limit_bytes=48 * 1024 * 1024),
         cost_estimate=pl.CostEstimate(flops=36 * elems, bytes_accessed=12 * elems, transcendentals=0),
-    )(wide.astype(jnp.float32), gpad, kernel)
+    )(wide.astype(jnp.float32), grad, kernel)
 
 
 def tree_sum(value, axes):
@@ -267,11 +277,11 @@
         * lax.axis_size("dp")
     )
     factor = float(cells_all) ** (-0.5)
-    wide_one = extend(fields, 1, seams)
+    wide_one = extend(fields, 1, seams).astype(jnp.float32)
     pre_one = depthwise(wide_one, kernel_one, 1, row_count)
     act_one = jax.nn.silu(pre_one).astype(jnp.bfloat16)
     hidden = (fields.astype(jnp.float32) + pointwise(act_one, weight_one)).astype(jnp.bfloat16)
-    wide_two = extend(hidden, 2, seams)
+    wide_two = extend(hidden, 2, seams).astype(jnp.float32)
     pre_two = depthwise(wide_two, kernel_two, 2, row_count)
     act_two = jax.nn.silu(pre_two).astype(jnp.bfloat16)
     grad_hidden, dk_two, dw_two = block_back(

time: 122 us -> 100 us (0.82)
  waiting for transfers between devices: 36 us -> 22.4 us
  local copies, waits for them, and re-layouts: 16.5 us -> 8.83 us
  starting transfers between devices: 26.8 us -> 34 us
  other arithmetic: 22.5 us -> 17.3 us
  Pallas kernels: 13.5 us -> 12 us
    ppermute x4, waiting for transfers between devices: 14.9 us -> 6.83 us  [with_halo(): before = lax.ppermute(last, axis, up)]
    ppermute x4, starting transfers between devices: 0.18 us -> 5.89 us  [with_halo(): before = lax.ppermute(last, axis, up)]
    ppermute x4, starting transfers between devices: 20.6 us -> 15.5 us  [with_halo(): after = lax.ppermute(first, axis, down)]
    ppermute x5, starting transfers between devices: 1.14 us -> 5.77 us  [tree_sum(): value = value + lax.ppermute(value, axes, pairs)]
    ppermute x5, waiting for transfers between devices: 12.9 us -> 9.07 us  [tree_sum(): value = value + lax.ppermute(value, axes, pairs)]
    pad x2 -> x0, local copies, waits for them, and re-layouts: 3.84 us -> none  [conv_back_kernel(): jnp.pad(grad, ((0, 0), (2 * margin, 2 * margin), (2 * margin, 2 * margin)...]
    convert_element_type x2 -> x5, other arithmetic: 2.93 us -> 6.58 us  [the longest x2 2.9 us: shards(): wide_one = extend(fields, 1, seams).astype(jnp.float32)]
    add x3 -> x0, other arithmetic: 3.58 us -> none  [the longest x2 3.41 us: depthwise(): summed = summed + tap_slice * kernel[3 * tap_row + tap_col]]
  transfers between devices with their start and end apart: 17 -> 17, of which waited for: 11 -> 10; matrix products, arithmetic and copies ran while one was open for 12% -> 7% of each run, Pallas kernels for 0% -> 0%
where the time goes in v3:
time: 100 us
  starting transfers between devices  34 us (34%)
  waiting for transfers between devices  22.4 us (22%)
  other arithmetic  17.3 us (17%)
  Pallas kernels  12 us (12%)
  local copies, waits for them, and re-layouts  8.83 us (9%)
  matrix products  3.14 us (3%)
  between operations  2.44 us (2%)
    ppermute x4, starting transfers between devices, with_halo(): after = lax.ppermute(first, axis, down)  15.5 us
    pallas_call x2, Pallas kernels, conv_back_kernel(): pl.pallas_call(functools.partial(conv_back_body, margin), out_shape=(jax....  12 us
    ppermute x5, waiting for transfers between devices, tree_sum(): value = value + lax.ppermute(value, axes, pairs)  9.07 us
    ppermute x4, waiting for transfers between devices, with_halo(): before = lax.ppermute(last, axis, up)  6.83 us
    ppermute x4, starting transfers between devices, swap_halo(): got = lax.ppermute(sent, axis, [(0, 1), (1, 0)])  6.78 us
    ppermute x4, waiting for transfers between devices, swap_halo(): got = lax.ppermute(sent, axis, [(0, 1), (1, 0)])  6.46 us
    ppermute x4, starting transfers between devices, with_halo(): before = lax.ppermute(last, axis, up)  5.89 us
    ppermute x5, starting transfers between devices, tree_sum(): value = value + lax.ppermute(value, axes, pairs)  5.77 us
  transfers between devices with their start and end apart: 17, of which 10 were waited for; matrix products, arithmetic and copies ran while one was open for 7% of the time, Pallas kernels for 0%

profile of v3, /device:TPU:0, one launch (start us, length us, event | category | flops | bytes accessed | tf_op | source)
XLA Modules:
  0.0 100.1 jit_solution(5057848614885158648)
XLA Ops:
  0.7 1.5 %fusion.59 = (bf16[2,128,1,1,128]{4,3,1,0,2:T(2,128)(2,1)S(1)}, bf16[2,128,1,1,128]{4,3,1,0,2:T(2,128)(2,1)S(1)}) fusion(bf16[2,128,1,16,128]{4,3,1,0,2:T(8,128)(2,1)} %bitcast.169), kind=kLoop, calls=%fused_computation.166 | loop fusion | bytes 262144 | tf_op jit(solution)/shard_map/slice | solution.py:162
  2.2 3.0 %collective-permute-start = (bf16[2,128,1,128]{3,1,0,2:T(8,128)(2,1)S(1)}, bf16[2,128,1,128]{3,1,0,2:T(8,128)(2,1)S(1)}, u32[]{:S(2)}, u32[]{:S(2)}) collective-permute-start(bf16[2,128,1,128]{3,1,0,2:T(8,128)(2,1)S(1)} %bitcast.181), channel_id=1, source_target_pairs={{0,4},{4,8},{8,12},{12,16},{16,20},{20,24},{24,28},{28,0},{1,5},{5... | collective-permute-start | bytes 196616 | tf_op jit(solution)/shard_map/ppermute | solution.py:139
  5.2 3.1 %collective-permute-start.1 = (bf16[2,128,1,128]{3,1,0,2:T(8,128)(2,1)S(1)}, bf16[2,128,1,128]{3,1,0,2:T(8,128)(2,1)S(1)}, u32[]{:S(2)}, u32[]{:S(2)}) collective-permute-start(bf16[2,128,1,128]{3,1,0,2:T(8,128)(2,1)S(1)} %bitcast.180), channel_id=1, source_target_pairs={{4,0},{8,4},{12,8},{16,12},{20,16},{24,20},{28,24},{0,28},{5,1},{9... | collective-permute-start | bytes 196616 | tf_op jit(solution)/shard_map/ppermute | solution.py:140
  8.3 1.3 %fusion.60 = (s32[1,1]{1,0:T(1,128)}, s32[1,1]{1,0:T(1,128)}) fusion(s32[2,8]{1,0:T(2,128)} %param.13, s32[]{:T(128)S(6)} %clamp.1, s32[]{:T(128)} %bitcast.2, s32[]{:T(128)} %bitcast.7), kind=kLoop, calls=%fused_computation.167 | loop fusion | bytes 28 | tf_op jit(solution)/shard_map/jit(_take)/gather | solution.py:152
  11.5 1.0 fusion.54
  12.5 1.7 %collective-permute-start.2 = (bf16[2,1,1,18,128]{4,3,1,0,2:T(8,128)(2,1)S(1)}, bf16[2,1,1,18,128]{4,3,1,0,2:T(8,128)(2,1)S(1)}, u32[]{:S(2)}, u32[]{:S(2)}) collective-permute-start(bf16[2,1,1,18,128]{4,3,1,0,2:T(8,128)(2,1)S(1)} %slice_select_fusion.1), channel_id=1, source_target_pairs={{0,2},{2,0},{1,3},{3,1},{4,6},{6,4},{5,7},{7,5},{8,10},{10,8},{9,1... | collective-permute-start | bytes 27656 | tf_op jit(solution)/shard_map/ppermute | solution.py:122
  14.2 2.0 %collective-permute-done.2 = bf16[2,1,1,18,128]{4,3,1,0,2:T(8,128)(2,1)S(1)} collective-permute-done((bf16[2,1,1,18,128]{4,3,1,0,2:T(8,128)(2,1)S(1)}, bf16[2,1,1,18,128]{4,3,1,0,2:T(8,128)(2,1)S(1)}, u32[]{:S(2)}, u32[]{:S(2)}) %collective-permute-start.2) | collective-permute-done | bytes 9248 | tf_op jit(solution)/shard_map/ppermute | solution.py:122
  16.2 0.9 maximum_convert_fusion.2
  17.1 3.6 %multiply_convert_fusion.1 = (bf16[2,128,16,128]{3,2,1,0:T(8,128)(2,1)S(1)}, f32[2,128,16,128]{3,2,1,0:T(8,128)}) fusion(f32[128]{0:T(128)S(1)} %get-tuple-element.113, f32[2,130,1,18,128]{4,3,1,0,2:T(8,128)S(1)} %maximum_convert_fusion.2, f32[128]{0:T(128)S(1)} %get-tuple-element.106, f32[128]{0:T(128)S(1)} %get-tuple-element.107, ...), kind=kLoop, calls=%fused_computation.57 | loop fusion | flops 11534336 | bytes 22024704 | tf_op jit(solution)/shard_map/convert_element_type | solution.py:282
  20.7 0.4 fusion.28
  21.4 0.8 collective-permute-start.3
  22.1 4.3 %collective-permute-start.4 = (bf16[2,128,2,128]{3,2,0,1:T(2,128)(2,1)S(1)}, bf16[2,128,2,128]{3,2,0,1:T(2,128)(2,1)S(1)}, u32[]{:S(2)}, u32[]{:S(2)}) collective-permute-start(bf16[2,128,2,128]{3,2,0,1:T(2,128)(2,1)S(1)} %get-tuple-element.73), channel_id=1, source_target_pairs={{4,0},{8,4},{12,8},{16,12},{20,16},{24,20},{28,24},{0,28},{5,1},{9... | collective-permute-start | bytes 393224 | tf_op jit(solution)/shard_map/ppermute | solution.py:140
  26.4 2.8 %collective-permute-done.3 = bf16[2,128,2,128]{3,2,0,1:T(2,128)(2,1)S(1)} collective-permute-done((bf16[2,128,2,128]{3,2,0,1:T(2,128)(2,1)S(1)}, bf16[2,128,2,128]{3,2,0,1:T(2,128)(2,1)S(1)}, u32[]{:S(2)}, u32[]{:S(2)}) %collective-permute-start.3) | collective-permute-done | bytes 131104 | tf_op jit(solution)/shard_map/ppermute | solution.py:139
  29.5 1.0 fusion.53
  30.5 1.7 %collective-permute-start.5 = (bf16[2,2,1,20,128]{4,3,0,1,2:T(8,128)(2,1)S(1)}, bf16[2,2,1,20,128]{4,3,0,1,2:T(8,128)(2,1)S(1)}, u32[]{:S(2)}, u32[]{:S(2)}) collective-permute-start(bf16[2,2,1,20,128]{4,3,0,1,2:T(8,128)(2,1)S(1)} %slice_select_fusion), channel_id=1, source_target_pairs={{0,2},{2,0},{1,3},{3,1},{4,6},{6,4},{5,7},{7,5},{8,10},{10,8},{9,1... | collective-permute-start | bytes 61448 | tf_op jit(solution)/shard_map/ppermute | solution.py:122
  32.2 2.0 %maximum_convert_fusion.3.wide_ref = f32[2,130,18,128]{3,2,1,0:T(8,128)} fusion(bf16[2,1,18,128]{3,2,1,0:T(8,128)(2,1)S(1)} %bitcast.179, bf16[2,128,18,128]{3,2,1,0:T(8,128)(2,1)S(1)} %get-tuple-element.70, bf16[2,1,18,128]{3,2,1,0:T(8,128)(2,1)S(1)} %bitcast.178), kind=kLoop, calls=%fused_computation.62 | loop fusion | flops 1797120 | bytes 3594240 | tf_op jit(solution)/shard_map/convert_element_type | solution.py:280
  34.4 0.9 maximum_convert_fusion.1
  35.2 2.5 %multiply_convert_fusion = (bf16[2,128,16,128]{3,2,0,1:T(8,128)(2,1)S(1)}, f32[2,128,16,128]{3,2,0,1:T(8,128)S(1)}) fusion(f32[128]{0:T(128)S(1)} %get-tuple-element.104, f32[2,132,1,20,128]{4,3,0,1,2:T(8,128)S(1)} %maximum_convert_fusion.1, f32[128]{0:T(128)S(1)} %get-tuple-element.97, f32[128]{0:T(128)S(1)} %get-tuple-element.98, ...), kind=kLoop, calls=%fused_computation.52 | loop fusion | flops 11534336 | bytes 22024704 | tf_op jit(solution)/shard_map/convert_element_type | solution.py:286
  37.7 0.9 add_multiply_fusion.1
  38.8 0.4 maximum_convert_fusion
  39.2 1.9 %copy.122.wide_ref = f32[2,132,20,128]{3,2,1,0:T(8,128)} copy(f32[2,132,20,128]{3,2,0,1:T(8,128)S(1)} %maximum_convert_fusion) | data formatting | bytes 5406720 | tf_op jit(solution)/shard_map/convert_element_type | solution.py:284
  41.0 6.0 %shard_map.110 = (f32[2,132,20,128]{3,2,1,0:T(8,128)S(1)}, f32[9,128]{1,0:T(8,128)S(1)}) custom-call(f32[2,132,20,128]{3,2,1,0:T(8,128)} %copy.122.wide_ref, f32[2,128,16,128]{3,2,1,0:T(8,128)S(1)} %copy.123.grad_ref, f32[9,128]{1,0:T(8,128)S(1)} %copy-done.1), custom_call_target="tpu_custom_call" | custom-call | flops 24330240 | bytes 8110080 | tf_op jit(solution)/shard_map/pallas_call | solution.py:78
  47.3 1.7 %collective-permute-start.6 = (bf16[2,2,1,20,128]{4,3,0,1,2:T(8,128)(2,1)S(1)}, bf16[2,2,1,20,128]{4,3,0,1,2:T(8,128)(2,1)S(1)}, u32[]{:S(2)}, u32[]{:S(2)}) collective-permute-start(bf16[2,2,1,20,128]{4,3,0,1,2:T(8,128)(2,1)S(1)} %get-tuple-element.61), channel_id=1, source_target_pairs={{0,2},{2,0},{1,3},{3,1},{4,6},{6,4},{5,7},{7,5},{8,10},{10,8},{9,1... | collective-permute-start | bytes 61448 | tf_op jit(solution)/shard_map/ppermute | solution.py:122
  49.0 2.2 %collective-permute-done.6 = bf16[2,2,1,20,128]{4,3,0,1,2:T(8,128)(2,1)S(1)} collective-permute-done((bf16[2,2,1,20,128]{4,3,0,1,2:T(8,128)(2,1)S(1)}, bf16[2,2,1,20,128]{4,3,0,1,2:T(8,128)(2,1)S(1)}, u32[]{:S(2)}, u32[]{:S(2)}) %collective-permute-start.6) | collective-permute-done | bytes 20512 | tf_op jit(solution)/shard_map/ppermute | solution.py:122
  52.0 5.0 %collective-permute-start.8 = (bf16[2,128,2,128]{3,2,0,1:T(2,128)(2,1)S(1)}, bf16[2,128,2,128]{3,2,0,1:T(2,128)(2,1)S(1)}, u32[]{:S(2)}, u32[]{:S(2)}) collective-permute-start(bf16[2,128,2,128]{3,2,0,1:T(2,128)(2,1)S(1)} %fusion.40), channel_id=1, source_target_pairs={{4,0},{8,4},{12,8},{16,12},{20,16},{24,20},{28,24},{0,28},{5,1},{9... | collective-permute-start | bytes 393224 | tf_op jit(solution)/shard_map/ppermute | solution.py:140
  57.0 0.5 convolution_bitcast_fusion
  57.5 2.0 %collective-permute-done.7 = bf16[2,128,2,128]{3,2,0,1:T(2,128)(2,1)S(1)} collective-permute-done((bf16[2,128,2,128]{3,2,0,1:T(2,128)(2,1)S(1)}, bf16[2,128,2,128]{3,2,0,1:T(2,128)(2,1)S(1)}, u32[]{:S(2)}, u32[]{:S(2)}) %collective-permute-start.7) | collective-permute-done | bytes 131104 | tf_op jit(solution)/shard_map/ppermute | solution.py:139
  59.5 1.0 convert_bitcast_fusion
  60.5 0.5 fusion.9
  61.1 0.5 convolution_bitcast_fusion.1
  61.5 1.1 %copy-done.4 = f32[2,128,16,128]{3,2,1,0:T(8,128)S(1)} copy-done((f32[2,128,16,128]{3,2,1,0:T(8,128)S(1)}, f32[2,128,16,128]{3,2,1,0:T(8,128)}, u32[]{:S(2)}) %copy-start.4) | copy-done | bytes 2097176
  62.6 0.9 add_multiply_fusion.grad_ref
  63.5 6.0 %shard_map.111 = (f32[2,130,18,128]{3,2,1,0:T(8,128)S(1)}, f32[9,128]{1,0:T(8,128)S(1)}) custom-call(f32[2,130,18,128]{3,2,1,0:T(8,128)} %maximum_convert_fusion.3.wide_ref, f32[2,128,16,128]{3,2,1,0:T(8,128)S(1)} %add_multiply_fusion.grad_ref, f32[9,128]{1,0:T(8,128)S(1)} %copy-done.2), custom_call_target="tpu_custom_call" | custom-call | flops 21565440 | bytes 7188480 | tf_op jit(solution)/shard_map/pallas_call | solution.py:78
  69.9 1.7 %collective-permute-start.9 = (bf16[2,1,1,18,128]{4,3,1,0,2:T(8,128)(2,1)S(1)}, bf16[2,1,1,18,128]{4,3,1,0,2:T(8,128)(2,1)S(1)}, u32[]{:S(2)}, u32[]{:S(2)}) collective-permute-start(bf16[2,1,1,18,128]{4,3,1,0,2:T(8,128)(2,1)S(1)} %bitcast_select_fusion), channel_id=1, source_target_pairs={{0,2},{2,0},{1,3},{3,1},{4,6},{6,4},{5,7},{7,5},{8,10},{10,8},{9,1... | collective-permute-start | bytes 27656 | tf_op jit(solution)/shard_map/ppermute | solution.py:122
  71.6 2.0 %collective-permute-done.9 = bf16[2,1,1,18,128]{4,3,1,0,2:T(8,128)(2,1)S(1)} collective-permute-done((bf16[2,1,1,18,128]{4,3,1,0,2:T(8,128)(2,1)S(1)}, bf16[2,1,1,18,128]{4,3,1,0,2:T(8,128)(2,1)S(1)}, u32[]{:S(2)}, u32[]{:S(2)}) %collective-permute-start.9) | collective-permute-done | bytes 9248 | tf_op jit(solution)/shard_map/ppermute | solution.py:122
  73.9 1.7 %collective-permute-start.13 = (f32[274,128]{1,0:T(8,128)S(1)}, f32[274,128]{1,0:T(8,128)S(1)}, u32[]{:S(2)}, u32[]{:S(2)}) collective-permute-start(f32[274,128]{1,0:T(8,128)S(1)} %fusion.63), channel_id=1, source_target_pairs={{0,2},{1,3},{2,0},{3,1},{4,6},{5,7},{6,4},{7,5},{8,10},{9,11},{10,... | collective-permute-start | bytes 420872 | tf_op jit(solution)/shard_map/ppermute | solution.py:102
  75.8 3.3 %collective-permute-done.13 = f32[274,128]{1,0:T(8,128)S(1)} collective-permute-done((f32[274,128]{1,0:T(8,128)S(1)}, f32[274,128]{1,0:T(8,128)S(1)}, u32[]{:S(2)}, u32[]{:S(2)}) %collective-permute-start.13) | collective-permute-done | bytes 140320 | tf_op jit(solution)/shard_map/ppermute | solution.py:102
  79.2 0.4 fusion.38
  79.7 2.1 %collective-permute-start.10 = (bf16[2,128,1,128]{3,0,1,2:T(2,128)(2,1)S(1)}, bf16[2,128,1,128]{3,0,1,2:T(2,128)(2,1)S(1)}, u32[]{:S(2)}, u32[]{:S(2)}) collective-permute-start(bf16[2,128,1,128]{3,0,1,2:T(2,128)(2,1)S(1)} %copy.135), channel_id=1, source_target_pairs={{0,4},{4,8},{8,12},{12,16},{16,20},{20,24},{24,28},{28,0},{1,5},{5... | collective-permute-start | bytes 196616 | tf_op jit(solution)/shard_map/ppermute | solution.py:139
  81.9 3.2 %collective-permute-start.11 = (bf16[2,128,1,128]{3,0,1,2:T(2,128)(2,1)S(1)}, bf16[2,128,1,128]{3,0,1,2:T(2,128)(2,1)S(1)}, u32[]{:S(2)}, u32[]{:S(2)}) collective-permute-start(bf16[2,128,1,128]{3,0,1,2:T(2,128)(2,1)S(1)} %copy.138), channel_id=1, source_target_pairs={{4,0},{8,4},{12,8},{16,12},{20,16},{24,20},{28,24},{0,28},{5,1},{9... | collective-permute-start | bytes 196616 | tf_op jit(solution)/shard_map/ppermute | solution.py:140
  85.2 2.0 %collective-permute-done.10 = bf16[2,128,1,128]{3,0,1,2:T(2,128)(2,1)S(1)} collective-permute-done((bf16[2,128,1,128]{3,0,1,2:T(2,128)(2,1)S(1)}, bf16[2,128,1,128]{3,0,1,2:T(2,128)(2,1)S(1)}, u32[]{:S(2)}, u32[]{:S(2)}) %collective-permute-start.10) | collective-permute-done | bytes 65568 | tf_op jit(solution)/shard_map/ppermute | solution.py:139
  87.3 2.9 %collective-permute-done.15 = f32[274,128]{1,0:T(8,128)S(1)} collective-permute-done((f32[274,128]{1,0:T(8,128)S(1)}, f32[274,128]{1,0:T(8,128)S(1)}, u32[]{:S(2)}, u32[]{:S(2)}) %collective-permute-start.15) | collective-permute-done | bytes 140320 | tf_op jit(solution)/shard_map/ppermute | solution.py:102
  90.3 3.9 %collective-permute-start.16 = (f32[274,128]{1,0:T(8,128)S(1)}, f32[274,128]{1,0:T(8,128)S(1)}, u32[]{:S(2)}, u32[]{:S(2)}) collective-permute-start(f32[274,128]{1,0:T(8,128)S(1)} %add.192), channel_id=1, source_target_pairs={{0,16},{1,17},{2,18},{3,19},{4,20},{5,21},{6,22},{7,23},{8,24},{9,... | collective-permute-start | bytes 420872 | tf_op jit(solution)/shard_map/ppermute | solution.py:102
  94.1 0.6 fusion.5
  94.8 1.2 %copy.143 = bf16[2,128,16,128]{3,2,1,0:T(8,128)(2,1)} copy(bf16[2,128,16,128]{3,2,0,1:T(8,128)(2,1)S(1)} %fusion.5) | data formatting | bytes 2097152
  95.9 2.8 %collective-permute-done.16 = f32[274,128]{1,0:T(8,128)S(1)} collective-permute-done((f32[274,128]{1,0:T(8,128)S(1)}, f32[274,128]{1,0:T(8,128)S(1)}, u32[]{:S(2)}, u32[]{:S(2)}) %collective-permute-start.16) | collective-permute-done | bytes 140320 | tf_op jit(solution)/shard_map/ppermute | solution.py:102
  98.8 0.7 slice_multiply_fusion.18
  99.4 0.6 slice_multiply_fusion.20
  (71 shorter events, 3.7 us)
Async XLA Ops:
  0.6 20.1 %copy-start = (bf16[128,128]{1,0:T(8,128)(2,1)S(1)}, bf16[128,128]{1,0:T(8,128)(2,1)}, u32[]{:S(2)}) copy-start(bf16[128,128]{1,0:T(8,128)(2,1)} %param.10) | copy-start | bytes 98308
  0.6 10.8 %copy-start.3 = (bf16[2,128,16,128]{3,2,1,0:T(8,128)(2,1)S(1)}, bf16[2,128,16,128]{3,2,1,0:T(8,128)(2,1)}, u32[]{:S(2)}) copy-start(bf16[2,128,16,128]{3,2,1,0:T(8,128)(2,1)} %param.7) | copy-start | bytes 3145732
  2.2 8.8 %collective-permute-start = (bf16[2,128,1,128]{3,1,0,2:T(8,128)(2,1)S(1)}, bf16[2,128,1,128]{3,1,0,2:T(8,128)(2,1)S(1)}, u32[]{:S(2)}, u32[]{:S(2)}) collective-permute-start(bf16[2,128,1,128]{3,1,0,2:T(8,128)(2,1)S(1)} %bitcast.181), channel_id=1, source_target_pairs={{0,4},{4,8},{8,12},{12,16},{16,20},{20,24},{24,28},{28,0},{1,5},{5... | collective-permute-start | bytes 196616 | tf_op jit(solution)/shard_map/ppermute | solution.py:139
  5.2 6.0 %collective-permute-start.1 = (bf16[2,128,1,128]{3,1,0,2:T(8,128)(2,1)S(1)}, bf16[2,128,1,128]{3,1,0,2:T(8,128)(2,1)S(1)}, u32[]{:S(2)}, u32[]{:S(2)}) collective-permute-start(bf16[2,128,1,128]{3,1,0,2:T(8,128)(2,1)S(1)} %bitcast.180), channel_id=1, source_target_pairs={{4,0},{8,4},{12,8},{16,12},{20,16},{24,20},{28,24},{0,28},{5,1},{9... | collective-permute-start | bytes 196616 | tf_op jit(solution)/shard_map/ppermute | solution.py:140
  11.5 2.7 %copy-start.2 = (f32[9,128]{1,0:T(8,128)S(1)}, f32[9,128]{1,0:T(8,128)}, u32[]{:S(2)}) copy-start(f32[9,128]{1,0:T(8,128)} %k_ref.3) | copy-start | bytes 13828
  12.5 3.8 %collective-permute-start.2 = (bf16[2,1,1,18,128]{4,3,1,0,2:T(8,128)(2,1)S(1)}, bf16[2,1,1,18,128]{4,3,1,0,2:T(8,128)(2,1)S(1)}, u32[]{:S(2)}, u32[]{:S(2)}) collective-permute-start(bf16[2,1,1,18,128]{4,3,1,0,2:T(8,128)(2,1)S(1)} %slice_select_fusion.1), channel_id=1, source_target_pairs={{0,2},{2,0},{1,3},{3,1},{4,6},{6,4},{5,7},{7,5},{8,10},{10,8},{9,1... | collective-permute-start | bytes 27656 | tf_op jit(solution)/shard_map/ppermute | solution.py:122
  20.7 1.4 %copy-start.1 = (f32[9,128]{1,0:T(8,128)S(1)}, f32[9,128]{1,0:T(8,128)}, u32[]{:S(2)}) copy-start(f32[9,128]{1,0:T(8,128)} %k_ref.2) | copy-start | bytes 13828
  21.4 7.8 %collective-permute-start.3 = (bf16[2,128,2,128]{3,2,0,1:T(2,128)(2,1)S(1)}, bf16[2,128,2,128]{3,2,0,1:T(2,128)(2,1)S(1)}, u32[]{:S(2)}, u32[]{:S(2)}) collective-permute-start(bf16[2,128,2,128]{3,2,0,1:T(2,128)(2,1)S(1)} %get-tuple-element.72), channel_id=1, source_target_pairs={{0,4},{4,8},{8,12},{12,16},{16,20},{20,24},{24,28},{28,0},{1,5},{5... | collective-permute-start | bytes 393224 | tf_op jit(solution)/shard_map/ppermute | solution.py:139
  22.1 7.2 %collective-permute-start.4 = (bf16[2,128,2,128]{3,2,0,1:T(2,128)(2,1)S(1)}, bf16[2,128,2,128]{3,2,0,1:T(2,128)(2,1)S(1)}, u32[]{:S(2)}, u32[]{:S(2)}) collective-permute-start(bf16[2,128,2,128]{3,2,0,1:T(2,128)(2,1)S(1)} %get-tuple-element.73), channel_id=1, source_target_pairs={{4,0},{8,4},{12,8},{16,12},{20,16},{24,20},{28,24},{0,28},{5,1},{9... | collective-permute-start | bytes 393224 | tf_op jit(solution)/shard_map/ppermute | solution.py:140
  30.5 3.9 %collective-permute-start.5 = (bf16[2,2,1,20,128]{4,3,0,1,2:T(8,128)(2,1)S(1)}, bf16[2,2,1,20,128]{4,3,0,1,2:T(8,128)(2,1)S(1)}, u32[]{:S(2)}, u32[]{:S(2)}) collective-permute-start(bf16[2,2,1,20,128]{4,3,0,1,2:T(8,128)(2,1)S(1)} %slice_select_fusion), channel_id=1, source_target_pairs={{0,2},{2,0},{1,3},{3,1},{4,6},{6,4},{5,7},{7,5},{8,10},{10,8},{9,1... | collective-permute-start | bytes 61448 | tf_op jit(solution)/shard_map/ppermute | solution.py:122
  35.2 2.5 %copy-start.5 = (bf16[2,128,16,128]{3,2,1,0:T(8,128)(2,1)S(1)}, bf16[2,128,16,128]{3,2,1,0:T(8,128)(2,1)}, u32[]{:S(2)}) copy-start(bf16[2,128,16,128]{3,2,1,0:T(8,128)(2,1)} %param.8) | copy-start | bytes 3145732
  35.2 2.5 %copy-start.6 = (bf16[128,128]{1,0:T(8,128)(2,1)S(1)}, bf16[128,128]{1,0:T(8,128)(2,1)}, u32[]{:S(2)}) copy-start(bf16[128,128]{1,0:T(8,128)(2,1)} %param.12) | copy-start | bytes 98308
  47.3 3.9 %collective-permute-start.6 = (bf16[2,2,1,20,128]{4,3,0,1,2:T(8,128)(2,1)S(1)}, bf16[2,2,1,20,128]{4,3,0,1,2:T(8,128)(2,1)S(1)}, u32[]{:S(2)}, u32[]{:S(2)}) collective-permute-start(bf16[2,2,1,20,128]{4,3,0,1,2:T(8,128)(2,1)S(1)} %get-tuple-element.61), channel_id=1, source_target_pairs={{0,2},{2,0},{1,3},{3,1},{4,6},{6,4},{5,7},{7,5},{8,10},{10,8},{9,1... | collective-permute-start | bytes 61448 | tf_op jit(solution)/shard_map/ppermute | solution.py:122
  51.8 7.7 %collective-permute-start.7 = (bf16[2,128,2,128]{3,2,0,1:T(2,128)(2,1)S(1)}, bf16[2,128,2,128]{3,2,0,1:T(2,128)(2,1)S(1)}, u32[]{:S(2)}, u32[]{:S(2)}) collective-permute-start(bf16[2,128,2,128]{3,2,0,1:T(2,128)(2,1)S(1)} %fusion.41), channel_id=1, source_target_pairs={{0,4},{4,8},{8,12},{12,16},{16,20},{20,24},{24,28},{28,0},{1,5},{5... | collective-permute-start | bytes 393224 | tf_op jit(solution)/shard_map/ppermute | solution.py:139
  52.0 7.5 %collective-permute-start.8 = (bf16[2,128,2,128]{3,2,0,1:T(2,128)(2,1)S(1)}, bf16[2,128,2,128]{3,2,0,1:T(2,128)(2,1)S(1)}, u32[]{:S(2)}, u32[]{:S(2)}) collective-permute-start(bf16[2,128,2,128]{3,2,0,1:T(2,128)(2,1)S(1)} %fusion.40), channel_id=1, source_target_pairs={{4,0},{8,4},{12,8},{16,12},{20,16},{24,20},{28,24},{0,28},{5,1},{9... | collective-permute-start | bytes 393224 | tf_op jit(solution)/shard_map/ppermute | solution.py:140
  61.0 1.6 %copy-start.4 = (f32[2,128,16,128]{3,2,1,0:T(8,128)S(1)}, f32[2,128,16,128]{3,2,1,0:T(8,128)}, u32[]{:S(2)}) copy-start(f32[2,128,16,128]{3,2,1,0:T(8,128)} %get-tuple-element.58) | copy-start | bytes 6291460
  69.8 4.1 %collective-permute-start.12 = (f32[274,128]{1,0:T(8,128)S(1)}, f32[274,128]{1,0:T(8,128)S(1)}, u32[]{:S(2)}, u32[]{:S(2)}) collective-permute-start(f32[274,128]{1,0:T(8,128)S(1)} %pad_maximum_fusion.2), channel_id=1, source_target_pairs={{0,1},{1,0},{2,3},{3,2},{4,5},{5,4},{6,7},{7,6},{8,9},{9,8},{10,11... | collective-permute-start | bytes 420872 | tf_op jit(solution)/shard_map/ppermute | solution.py:102
  69.9 3.8 %collective-permute-start.9 = (bf16[2,1,1,18,128]{4,3,1,0,2:T(8,128)(2,1)S(1)}, bf16[2,1,1,18,128]{4,3,1,0,2:T(8,128)(2,1)S(1)}, u32[]{:S(2)}, u32[]{:S(2)}) collective-permute-start(bf16[2,1,1,18,128]{4,3,1,0,2:T(8,128)(2,1)S(1)} %bitcast_select_fusion), channel_id=1, source_target_pairs={{0,2},{2,0},{1,3},{3,1},{4,6},{6,4},{5,7},{7,5},{8,10},{10,8},{9,1... | collective-permute-start | bytes 27656 | tf_op jit(solution)/shard_map/ppermute | solution.py:122
  73.9 5.2 %collective-permute-start.13 = (f32[274,128]{1,0:T(8,128)S(1)}, f32[274,128]{1,0:T(8,128)S(1)}, u32[]{:S(2)}, u32[]{:S(2)}) collective-permute-start(f32[274,128]{1,0:T(8,128)S(1)} %fusion.63), channel_id=1, source_target_pairs={{0,2},{1,3},{2,0},{3,1},{4,6},{5,7},{6,4},{7,5},{8,10},{9,11},{10,... | collective-permute-start | bytes 420872 | tf_op jit(solution)/shard_map/ppermute | solution.py:102
  79.1 6.0 %collective-permute-start.14 = (f32[274,128]{1,0:T(8,128)S(1)}, f32[274,128]{1,0:T(8,128)S(1)}, u32[]{:S(2)}, u32[]{:S(2)}) collective-permute-start(f32[274,128]{1,0:T(8,128)S(1)} %add.190), channel_id=1, source_target_pairs={{0,4},{1,5},{2,6},{3,7},{4,0},{5,1},{6,2},{7,3},{8,12},{9,13},{10,... | collective-permute-start | bytes 420872 | tf_op jit(solution)/shard_map/ppermute | solution.py:102
  79.7 7.4 %collective-permute-start.10 = (bf16[2,128,1,128]{3,0,1,2:T(2,128)(2,1)S(1)}, bf16[2,128,1,128]{3,0,1,2:T(2,128)(2,1)S(1)}, u32[]{:S(2)}, u32[]{:S(2)}) collective-permute-start(bf16[2,128,1,128]{3,0,1,2:T(2,128)(2,1)S(1)} %copy.135), channel_id=1, source_target_pairs={{0,4},{4,8},{8,12},{12,16},{16,20},{20,24},{24,28},{28,0},{1,5},{5... | collective-permute-start | bytes 196616 | tf_op jit(solution)/shard_map/ppermute | solution.py:139
  81.9 5.3 %collective-permute-start.11 = (bf16[2,128,1,128]{3,0,1,2:T(2,128)(2,1)S(1)}, bf16[2,128,1,128]{3,0,1,2:T(2,128)(2,1)S(1)}, u32[]{:S(2)}, u32[]{:S(2)}) collective-permute-start(bf16[2,128,1,128]{3,0,1,2:T(2,128)(2,1)S(1)} %copy.138), channel_id=1, source_target_pairs={{4,0},{8,4},{12,8},{16,12},{20,16},{24,20},{28,24},{0,28},{5,1},{9... | collective-permute-start | bytes 196616 | tf_op jit(solution)/shard_map/ppermute | solution.py:140
  85.1 5.2 %collective-permute-start.15 = (f32[274,128]{1,0:T(8,128)S(1)}, f32[274,128]{1,0:T(8,128)S(1)}, u32[]{:S(2)}, u32[]{:S(2)}) collective-permute-start(f32[274,128]{1,0:T(8,128)S(1)} %add.191), channel_id=1, source_target_pairs={{0,8},{1,9},{2,10},{3,11},{4,12},{5,13},{6,14},{7,15},{8,0},{9,1},... | collective-permute-start | bytes 420872 | tf_op jit(solution)/shard_map/ppermute | solution.py:102
  90.3 8.5 %collective-permute-start.16 = (f32[274,128]{1,0:T(8,128)S(1)}, f32[274,128]{1,0:T(8,128)S(1)}, u32[]{:S(2)}, u32[]{:S(2)}) collective-permute-start(f32[274,128]{1,0:T(8,128)S(1)} %add.192), channel_id=1, source_target_pairs={{0,16},{1,17},{2,18},{3,19},{4,20},{5,21},{6,22},{7,23},{8,24},{9,... | collective-permute-start | bytes 420872 | tf_op jit(solution)/shard_map/ppermute | solution.py:102

commit v4 on v3

--- a/solution.py
+++ b/solution.py
@@ -10,13 +10,34 @@
 ROW_BLOCK = 8
 
 
-def conv_back_body(margin, wide_ref, grad_ref, k_ref, gw_ref, dk_ref, gpad_ref):
+def tap_sum_body(margin, wide_ref, grad_ref, dk_ref):
     batch, wide_rows, wide_cols, channels = wide_ref.shape
     row_count = wide_rows - 2 * margin
     col_count = wide_cols - 2 * margin
-    taps = [(a, b) for a in range(3) for b in range(3)]
+    span = ROW_BLOCK + 2 * margin
+    sums = [jnp.zeros((col_count, channels), jnp.float32) for _ in range(9)]
+    for item in range(batch):
+
+        def tap_step(step, sums):
+            r0 = pl.multiple_of(step * ROW_BLOCK, ROW_BLOCK)
+            grad = grad_ref[item, pl.ds(r0, ROW_BLOCK)]
+            out = list(sums)
+            for b in range(3):
+                slab = wide_ref[item, pl.ds(r0, span), pl.ds(b * margin, col_count), :]
+                for a in range(3):
+                    seen = slab[a * margin : a * margin + ROW_BLOCK]
+                    out[3 * a + b] = out[3 * a + b] + jnp.sum(seen * grad, axis=0)
+            return out
+
+        sums = lax.fori_loop(0, row_count // ROW_BLOCK, tap_step, sums)
+    dk_ref[...] = jnp.concatenate([jnp.sum(s, axis=0, keepdims=True) for s in sums], axis=0)
+
+
+def wide_grad_body(margin, grad_ref, k_ref, gw_ref, gpad_ref):
+    batch, wide_rows, wide_cols, channels = gw_ref.shape
+    row_count = wide_rows - 2 * margin
+    col_count = wide_cols - 2 * margin
     kern = k_ref[...]
-    sums = [jnp.zeros((col_count, channels), jnp.float32) for _ in taps]
     for item in range(batch):
         gpad_ref[...] = jnp.zeros(gpad_ref.shape, jnp.float32)
 
@@ -29,45 +50,23 @@
 
         lax.fori_loop(0, row_count // ROW_BLOCK, fill_step, 0)
 
-        def tap_step(step, sums):
-            r0 = pl.multiple_of(step * ROW_BLOCK, ROW_BLOCK)
-            grad = grad_ref[item, pl.ds(r0, ROW_BLOCK)]
-            out = []
-            for t, (a, b) in enumerate(taps):
-                seen = wide_ref[item, pl.ds(r0 + a * margin, ROW_BLOCK), pl.ds(b * margin, col_count), :]
-                out.append(sums[t] + jnp.sum(seen * grad, axis=0))
-            return out
-
-        sums = lax.fori_loop(0, row_count // ROW_BLOCK, tap_step, sums)
+        def wide_rows_at(r0, count):
+            total = jnp.zeros((count, wide_cols, channels), jnp.float32)
+            for b in range(3):
+                slab = gpad_ref[pl.ds(r0, count + 2 * margin), pl.ds(2 * margin - b * margin, wide_cols), :]
+                for a in range(3):
+                    part = slab[2 * margin - a * margin : 2 * margin - a * margin + count]
+                    total = total + part * kern[3 * a + b][None, None, :]
+            gw_ref[item, pl.ds(r0, count), :, :] = total
 
         def wide_step(step, carry):
-            r0 = step * ROW_BLOCK
-            total = jnp.zeros((ROW_BLOCK, wide_cols, channels), jnp.float32)
-            for t, (a, b) in enumerate(taps):
-                part = gpad_ref[
-                    pl.ds(r0 + 2 * margin - a * margin, ROW_BLOCK),
-                    pl.ds(2 * margin - b * margin, wide_cols),
-                    :,
-                ]
-                total = total + part * kern[t][None, None, :]
-            gw_ref[item, pl.ds(r0, ROW_BLOCK), :, :] = total
+            wide_rows_at(pl.multiple_of(step * ROW_BLOCK, ROW_BLOCK), ROW_BLOCK)
             return carry
 
         full = wide_rows // ROW_BLOCK
         lax.fori_loop(0, full, wide_step, 0)
-        rest = wide_rows - full * ROW_BLOCK
-        if rest:
-            r0 = full * ROW_BLOCK
-            total = jnp.zeros((rest, wide_cols, channels), jnp.float32)
-            for t, (a, b) in enumerate(taps):
-                part = gpad_ref[
-                    pl.ds(r0 + 2 * margin - a * margin, rest),
-                    pl.ds(2 * margin - b * margin, wide_cols),
-                    :,
-                ]
-                total = total + part * kern[t][None, None, :]
-            gw_ref[item, pl.ds(r0, rest), :, :] = total
-    dk_ref[...] = jnp.concatenate([jnp.sum(s, axis=0, keepdims=True) for s in sums], axis=0)
+        if wide_rows - full * ROW_BLOCK:
+            wide_rows_at(full * ROW_BLOCK, wide_rows - full * ROW_BLOCK)
 
 
 def conv_back_kernel(wide, grad, kernel, margin):
@@ -75,18 +74,26 @@
     elems = batch * wide_rows * wide_cols * channels
     pad_rows = grad.shape[1] + 4 * margin
     pad_cols = -(-(grad.shape[2] + 4 * margin) // 8) * 8
-    return pl.pallas_call(
-        functools.partial(conv_back_body, margin),
-        out_shape=(
-            jax.ShapeDtypeStruct(wide.shape, jnp.float32),
-            jax.ShapeDtypeStruct((9, channels), jnp.float32),
-        ),
-        in_specs=[pl.BlockSpec(memory_space=pltpu.VMEM)] * 3,
-        out_specs=(pl.BlockSpec(memory_space=pltpu.VMEM), pl.BlockSpec(memory_space=pltpu.VMEM)),
+    vmem = pl.BlockSpec(memory_space=pltpu.VMEM)
+    params = pltpu.CompilerParams(vmem_limit_bytes=48 * 1024 * 1024)
+    grad_wide = pl.pallas_call(
+        functools.partial(wide_grad_body, margin),
+        out_shape=jax.ShapeDtypeStruct(wide.shape, jnp.float32),
+        in_specs=[vmem, vmem],
+        out_specs=vmem,
         scratch_shapes=[pltpu.VMEM((pad_rows, pad_cols, channels), jnp.float32)],
-        compiler_params=pltpu.CompilerParams(vmem_limit_bytes=48 * 1024 * 1024),
-        cost_estimate=pl.CostEstimate(flops=36 * elems, bytes_accessed=12 * elems, transcendentals=0),
-    )(wide.astype(jnp.float32), grad, kernel)
+        compiler_params=params,
+        cost_estimate=pl.CostEstimate(flops=18 * elems, bytes_accessed=8 * elems, transcendentals=0),
+    )(grad, kernel)
+    tap_sums = pl.pallas_call(
+        functools.partial(tap_sum_body, margin),
+        out_shape=jax.ShapeDtypeStruct((9, channels), jnp.float32),
+        in_specs=[vmem, vmem],
+        out_specs=vmem,
+        compiler_params=params,
+        cost_estimate=pl.CostEstimate(flops=18 * elems, bytes_accessed=8 * elems, transcendentals=0),
+    )(wide.astype(jnp.float32), grad)
+    return grad_wide, tap_sums
 
 
 def tree_sum(value, axes):

time: 100 us -> 94.6 us (0.946)
  Pallas kernels: 12 us -> 8.13 us
  local copies, waits for them, and re-layouts: 8.83 us -> 7.69 us
    pallas_call x2 -> x4, Pallas kernels: 12 us -> 8.13 us  [the longest x2 4.91 us: conv_back_kernel(): pl.pallas_call(functools.partial(wide_grad_body, margin), out_shape=jax.S...]
    ppermute x4, waiting for transfers between devices: 6.83 us -> 5.07 us  [with_halo(): before = lax.ppermute(last, axis, up)]
    convert_element_type x2, other arithmetic: 2.9 us -> 1.23 us  [shards(): wide_one = extend(fields, 1, seams).astype(jnp.float32)]
    convert_element_type x1, local copies, waits for them, and re-layouts: 1.87 us -> 0.21 us  [shards(): wide_two = extend(hidden, 2, seams).astype(jnp.float32)]
    ppermute x4, waiting for transfers between devices: 6.46 us -> 7.6 us  [swap_halo(): got = lax.ppermute(sent, axis, [(0, 1), (1, 0)])]
    concatenate x2, other arithmetic: 1.95 us -> 3.08 us  [extend(): jnp.concatenate([padded_rows[:, :margin], widened, padded_rows[:, 3 * mar...]
    unnamed x17 -> x25, local copies, waits for them, and re-layouts: 2.31 us -> 2.99 us
  transfers between devices with their start and end apart: 17 -> 17, of which waited for: 10 -> 10; matrix products, arithmetic and copies ran while one was open for 7% -> 6% of each run, Pallas kernels for 0% -> 2%
where the time goes in v4:
time: 94.6 us; the launch traced here: 94.4 us
  starting transfers between devices  34 us (36%)
  waiting for transfers between devices  21.8 us (23%)
  other arithmetic  17.4 us (18%)
  Pallas kernels  8.13 us (9%)
  local copies, waits for them, and re-layouts  7.69 us (8%)
  matrix products  2.95 us (3%)
  between operations  2.47 us (3%)
    ppermute x4, starting transfers between devices, with_halo(): after = lax.ppermute(first, axis, down)  15.6 us
    ppermute x5, waiting for transfers between devices, tree_sum(): value = value + lax.ppermute(value, axes, pairs)  9.09 us
    ppermute x4, waiting for transfers between devices, swap_halo(): got = lax.ppermute(sent, axis, [(0, 1), (1, 0)])  7.6 us
    ppermute x4, starting transfers between devices, swap_halo(): got = lax.ppermute(sent, axis, [(0, 1), (1, 0)])  6.77 us
    ppermute x4, starting transfers between devices, with_halo(): before = lax.ppermute(last, axis, up)  5.9 us
    ppermute x5, starting transfers between devices, tree_sum(): value = value + lax.ppermute(value, axes, pairs)  5.79 us
    ppermute x4, waiting for transfers between devices, with_halo(): before = lax.ppermute(last, axis, up)  5.07 us
    pallas_call x2, Pallas kernels, conv_back_kernel(): pl.pallas_call(functools.partial(wide_grad_body, margin), out_shape=jax.S...  4.91 us
  transfers between devices with their start and end apart: 17, of which 10 were waited for; matrix products, arithmetic and copies ran while one was open for 6% of the time, Pallas kernels for 2%

profile of v4, /device:TPU:0, one launch (start us, length us, event | category | flops | bytes accessed | tf_op | source)
XLA Modules:
  0.0 94.4 jit_solution(9662505117254907653)
XLA Ops:
  0.7 1.5 %fusion.59 = (bf16[2,128,1,1,128]{4,3,1,0,2:T(2,128)(2,1)S(1)}, bf16[2,128,1,1,128]{4,3,1,0,2:T(2,128)(2,1)S(1)}) fusion(bf16[2,128,1,16,128]{4,3,1,0,2:T(8,128)(2,1)} %bitcast.169), kind=kLoop, calls=%fused_computation.169 | loop fusion | bytes 262144 | tf_op jit(solution)/shard_map/slice | solution.py:169
  2.2 3.0 %collective-permute-start = (bf16[2,128,1,128]{3,1,0,2:T(8,128)(2,1)S(1)}, bf16[2,128,1,128]{3,1,0,2:T(8,128)(2,1)S(1)}, u32[]{:S(2)}, u32[]{:S(2)}) collective-permute-start(bf16[2,128,1,128]{3,1,0,2:T(8,128)(2,1)S(1)} %bitcast.181), channel_id=1, source_target_pairs={{0,4},{4,8},{8,12},{12,16},{16,20},{20,24},{24,28},{28,0},{1,5},{5... | collective-permute-start | bytes 196616 | tf_op jit(solution)/shard_map/ppermute | solution.py:146
  5.2 3.1 %collective-permute-start.1 = (bf16[2,128,1,128]{3,1,0,2:T(8,128)(2,1)S(1)}, bf16[2,128,1,128]{3,1,0,2:T(8,128)(2,1)S(1)}, u32[]{:S(2)}, u32[]{:S(2)}) collective-permute-start(bf16[2,128,1,128]{3,1,0,2:T(8,128)(2,1)S(1)} %bitcast.180), channel_id=1, source_target_pairs={{4,0},{8,4},{12,8},{16,12},{20,16},{24,20},{28,24},{0,28},{5,1},{9... | collective-permute-start | bytes 196616 | tf_op jit(solution)/shard_map/ppermute | solution.py:147
  8.3 1.3 %fusion.60 = (s32[1,1]{1,0:T(1,128)}, s32[1,1]{1,0:T(1,128)}) fusion(s32[2,8]{1,0:T(2,128)} %param.13, s32[]{:T(128)S(6)} %clamp.1, s32[]{:T(128)} %bitcast.3, s32[]{:T(128)} %bitcast.8), kind=kLoop, calls=%fused_computation.170 | loop fusion | bytes 28 | tf_op jit(solution)/shard_map/jit(_take)/gather | solution.py:159
  11.5 1.0 %fusion.54 = (bf16[2,128,18,128]{3,2,1,0:T(8,128)(2,1)S(1)}, bf16[2,128,1,18,128]{4,3,1,0,2:T(8,128)(2,1)S(1)}) fusion(bf16[2,128,1,1,128]{4,3,1,0,2:T(2,128)(2,1)S(1)} %copy.114, bf16[2,128,1,16,128]{4,3,1,0,2:T(8,128)(2,1)S(1)} %bitcast.170, bf16[2,128,1,1,128]{4,3,1,0,2:T(2,128)(2,1)S(1)} %copy.113), kind=kLoop, calls=%fused_computation.166 | loop fusion | flops 3538944 | bytes 3538944 | tf_op jit(solution)/shard_map/concatenate | solution.py:183
  12.5 1.7 %collective-permute-start.2 = (bf16[2,1,1,18,128]{4,3,1,0,2:T(8,128)(2,1)S(1)}, bf16[2,1,1,18,128]{4,3,1,0,2:T(8,128)(2,1)S(1)}, u32[]{:S(2)}, u32[]{:S(2)}) collective-permute-start(bf16[2,1,1,18,128]{4,3,1,0,2:T(8,128)(2,1)S(1)} %slice_select_fusion.1), channel_id=1, source_target_pairs={{0,2},{2,0},{1,3},{3,1},{4,6},{6,4},{5,7},{7,5},{8,10},{10,8},{9,1... | collective-permute-start | bytes 27656 | tf_op jit(solution)/shard_map/ppermute | solution.py:129
  14.2 2.0 %collective-permute-done.2 = bf16[2,1,1,18,128]{4,3,1,0,2:T(8,128)(2,1)S(1)} collective-permute-done((bf16[2,1,1,18,128]{4,3,1,0,2:T(8,128)(2,1)S(1)}, bf16[2,1,1,18,128]{4,3,1,0,2:T(8,128)(2,1)S(1)}, u32[]{:S(2)}, u32[]{:S(2)}) %collective-permute-start.2) | collective-permute-done | bytes 9248 | tf_op jit(solution)/shard_map/ppermute | solution.py:129
  16.2 0.9 maximum_convert_fusion.2
  17.1 3.5 %multiply_convert_fusion.1 = (bf16[2,128,16,128]{3,2,1,0:T(8,128)(2,1)S(1)}, f32[2,128,16,128]{3,2,1,0:T(8,128)}) fusion(f32[128]{0:T(128)S(1)} %get-tuple-element.105, f32[2,130,1,18,128]{4,3,1,0,2:T(8,128)S(1)} %maximum_convert_fusion.2, f32[128]{0:T(128)S(1)} %get-tuple-element.98, f32[128]{0:T(128)S(1)} %get-tuple-element.99, ...), kind=kLoop, calls=%fused_computation.59 | loop fusion | flops 11534336 | bytes 22024704 | tf_op jit(solution)/shard_map/convert_element_type | solution.py:289
  20.7 0.4 fusion.28
  21.3 0.8 collective-permute-start.3
  22.1 4.2 %collective-permute-start.4 = (bf16[2,128,2,128]{3,2,0,1:T(2,128)(2,1)S(1)}, bf16[2,128,2,128]{3,2,0,1:T(2,128)(2,1)S(1)}, u32[]{:S(2)}, u32[]{:S(2)}) collective-permute-start(bf16[2,128,2,128]{3,2,0,1:T(2,128)(2,1)S(1)} %get-tuple-element.65), channel_id=1, source_target_pairs={{4,0},{8,4},{12,8},{16,12},{20,16},{24,20},{28,24},{0,28},{5,1},{9... | collective-permute-start | bytes 393224 | tf_op jit(solution)/shard_map/ppermute | solution.py:147
  26.3 2.8 %collective-permute-done.3 = bf16[2,128,2,128]{3,2,0,1:T(2,128)(2,1)S(1)} collective-permute-done((bf16[2,128,2,128]{3,2,0,1:T(2,128)(2,1)S(1)}, bf16[2,128,2,128]{3,2,0,1:T(2,128)(2,1)S(1)}, u32[]{:S(2)}, u32[]{:S(2)}) %collective-permute-start.3) | collective-permute-done | bytes 131104 | tf_op jit(solution)/shard_map/ppermute | solution.py:146
  29.4 2.1 %fusion.53 = (bf16[2,128,20,128]{3,2,0,1:T(8,128)(2,1)}, bf16[2,128,1,20,128]{4,3,0,1,2:T(8,128)(2,1)S(1)}) fusion(bf16[2,128,1,2,128]{4,3,0,1,2:T(2,128)(2,1)S(1)} %fusion.37, bf16[2,128,1,16,128]{4,3,0,1,2:T(8,128)(2,1)S(1)} %fusion.28, bf16[2,128,1,2,128]{4,3,0,1,2:T(2,128)(2,1)S(1)} %fusion.36), kind=kLoop, calls=%fused_computation.165 | loop fusion | flops 3932160 | bytes 3932160 | tf_op jit(solution)/shard_map/concatenate | solution.py:183
  31.5 1.6 %collective-permute-start.5 = (bf16[2,2,1,20,128]{4,3,0,1,2:T(8,128)(2,1)S(1)}, bf16[2,2,1,20,128]{4,3,0,1,2:T(8,128)(2,1)S(1)}, u32[]{:S(2)}, u32[]{:S(2)}) collective-permute-start(bf16[2,2,1,20,128]{4,3,0,1,2:T(8,128)(2,1)S(1)} %slice_select_fusion), channel_id=1, source_target_pairs={{0,2},{2,0},{1,3},{3,1},{4,6},{6,4},{5,7},{7,5},{8,10},{10,8},{9,1... | collective-permute-start | bytes 61448 | tf_op jit(solution)/shard_map/ppermute | solution.py:129
  33.5 1.8 %collective-permute-done.5 = bf16[2,2,1,20,128]{4,3,0,1,2:T(8,128)(2,1)S(1)} collective-permute-done((bf16[2,2,1,20,128]{4,3,0,1,2:T(8,128)(2,1)S(1)}, bf16[2,2,1,20,128]{4,3,0,1,2:T(8,128)(2,1)S(1)}, u32[]{:S(2)}, u32[]{:S(2)}) %collective-permute-start.5) | collective-permute-done | bytes 20512 | tf_op jit(solution)/shard_map/ppermute | solution.py:129
  35.4 0.9 maximum_convert_fusion
  36.3 2.5 %multiply_convert_fusion = (bf16[2,128,16,128]{3,2,0,1:T(8,128)(2,1)S(1)}, f32[2,128,16,128]{3,2,0,1:T(8,128)S(1)}) fusion(f32[128]{0:T(128)S(1)} %get-tuple-element.96, f32[2,132,1,20,128]{4,3,0,1,2:T(8,128)S(1)} %maximum_convert_fusion, f32[128]{0:T(128)S(1)} %get-tuple-element.89, f32[128]{0:T(128)S(1)} %get-tuple-element.90, ...), kind=kLoop, calls=%fused_computation.54 | loop fusion | flops 11534336 | bytes 22024704 | tf_op jit(solution)/shard_map/convert_element_type | solution.py:293
  38.7 0.7 convolution_multiply_fusion
  39.4 0.7 copy_multiply_fusion.grad_ref
  40.1 2.5 %shard_map.110 = f32[2,132,20,128]{3,2,1,0:T(8,128)S(1)} custom-call(f32[2,128,16,128]{3,2,1,0:T(8,128)S(1)} %copy_multiply_fusion.grad_ref, f32[9,128]{1,0:T(8,128)S(1)} %copy-done.1), custom_call_target="tpu_custom_call" | custom-call | flops 12165120 | bytes 5406720 | tf_op jit(solution)/shard_map/pallas_call | solution.py:79
  42.9 1.7 %collective-permute-start.6 = (bf16[2,2,1,20,128]{4,3,0,1,2:T(8,128)(2,1)S(1)}, bf16[2,2,1,20,128]{4,3,0,1,2:T(8,128)(2,1)S(1)}, u32[]{:S(2)}, u32[]{:S(2)}) collective-permute-start(bf16[2,2,1,20,128]{4,3,0,1,2:T(8,128)(2,1)S(1)} %get-tuple-element.53), channel_id=1, source_target_pairs={{0,2},{2,0},{1,3},{3,1},{4,6},{6,4},{5,7},{7,5},{8,10},{10,8},{9,1... | collective-permute-start | bytes 61448 | tf_op jit(solution)/shard_map/ppermute | solution.py:129
  44.6 0.5 convolution_bitcast_fusion
  45.1 1.7 %collective-permute-done.6 = bf16[2,2,1,20,128]{4,3,0,1,2:T(8,128)(2,1)S(1)} collective-permute-done((bf16[2,2,1,20,128]{4,3,0,1,2:T(8,128)(2,1)S(1)}, bf16[2,2,1,20,128]{4,3,0,1,2:T(8,128)(2,1)S(1)}, u32[]{:S(2)}, u32[]{:S(2)}) %collective-permute-start.6) | collective-permute-done | bytes 20512 | tf_op jit(solution)/shard_map/ppermute | solution.py:129
  47.6 5.0 %collective-permute-start.8 = (bf16[2,128,2,128]{3,2,0,1:T(2,128)(2,1)S(1)}, bf16[2,128,2,128]{3,2,0,1:T(2,128)(2,1)S(1)}, u32[]{:S(2)}, u32[]{:S(2)}) collective-permute-start(bf16[2,128,2,128]{3,2,0,1:T(2,128)(2,1)S(1)} %fusion.40), channel_id=1, source_target_pairs={{4,0},{8,4},{12,8},{16,12},{20,16},{24,20},{28,24},{0,28},{5,1},{9... | collective-permute-start | bytes 393224 | tf_op jit(solution)/shard_map/ppermute | solution.py:147
  53.2 1.6 %shard_map.113 = f32[9,128]{1,0:T(8,128)S(1)} custom-call(f32[2,132,20,128]{3,2,1,0:T(8,128)S(1)} %copy.141.wide_ref, f32[2,128,16,128]{3,2,1,0:T(8,128)S(1)} %copy_multiply_fusion.grad_ref), custom_call_target="tpu_custom_call" | custom-call | flops 12165120 | bytes 5406720 | tf_op jit(solution)/shard_map/pallas_call | solution.py:88
  55.1 1.0 %convert_bitcast_fusion = (f32[2,128,1,2,128]{4,3,0,1,2:T(2,128)S(1)}, f32[2,128,1,2,128]{4,3,0,1,2:T(2,128)S(1)}) fusion(bf16[2,128,2,128]{3,2,0,1:T(2,128)(2,1)S(1)} %collective-permute-done.8, bf16[2,128,2,128]{3,2,0,1:T(2,128)(2,1)S(1)} %fusion.41, bf16[2,128,2,128]{3,2,0,1:T(2,128)(2,1)S(1)} %fusion.40, ...), kind=kLoop, calls=%fused_computation.80 | loop fusion | flops 1048576 | bytes 1048576 | tf_op jit(solution)/shard_map/broadcast_in_dim | solution.py:235
  56.1 0.6 fusion.9
  56.7 0.7 copy-done.6
  57.3 0.5 convolution_bitcast_fusion.1
  57.8 1.1 %copy-done.7 = f32[2,128,16,128]{3,2,1,0:T(8,128)S(1)} copy-done((f32[2,128,16,128]{3,2,1,0:T(8,128)S(1)}, f32[2,128,16,128]{3,2,1,0:T(8,128)}, u32[]{:S(2)}) %copy-start.7) | copy-done | bytes 2097176
  58.9 0.9 add_multiply_fusion.grad_ref
  59.8 2.4 %shard_map.111 = f32[2,130,18,128]{3,2,1,0:T(8,128)S(1)} custom-call(f32[2,128,16,128]{3,2,1,0:T(8,128)S(1)} %add_multiply_fusion.grad_ref, f32[9,128]{1,0:T(8,128)S(1)} %copy-done.2), custom_call_target="tpu_custom_call" | custom-call | flops 10782720 | bytes 4792320 | tf_op jit(solution)/shard_map/pallas_call | solution.py:79
  62.5 1.6 %shard_map.112 = f32[9,128]{1,0:T(8,128)S(1)} custom-call(f32[2,130,18,128]{3,2,1,0:T(8,128)S(1)} %maximum_convert_fusion.3.wide_ref, f32[2,128,16,128]{3,2,1,0:T(8,128)S(1)} %add_multiply_fusion.grad_ref), custom_call_target="tpu_custom_call" | custom-call | flops 10782720 | bytes 4792320 | tf_op jit(solution)/shard_map/pallas_call | solution.py:88
  64.2 1.7 %collective-permute-start.9 = (bf16[2,1,1,18,128]{4,3,1,0,2:T(8,128)(2,1)S(1)}, bf16[2,1,1,18,128]{4,3,1,0,2:T(8,128)(2,1)S(1)}, u32[]{:S(2)}, u32[]{:S(2)}) collective-permute-start(bf16[2,1,1,18,128]{4,3,1,0,2:T(8,128)(2,1)S(1)} %bitcast_select_fusion), channel_id=1, source_target_pairs={{0,2},{2,0},{1,3},{3,1},{4,6},{6,4},{5,7},{7,5},{8,10},{10,8},{9,1... | collective-permute-start | bytes 27656 | tf_op jit(solution)/shard_map/ppermute | solution.py:129
  66.0 2.0 %collective-permute-done.9 = bf16[2,1,1,18,128]{4,3,1,0,2:T(8,128)(2,1)S(1)} collective-permute-done((bf16[2,1,1,18,128]{4,3,1,0,2:T(8,128)(2,1)S(1)}, bf16[2,1,1,18,128]{4,3,1,0,2:T(8,128)(2,1)S(1)}, u32[]{:S(2)}, u32[]{:S(2)}) %collective-permute-start.9) | collective-permute-done | bytes 9248 | tf_op jit(solution)/shard_map/ppermute | solution.py:129
  68.3 1.7 %collective-permute-start.13 = (f32[274,128]{1,0:T(8,128)S(1)}, f32[274,128]{1,0:T(8,128)S(1)}, u32[]{:S(2)}, u32[]{:S(2)}) collective-permute-start(f32[274,128]{1,0:T(8,128)S(1)} %fusion.63), channel_id=1, source_target_pairs={{0,2},{1,3},{2,0},{3,1},{4,6},{5,7},{6,4},{7,5},{8,10},{9,11},{10,... | collective-permute-start | bytes 420872 | tf_op jit(solution)/shard_map/ppermute | solution.py:109
  70.2 3.3 %collective-permute-done.13 = f32[274,128]{1,0:T(8,128)S(1)} collective-permute-done((f32[274,128]{1,0:T(8,128)S(1)}, f32[274,128]{1,0:T(8,128)S(1)}, u32[]{:S(2)}, u32[]{:S(2)}) %collective-permute-start.13) | collective-permute-done | bytes 140320 | tf_op jit(solution)/shard_map/ppermute | solution.py:109
  74.1 2.1 %collective-permute-start.10 = (bf16[2,128,1,128]{3,0,1,2:T(2,128)(2,1)S(1)}, bf16[2,128,1,128]{3,0,1,2:T(2,128)(2,1)S(1)}, u32[]{:S(2)}, u32[]{:S(2)}) collective-permute-start(bf16[2,128,1,128]{3,0,1,2:T(2,128)(2,1)S(1)} %copy.132), channel_id=1, source_target_pairs={{0,4},{4,8},{8,12},{12,16},{16,20},{20,24},{24,28},{28,0},{1,5},{5... | collective-permute-start | bytes 196616 | tf_op jit(solution)/shard_map/ppermute | solution.py:146
  76.2 3.2 %collective-permute-start.11 = (bf16[2,128,1,128]{3,0,1,2:T(2,128)(2,1)S(1)}, bf16[2,128,1,128]{3,0,1,2:T(2,128)(2,1)S(1)}, u32[]{:S(2)}, u32[]{:S(2)}) collective-permute-start(bf16[2,128,1,128]{3,0,1,2:T(2,128)(2,1)S(1)} %copy.135), channel_id=1, source_target_pairs={{4,0},{8,4},{12,8},{16,12},{20,16},{24,20},{28,24},{0,28},{5,1},{9... | collective-permute-start | bytes 196616 | tf_op jit(solution)/shard_map/ppermute | solution.py:147
  79.5 2.0 %collective-permute-done.10 = bf16[2,128,1,128]{3,0,1,2:T(2,128)(2,1)S(1)} collective-permute-done((bf16[2,128,1,128]{3,0,1,2:T(2,128)(2,1)S(1)}, bf16[2,128,1,128]{3,0,1,2:T(2,128)(2,1)S(1)}, u32[]{:S(2)}, u32[]{:S(2)}) %collective-permute-start.10) | collective-permute-done | bytes 65568 | tf_op jit(solution)/shard_map/ppermute | solution.py:146
  81.7 2.9 %collective-permute-done.15 = f32[274,128]{1,0:T(8,128)S(1)} collective-permute-done((f32[274,128]{1,0:T(8,128)S(1)}, f32[274,128]{1,0:T(8,128)S(1)}, u32[]{:S(2)}, u32[]{:S(2)}) %collective-permute-start.15) | collective-permute-done | bytes 140320 | tf_op jit(solution)/shard_map/ppermute | solution.py:109
  84.6 3.9 %collective-permute-start.16 = (f32[274,128]{1,0:T(8,128)S(1)}, f32[274,128]{1,0:T(8,128)S(1)}, u32[]{:S(2)}, u32[]{:S(2)}) collective-permute-start(f32[274,128]{1,0:T(8,128)S(1)} %add.192), channel_id=1, source_target_pairs={{0,16},{1,17},{2,18},{3,19},{4,20},{5,21},{6,22},{7,23},{8,24},{9,... | collective-permute-start | bytes 420872 | tf_op jit(solution)/shard_map/ppermute | solution.py:109
  88.5 0.6 fusion.5
  89.0 1.2 %copy.143 = bf16[2,128,16,128]{3,2,1,0:T(8,128)(2,1)} copy(bf16[2,128,16,128]{3,2,0,1:T(8,128)(2,1)S(1)} %fusion.5) | data formatting | bytes 2097152
  90.2 2.9 %collective-permute-done.16 = f32[274,128]{1,0:T(8,128)S(1)} collective-permute-done((f32[274,128]{1,0:T(8,128)S(1)}, f32[274,128]{1,0:T(8,128)S(1)}, u32[]{:S(2)}, u32[]{:S(2)}) %collective-permute-start.16) | collective-permute-done | bytes 140320 | tf_op jit(solution)/shard_map/ppermute | solution.py:109
  93.1 0.7 slice_multiply_fusion.18
  93.8 0.6 slice_multiply_fusion.20
  (81 shorter events, 5.0 us)
Async XLA Ops:
  0.6 20.0 %copy-start = (bf16[128,128]{1,0:T(8,128)(2,1)S(1)}, bf16[128,128]{1,0:T(8,128)(2,1)}, u32[]{:S(2)}) copy-start(bf16[128,128]{1,0:T(8,128)(2,1)} %param.10) | copy-start | bytes 98308
  0.6 10.8 %copy-start.3 = (bf16[2,128,16,128]{3,2,1,0:T(8,128)(2,1)S(1)}, bf16[2,128,16,128]{3,2,1,0:T(8,128)(2,1)}, u32[]{:S(2)}) copy-start(bf16[2,128,16,128]{3,2,1,0:T(8,128)(2,1)} %param.7) | copy-start | bytes 3145732
  2.2 8.8 %collective-permute-start = (bf16[2,128,1,128]{3,1,0,2:T(8,128)(2,1)S(1)}, bf16[2,128,1,128]{3,1,0,2:T(8,128)(2,1)S(1)}, u32[]{:S(2)}, u32[]{:S(2)}) collective-permute-start(bf16[2,128,1,128]{3,1,0,2:T(8,128)(2,1)S(1)} %bitcast.181), channel_id=1, source_target_pairs={{0,4},{4,8},{8,12},{12,16},{16,20},{20,24},{24,28},{28,0},{1,5},{5... | collective-permute-start | bytes 196616 | tf_op jit(solution)/shard_map/ppermute | solution.py:146
  5.2 6.0 %collective-permute-start.1 = (bf16[2,128,1,128]{3,1,0,2:T(8,128)(2,1)S(1)}, bf16[2,128,1,128]{3,1,0,2:T(8,128)(2,1)S(1)}, u32[]{:S(2)}, u32[]{:S(2)}) collective-permute-start(bf16[2,128,1,128]{3,1,0,2:T(8,128)(2,1)S(1)} %bitcast.180), channel_id=1, source_target_pairs={{4,0},{8,4},{12,8},{16,12},{20,16},{24,20},{28,24},{0,28},{5,1},{9... | collective-permute-start | bytes 196616 | tf_op jit(solution)/shard_map/ppermute | solution.py:147
  11.5 2.7 %copy-start.2 = (f32[9,128]{1,0:T(8,128)S(1)}, f32[9,128]{1,0:T(8,128)}, u32[]{:S(2)}) copy-start(f32[9,128]{1,0:T(8,128)} %k_ref.3) | copy-start | bytes 13828
  12.5 3.8 %collective-permute-start.2 = (bf16[2,1,1,18,128]{4,3,1,0,2:T(8,128)(2,1)S(1)}, bf16[2,1,1,18,128]{4,3,1,0,2:T(8,128)(2,1)S(1)}, u32[]{:S(2)}, u32[]{:S(2)}) collective-permute-start(bf16[2,1,1,18,128]{4,3,1,0,2:T(8,128)(2,1)S(1)} %slice_select_fusion.1), channel_id=1, source_target_pairs={{0,2},{2,0},{1,3},{3,1},{4,6},{6,4},{5,7},{7,5},{8,10},{10,8},{9,1... | collective-permute-start | bytes 27656 | tf_op jit(solution)/shard_map/ppermute | solution.py:129
  20.7 8.8 %copy-start.5 = (bf16[2,128,16,128]{3,2,1,0:T(8,128)(2,1)}, bf16[2,128,16,128]{3,2,1,0:T(8,128)(2,1)S(1)}, u32[]{:S(2)}) copy-start(bf16[2,128,16,128]{3,2,1,0:T(8,128)(2,1)S(1)} %get-tuple-element.49) | copy-start | bytes 3145732
  20.7 1.4 %copy-start.1 = (f32[9,128]{1,0:T(8,128)S(1)}, f32[9,128]{1,0:T(8,128)}, u32[]{:S(2)}) copy-start(f32[9,128]{1,0:T(8,128)} %k_ref.2) | copy-start | bytes 13828
  21.3 7.8 %collective-permute-start.3 = (bf16[2,128,2,128]{3,2,0,1:T(2,128)(2,1)S(1)}, bf16[2,128,2,128]{3,2,0,1:T(2,128)(2,1)S(1)}, u32[]{:S(2)}, u32[]{:S(2)}) collective-permute-start(bf16[2,128,2,128]{3,2,0,1:T(2,128)(2,1)S(1)} %get-tuple-element.64), channel_id=1, source_target_pairs={{0,4},{4,8},{8,12},{12,16},{16,20},{20,24},{24,28},{28,0},{1,5},{5... | collective-permute-start | bytes 393224 | tf_op jit(solution)/shard_map/ppermute | solution.py:146
  22.1 7.2 %collective-permute-start.4 = (bf16[2,128,2,128]{3,2,0,1:T(2,128)(2,1)S(1)}, bf16[2,128,2,128]{3,2,0,1:T(2,128)(2,1)S(1)}, u32[]{:S(2)}, u32[]{:S(2)}) collective-permute-start(bf16[2,128,2,128]{3,2,0,1:T(2,128)(2,1)S(1)} %get-tuple-element.65), channel_id=1, source_target_pairs={{4,0},{8,4},{12,8},{16,12},{20,16},{24,20},{28,24},{0,28},{5,1},{9... | collective-permute-start | bytes 393224 | tf_op jit(solution)/shard_map/ppermute | solution.py:147
  31.5 3.8 %collective-permute-start.5 = (bf16[2,2,1,20,128]{4,3,0,1,2:T(8,128)(2,1)S(1)}, bf16[2,2,1,20,128]{4,3,0,1,2:T(8,128)(2,1)S(1)}, u32[]{:S(2)}, u32[]{:S(2)}) collective-permute-start(bf16[2,2,1,20,128]{4,3,0,1,2:T(8,128)(2,1)S(1)} %slice_select_fusion), channel_id=1, source_target_pairs={{0,2},{2,0},{1,3},{3,1},{4,6},{6,4},{5,7},{7,5},{8,10},{10,8},{9,1... | collective-permute-start | bytes 61448 | tf_op jit(solution)/shard_map/ppermute | solution.py:129
  36.2 2.5 %copy-start.8 = (bf16[2,128,16,128]{3,2,1,0:T(8,128)(2,1)S(1)}, bf16[2,128,16,128]{3,2,1,0:T(8,128)(2,1)}, u32[]{:S(2)}) copy-start(bf16[2,128,16,128]{3,2,1,0:T(8,128)(2,1)} %param.8) | copy-start | bytes 3145732
  36.3 2.5 %copy-start.10 = (bf16[128,128]{1,0:T(8,128)(2,1)S(1)}, bf16[128,128]{1,0:T(8,128)(2,1)}, u32[]{:S(2)}) copy-start(bf16[128,128]{1,0:T(8,128)(2,1)} %param.12) | copy-start | bytes 98308
  42.9 3.9 %collective-permute-start.6 = (bf16[2,2,1,20,128]{4,3,0,1,2:T(8,128)(2,1)S(1)}, bf16[2,2,1,20,128]{4,3,0,1,2:T(8,128)(2,1)S(1)}, u32[]{:S(2)}, u32[]{:S(2)}) collective-permute-start(bf16[2,2,1,20,128]{4,3,0,1,2:T(8,128)(2,1)S(1)} %get-tuple-element.53), channel_id=1, source_target_pairs={{0,2},{2,0},{1,3},{3,1},{4,6},{6,4},{5,7},{7,5},{8,10},{10,8},{9,1... | collective-permute-start | bytes 61448 | tf_op jit(solution)/shard_map/ppermute | solution.py:129
  46.8 5.8 %copy-start.4 = (bf16[2,128,20,128]{3,2,0,1:T(8,128)(2,1)S(1)}, bf16[2,128,20,128]{3,2,0,1:T(8,128)(2,1)}, u32[]{:S(2)}) copy-start(bf16[2,128,20,128]{3,2,0,1:T(8,128)(2,1)} %get-tuple-element.62) | copy-start | bytes 3932164
  47.4 7.7 %collective-permute-start.7 = (bf16[2,128,2,128]{3,2,0,1:T(2,128)(2,1)S(1)}, bf16[2,128,2,128]{3,2,0,1:T(2,128)(2,1)S(1)}, u32[]{:S(2)}, u32[]{:S(2)}) collective-permute-start(bf16[2,128,2,128]{3,2,0,1:T(2,128)(2,1)S(1)} %fusion.41), channel_id=1, source_target_pairs={{0,4},{4,8},{8,12},{12,16},{16,20},{20,24},{24,28},{28,0},{1,5},{5... | collective-permute-start | bytes 393224 | tf_op jit(solution)/shard_map/ppermute | solution.py:146
  47.6 7.5 %collective-permute-start.8 = (bf16[2,128,2,128]{3,2,0,1:T(2,128)(2,1)S(1)}, bf16[2,128,2,128]{3,2,0,1:T(2,128)(2,1)S(1)}, u32[]{:S(2)}, u32[]{:S(2)}) collective-permute-start(bf16[2,128,2,128]{3,2,0,1:T(2,128)(2,1)S(1)} %fusion.40), channel_id=1, source_target_pairs={{4,0},{8,4},{12,8},{16,12},{20,16},{24,20},{28,24},{0,28},{5,1},{9... | collective-permute-start | bytes 393224 | tf_op jit(solution)/shard_map/ppermute | solution.py:147
  53.2 2.9 %copy-start.9 = (bf16[2,128,16,128]{3,2,1,0:T(8,128)(2,1)S(1)}, bf16[2,128,16,128]{3,2,1,0:T(8,128)(2,1)}, u32[]{:S(2)}) copy-start(bf16[2,128,16,128]{3,2,1,0:T(8,128)(2,1)} %param.8) | copy-start | bytes 3145732
  56.1 1.2 %copy-start.6 = (bf16[2,128,16,128]{3,2,1,0:T(8,128)(2,1)S(1)}, bf16[2,128,16,128]{3,2,1,0:T(8,128)(2,1)}, u32[]{:S(2)}) copy-start(bf16[2,128,16,128]{3,2,1,0:T(8,128)(2,1)} %copy-done.5) | copy-start | bytes 3145732
  57.3 1.6 %copy-start.7 = (f32[2,128,16,128]{3,2,1,0:T(8,128)S(1)}, f32[2,128,16,128]{3,2,1,0:T(8,128)}, u32[]{:S(2)}) copy-start(f32[2,128,16,128]{3,2,1,0:T(8,128)} %get-tuple-element.50) | copy-start | bytes 6291460
  64.2 4.1 %collective-permute-start.12 = (f32[274,128]{1,0:T(8,128)S(1)}, f32[274,128]{1,0:T(8,128)S(1)}, u32[]{:S(2)}, u32[]{:S(2)}) collective-permute-start(f32[274,128]{1,0:T(8,128)S(1)} %pad_maximum_fusion.2), channel_id=1, source_target_pairs={{0,1},{1,0},{2,3},{3,2},{4,5},{5,4},{6,7},{7,6},{8,9},{9,8},{10,11... | collective-permute-start | bytes 420872 | tf_op jit(solution)/shard_map/ppermute | solution.py:109
  64.2 3.8 %collective-permute-start.9 = (bf16[2,1,1,18,128]{4,3,1,0,2:T(8,128)(2,1)S(1)}, bf16[2,1,1,18,128]{4,3,1,0,2:T(8,128)(2,1)S(1)}, u32[]{:S(2)}, u32[]{:S(2)}) collective-permute-start(bf16[2,1,1,18,128]{4,3,1,0,2:T(8,128)(2,1)S(1)} %bitcast_select_fusion), channel_id=1, source_target_pairs={{0,2},{2,0},{1,3},{3,1},{4,6},{6,4},{5,7},{7,5},{8,10},{10,8},{9,1... | collective-permute-start | bytes 27656 | tf_op jit(solution)/shard_map/ppermute | solution.py:129
  68.3 5.2 %collective-permute-start.13 = (f32[274,128]{1,0:T(8,128)S(1)}, f32[274,128]{1,0:T(8,128)S(1)}, u32[]{:S(2)}, u32[]{:S(2)}) collective-permute-start(f32[274,128]{1,0:T(8,128)S(1)} %fusion.63), channel_id=1, source_target_pairs={{0,2},{1,3},{2,0},{3,1},{4,6},{5,7},{6,4},{7,5},{8,10},{9,11},{10,... | collective-permute-start | bytes 420872 | tf_op jit(solution)/shard_map/ppermute | solution.py:109
  73.5 6.0 %collective-permute-start.14 = (f32[274,128]{1,0:T(8,128)S(1)}, f32[274,128]{1,0:T(8,128)S(1)}, u32[]{:S(2)}, u32[]{:S(2)}) collective-permute-start(f32[274,128]{1,0:T(8,128)S(1)} %add.190), channel_id=1, source_target_pairs={{0,4},{1,5},{2,6},{3,7},{4,0},{5,1},{6,2},{7,3},{8,12},{9,13},{10,... | collective-permute-start | bytes 420872 | tf_op jit(solution)/shard_map/ppermute | solution.py:109
  74.1 7.4 %collective-permute-start.10 = (bf16[2,128,1,128]{3,0,1,2:T(2,128)(2,1)S(1)}, bf16[2,128,1,128]{3,0,1,2:T(2,128)(2,1)S(1)}, u32[]{:S(2)}, u32[]{:S(2)}) collective-permute-start(bf16[2,128,1,128]{3,0,1,2:T(2,128)(2,1)S(1)} %copy.132), channel_id=1, source_target_pairs={{0,4},{4,8},{8,12},{12,16},{16,20},{20,24},{24,28},{28,0},{1,5},{5... | collective-permute-start | bytes 196616 | tf_op jit(solution)/shard_map/ppermute | solution.py:146
  76.2 5.3 %collective-permute-start.11 = (bf16[2,128,1,128]{3,0,1,2:T(2,128)(2,1)S(1)}, bf16[2,128,1,128]{3,0,1,2:T(2,128)(2,1)S(1)}, u32[]{:S(2)}, u32[]{:S(2)}) collective-permute-start(bf16[2,128,1,128]{3,0,1,2:T(2,128)(2,1)S(1)} %copy.135), channel_id=1, source_target_pairs={{4,0},{8,4},{12,8},{16,12},{20,16},{24,20},{28,24},{0,28},{5,1},{9... | collective-permute-start | bytes 196616 | tf_op jit(solution)/shard_map/ppermute | solution.py:147
  79.4 5.2 %collective-permute-start.15 = (f32[274,128]{1,0:T(8,128)S(1)}, f32[274,128]{1,0:T(8,128)S(1)}, u32[]{:S(2)}, u32[]{:S(2)}) collective-permute-start(f32[274,128]{1,0:T(8,128)S(1)} %add.191), channel_id=1, source_target_pairs={{0,8},{1,9},{2,10},{3,11},{4,12},{5,13},{6,14},{7,15},{8,0},{9,1},... | collective-permute-start | bytes 420872 | tf_op jit(solution)/shard_map/ppermute | solution.py:109
  84.6 8.5 %collective-permute-start.16 = (f32[274,128]{1,0:T(8,128)S(1)}, f32[274,128]{1,0:T(8,128)S(1)}, u32[]{:S(2)}, u32[]{:S(2)}) collective-permute-start(f32[274,128]{1,0:T(8,128)S(1)} %add.192), channel_id=1, source_target_pairs={{0,16},{1,17},{2,18},{3,19},{4,20},{5,21},{6,22},{7,23},{8,24},{9,... | collective-permute-start | bytes 420872 | tf_op jit(solution)/shard_map/ppermute | solution.py:109

commit v5 on v4

--- a/solution.py
+++ b/solution.py
@@ -103,11 +103,11 @@
         count *= size
     if count & (count - 1):
         return lax.psum(value, axes)
-    bit = 1
-    while bit < count:
+    bit = count // 2
+    while bit >= 1:
         pairs = [(i, i ^ bit) for i in range(count)]
         value = value + lax.ppermute(value, axes, pairs)
-        bit *= 2
+        bit //= 2
     return value
 
 

time: 94.6 us -> 92.4 us (0.977)
  starting transfers between devices: 34 us -> 31.3 us
    ppermute x5, starting transfers between devices: 5.79 us -> 3.74 us  [tree_sum(): value = value + lax.ppermute(value, axes, pairs)]
    ppermute x5, waiting for transfers between devices: 9.09 us -> 11 us  [tree_sum(): value = value + lax.ppermute(value, axes, pairs)]
    ppermute x4, waiting for transfers between devices: 5.07 us -> 3.45 us  [with_halo(): before = lax.ppermute(last, axis, up)]
    ppermute x4, starting transfers between devices: 5.9 us -> 4.55 us  [with_halo(): before = lax.ppermute(last, axis, up)]
  transfers between devices with their start and end apart: 17 -> 17, of which waited for: 10 -> 10; matrix products, arithmetic and copies ran while one was open for 6% -> 7% of each run, Pallas kernels for 2% -> 2%
where the time goes in v5:
time: 92.4 us; the launch traced here: 92.1 us
  starting transfers between devices  31.3 us (34%)
  waiting for transfers between devices  22.3 us (24%)
  other arithmetic  17.4 us (19%)
  Pallas kernels  8.13 us (9%)
  local copies, waits for them, and re-layouts  7.69 us (8%)
  matrix products  2.95 us (3%)
  between operations  2.46 us (3%)
    ppermute x4, starting transfers between devices, with_halo(): after = lax.ppermute(first, axis, down)  16.5 us
    ppermute x5, waiting for transfers between devices, tree_sum(): value = value + lax.ppermute(value, axes, pairs)  11 us
    ppermute x4, waiting for transfers between devices, swap_halo(): got = lax.ppermute(sent, axis, [(0, 1), (1, 0)])  7.78 us
    ppermute x4, starting transfers between devices, swap_halo(): got = lax.ppermute(sent, axis, [(0, 1), (1, 0)])  6.52 us
    pallas_call x2, Pallas kernels, conv_back_kernel(): pl.pallas_call(functools.partial(wide_grad_body, margin), out_shape=jax.S...  4.91 us
    ppermute x4, starting transfers between devices, with_halo(): before = lax.ppermute(last, axis, up)  4.55 us
    ppermute x5, starting transfers between devices, tree_sum(): value = value + lax.ppermute(value, axes, pairs)  3.74 us
    convert_element_type x1, other arithmetic, shards(): act_one = jax.nn.silu(pre_one).astype(jnp.bfloat16)  3.53 us
  transfers between devices with their start and end apart: 17, of which 10 were waited for; matrix products, arithmetic and copies ran while one was open for 7% of the time, Pallas kernels for 2%

profile of v5, /device:TPU:0, one launch (start us, length us, event | category | flops | bytes accessed | tf_op | source)
XLA Modules:
  0.0 92.1 jit_solution(13036849105929680193)
XLA Ops:
  0.7 1.5 %fusion.59 = (bf16[2,128,1,1,128]{4,3,1,0,2:T(2,128)(2,1)S(1)}, bf16[2,128,1,1,128]{4,3,1,0,2:T(2,128)(2,1)S(1)}) fusion(bf16[2,128,1,16,128]{4,3,1,0,2:T(8,128)(2,1)} %bitcast.169), kind=kLoop, calls=%fused_computation.169 | loop fusion | bytes 262144 | tf_op jit(solution)/shard_map/slice | solution.py:169
  2.2 3.0 %collective-permute-start = (bf16[2,128,1,128]{3,1,0,2:T(8,128)(2,1)S(1)}, bf16[2,128,1,128]{3,1,0,2:T(8,128)(2,1)S(1)}, u32[]{:S(2)}, u32[]{:S(2)}) collective-permute-start(bf16[2,128,1,128]{3,1,0,2:T(8,128)(2,1)S(1)} %bitcast.181), channel_id=1, source_target_pairs={{0,4},{4,8},{8,12},{12,16},{16,20},{20,24},{24,28},{28,0},{1,5},{5... | collective-permute-start | bytes 196616 | tf_op jit(solution)/shard_map/ppermute | solution.py:146
  5.2 3.1 %collective-permute-start.1 = (bf16[2,128,1,128]{3,1,0,2:T(8,128)(2,1)S(1)}, bf16[2,128,1,128]{3,1,0,2:T(8,128)(2,1)S(1)}, u32[]{:S(2)}, u32[]{:S(2)}) collective-permute-start(bf16[2,128,1,128]{3,1,0,2:T(8,128)(2,1)S(1)} %bitcast.180), channel_id=1, source_target_pairs={{4,0},{8,4},{12,8},{16,12},{20,16},{24,20},{28,24},{0,28},{5,1},{9... | collective-permute-start | bytes 196616 | tf_op jit(solution)/shard_map/ppermute | solution.py:147
  8.3 1.3 %fusion.60 = (s32[1,1]{1,0:T(1,128)}, s32[1,1]{1,0:T(1,128)}) fusion(s32[2,8]{1,0:T(2,128)} %param.13, s32[]{:T(128)S(6)} %clamp.1, s32[]{:T(128)} %bitcast.3, s32[]{:T(128)} %bitcast.8), kind=kLoop, calls=%fused_computation.170 | loop fusion | bytes 28 | tf_op jit(solution)/shard_map/jit(_take)/gather | solution.py:159
  11.5 1.0 %fusion.54 = (bf16[2,128,18,128]{3,2,1,0:T(8,128)(2,1)S(1)}, bf16[2,128,1,18,128]{4,3,1,0,2:T(8,128)(2,1)S(1)}) fusion(bf16[2,128,1,1,128]{4,3,1,0,2:T(2,128)(2,1)S(1)} %copy.114, bf16[2,128,1,16,128]{4,3,1,0,2:T(8,128)(2,1)S(1)} %bitcast.170, bf16[2,128,1,1,128]{4,3,1,0,2:T(2,128)(2,1)S(1)} %copy.113), kind=kLoop, calls=%fused_computation.166 | loop fusion | flops 3538944 | bytes 3538944 | tf_op jit(solution)/shard_map/concatenate | solution.py:183
  12.5 1.7 %collective-permute-start.2 = (bf16[2,1,1,18,128]{4,3,1,0,2:T(8,128)(2,1)S(1)}, bf16[2,1,1,18,128]{4,3,1,0,2:T(8,128)(2,1)S(1)}, u32[]{:S(2)}, u32[]{:S(2)}) collective-permute-start(bf16[2,1,1,18,128]{4,3,1,0,2:T(8,128)(2,1)S(1)} %slice_select_fusion.1), channel_id=1, source_target_pairs={{0,2},{2,0},{1,3},{3,1},{4,6},{6,4},{5,7},{7,5},{8,10},{10,8},{9,1... | collective-permute-start | bytes 27656 | tf_op jit(solution)/shard_map/ppermute | solution.py:129
  14.2 2.0 %collective-permute-done.2 = bf16[2,1,1,18,128]{4,3,1,0,2:T(8,128)(2,1)S(1)} collective-permute-done((bf16[2,1,1,18,128]{4,3,1,0,2:T(8,128)(2,1)S(1)}, bf16[2,1,1,18,128]{4,3,1,0,2:T(8,128)(2,1)S(1)}, u32[]{:S(2)}, u32[]{:S(2)}) %collective-permute-start.2) | collective-permute-done | bytes 9248 | tf_op jit(solution)/shard_map/ppermute | solution.py:129
  16.2 0.9 maximum_convert_fusion.2
  17.1 3.5 %multiply_convert_fusion.1 = (bf16[2,128,16,128]{3,2,1,0:T(8,128)(2,1)S(1)}, f32[2,128,16,128]{3,2,1,0:T(8,128)}) fusion(f32[128]{0:T(128)S(1)} %get-tuple-element.105, f32[2,130,1,18,128]{4,3,1,0,2:T(8,128)S(1)} %maximum_convert_fusion.2, f32[128]{0:T(128)S(1)} %get-tuple-element.98, f32[128]{0:T(128)S(1)} %get-tuple-element.99, ...), kind=kLoop, calls=%fused_computation.59 | loop fusion | flops 11534336 | bytes 22024704 | tf_op jit(solution)/shard_map/convert_element_type | solution.py:289
  20.7 0.4 fusion.28
  21.3 0.8 collective-permute-start.3
  22.1 4.2 %collective-permute-start.4 = (bf16[2,128,2,128]{3,2,0,1:T(2,128)(2,1)S(1)}, bf16[2,128,2,128]{3,2,0,1:T(2,128)(2,1)S(1)}, u32[]{:S(2)}, u32[]{:S(2)}) collective-permute-start(bf16[2,128,2,128]{3,2,0,1:T(2,128)(2,1)S(1)} %get-tuple-element.65), channel_id=1, source_target_pairs={{4,0},{8,4},{12,8},{16,12},{20,16},{24,20},{28,24},{0,28},{5,1},{9... | collective-permute-start | bytes 393224 | tf_op jit(solution)/shard_map/ppermute | solution.py:147
  26.3 2.8 %collective-permute-done.3 = bf16[2,128,2,128]{3,2,0,1:T(2,128)(2,1)S(1)} collective-permute-done((bf16[2,128,2,128]{3,2,0,1:T(2,128)(2,1)S(1)}, bf16[2,128,2,128]{3,2,0,1:T(2,128)(2,1)S(1)}, u32[]{:S(2)}, u32[]{:S(2)}) %collective-permute-start.3) | collective-permute-done | bytes 131104 | tf_op jit(solution)/shard_map/ppermute | solution.py:146
  29.4 2.1 %fusion.53 = (bf16[2,128,20,128]{3,2,0,1:T(8,128)(2,1)}, bf16[2,128,1,20,128]{4,3,0,1,2:T(8,128)(2,1)S(1)}) fusion(bf16[2,128,1,2,128]{4,3,0,1,2:T(2,128)(2,1)S(1)} %fusion.37, bf16[2,128,1,16,128]{4,3,0,1,2:T(8,128)(2,1)S(1)} %fusion.28, bf16[2,128,1,2,128]{4,3,0,1,2:T(2,128)(2,1)S(1)} %fusion.36), kind=kLoop, calls=%fused_computation.165 | loop fusion | flops 3932160 | bytes 3932160 | tf_op jit(solution)/shard_map/concatenate | solution.py:183
  31.5 1.6 %collective-permute-start.5 = (bf16[2,2,1,20,128]{4,3,0,1,2:T(8,128)(2,1)S(1)}, bf16[2,2,1,20,128]{4,3,0,1,2:T(8,128)(2,1)S(1)}, u32[]{:S(2)}, u32[]{:S(2)}) collective-permute-start(bf16[2,2,1,20,128]{4,3,0,1,2:T(8,128)(2,1)S(1)} %slice_select_fusion), channel_id=1, source_target_pairs={{0,2},{2,0},{1,3},{3,1},{4,6},{6,4},{5,7},{7,5},{8,10},{10,8},{9,1... | collective-permute-start | bytes 61448 | tf_op jit(solution)/shard_map/ppermute | solution.py:129
  33.5 1.8 %collective-permute-done.5 = bf16[2,2,1,20,128]{4,3,0,1,2:T(8,128)(2,1)S(1)} collective-permute-done((bf16[2,2,1,20,128]{4,3,0,1,2:T(8,128)(2,1)S(1)}, bf16[2,2,1,20,128]{4,3,0,1,2:T(8,128)(2,1)S(1)}, u32[]{:S(2)}, u32[]{:S(2)}) %collective-permute-start.5) | collective-permute-done | bytes 20512 | tf_op jit(solution)/shard_map/ppermute | solution.py:129
  35.4 0.9 maximum_convert_fusion
  36.3 2.5 %multiply_convert_fusion = (bf16[2,128,16,128]{3,2,0,1:T(8,128)(2,1)S(1)}, f32[2,128,16,128]{3,2,0,1:T(8,128)S(1)}) fusion(f32[128]{0:T(128)S(1)} %get-tuple-element.96, f32[2,132,1,20,128]{4,3,0,1,2:T(8,128)S(1)} %maximum_convert_fusion, f32[128]{0:T(128)S(1)} %get-tuple-element.89, f32[128]{0:T(128)S(1)} %get-tuple-element.90, ...), kind=kLoop, calls=%fused_computation.54 | loop fusion | flops 11534336 | bytes 22024704 | tf_op jit(solution)/shard_map/convert_element_type | solution.py:293
  38.7 0.7 convolution_multiply_fusion
  39.4 0.7 copy_multiply_fusion.grad_ref
  40.1 2.5 %shard_map.110 = f32[2,132,20,128]{3,2,1,0:T(8,128)S(1)} custom-call(f32[2,128,16,128]{3,2,1,0:T(8,128)S(1)} %copy_multiply_fusion.grad_ref, f32[9,128]{1,0:T(8,128)S(1)} %copy-done.1), custom_call_target="tpu_custom_call" | custom-call | flops 12165120 | bytes 5406720 | tf_op jit(solution)/shard_map/pallas_call | solution.py:79
  42.9 1.7 %collective-permute-start.6 = (bf16[2,2,1,20,128]{4,3,0,1,2:T(8,128)(2,1)S(1)}, bf16[2,2,1,20,128]{4,3,0,1,2:T(8,128)(2,1)S(1)}, u32[]{:S(2)}, u32[]{:S(2)}) collective-permute-start(bf16[2,2,1,20,128]{4,3,0,1,2:T(8,128)(2,1)S(1)} %get-tuple-element.53), channel_id=1, source_target_pairs={{0,2},{2,0},{1,3},{3,1},{4,6},{6,4},{5,7},{7,5},{8,10},{10,8},{9,1... | collective-permute-start | bytes 61448 | tf_op jit(solution)/shard_map/ppermute | solution.py:129
  44.6 0.5 convolution_bitcast_fusion
  45.1 1.7 %collective-permute-done.6 = bf16[2,2,1,20,128]{4,3,0,1,2:T(8,128)(2,1)S(1)} collective-permute-done((bf16[2,2,1,20,128]{4,3,0,1,2:T(8,128)(2,1)S(1)}, bf16[2,2,1,20,128]{4,3,0,1,2:T(8,128)(2,1)S(1)}, u32[]{:S(2)}, u32[]{:S(2)}) %collective-permute-start.6) | collective-permute-done | bytes 20512 | tf_op jit(solution)/shard_map/ppermute | solution.py:129
  47.6 5.0 %collective-permute-start.8 = (bf16[2,128,2,128]{3,2,0,1:T(2,128)(2,1)S(1)}, bf16[2,128,2,128]{3,2,0,1:T(2,128)(2,1)S(1)}, u32[]{:S(2)}, u32[]{:S(2)}) collective-permute-start(bf16[2,128,2,128]{3,2,0,1:T(2,128)(2,1)S(1)} %fusion.40), channel_id=1, source_target_pairs={{4,0},{8,4},{12,8},{16,12},{20,16},{24,20},{28,24},{0,28},{5,1},{9... | collective-permute-start | bytes 393224 | tf_op jit(solution)/shard_map/ppermute | solution.py:147
  53.2 1.6 %shard_map.113 = f32[9,128]{1,0:T(8,128)S(1)} custom-call(f32[2,132,20,128]{3,2,1,0:T(8,128)S(1)} %copy.141.wide_ref, f32[2,128,16,128]{3,2,1,0:T(8,128)S(1)} %copy_multiply_fusion.grad_ref), custom_call_target="tpu_custom_call" | custom-call | flops 12165120 | bytes 5406720 | tf_op jit(solution)/shard_map/pallas_call | solution.py:88
  55.1 1.0 %convert_bitcast_fusion = (f32[2,128,1,2,128]{4,3,0,1,2:T(2,128)S(1)}, f32[2,128,1,2,128]{4,3,0,1,2:T(2,128)S(1)}) fusion(bf16[2,128,2,128]{3,2,0,1:T(2,128)(2,1)S(1)} %collective-permute-done.8, bf16[2,128,2,128]{3,2,0,1:T(2,128)(2,1)S(1)} %fusion.41, bf16[2,128,2,128]{3,2,0,1:T(2,128)(2,1)S(1)} %fusion.40, ...), kind=kLoop, calls=%fused_computation.80 | loop fusion | flops 1048576 | bytes 1048576 | tf_op jit(solution)/shard_map/broadcast_in_dim | solution.py:235
  56.1 0.6 fusion.9
  56.7 0.7 copy-done.6
  57.3 0.5 convolution_bitcast_fusion.1
  57.8 1.1 %copy-done.7 = f32[2,128,16,128]{3,2,1,0:T(8,128)S(1)} copy-done((f32[2,128,16,128]{3,2,1,0:T(8,128)S(1)}, f32[2,128,16,128]{3,2,1,0:T(8,128)}, u32[]{:S(2)}) %copy-start.7) | copy-done | bytes 2097176
  58.9 0.9 add_multiply_fusion.grad_ref
  59.8 2.4 %shard_map.111 = f32[2,130,18,128]{3,2,1,0:T(8,128)S(1)} custom-call(f32[2,128,16,128]{3,2,1,0:T(8,128)S(1)} %add_multiply_fusion.grad_ref, f32[9,128]{1,0:T(8,128)S(1)} %copy-done.2), custom_call_target="tpu_custom_call" | custom-call | flops 10782720 | bytes 4792320 | tf_op jit(solution)/shard_map/pallas_call | solution.py:79
  62.5 1.6 %shard_map.112 = f32[9,128]{1,0:T(8,128)S(1)} custom-call(f32[2,130,18,128]{3,2,1,0:T(8,128)S(1)} %maximum_convert_fusion.3.wide_ref, f32[2,128,16,128]{3,2,1,0:T(8,128)S(1)} %add_multiply_fusion.grad_ref), custom_call_target="tpu_custom_call" | custom-call | flops 10782720 | bytes 4792320 | tf_op jit(solution)/shard_map/pallas_call | solution.py:88
  64.2 0.5 collective-permute-start.12
  64.6 1.5 %collective-permute-start.9 = (bf16[2,1,1,18,128]{4,3,1,0,2:T(8,128)(2,1)S(1)}, bf16[2,1,1,18,128]{4,3,1,0,2:T(8,128)(2,1)S(1)}, u32[]{:S(2)}, u32[]{:S(2)}) collective-permute-start(bf16[2,1,1,18,128]{4,3,1,0,2:T(8,128)(2,1)S(1)} %bitcast_select_fusion), channel_id=1, source_target_pairs={{0,2},{2,0},{1,3},{3,1},{4,6},{6,4},{5,7},{7,5},{8,10},{10,8},{9,1... | collective-permute-start | bytes 27656 | tf_op jit(solution)/shard_map/ppermute | solution.py:129
  66.1 2.2 %collective-permute-done.9 = bf16[2,1,1,18,128]{4,3,1,0,2:T(8,128)(2,1)S(1)} collective-permute-done((bf16[2,1,1,18,128]{4,3,1,0,2:T(8,128)(2,1)S(1)}, bf16[2,1,1,18,128]{4,3,1,0,2:T(8,128)(2,1)S(1)}, u32[]{:S(2)}, u32[]{:S(2)}) %collective-permute-start.9) | collective-permute-done | bytes 9248 | tf_op jit(solution)/shard_map/ppermute | solution.py:129
  68.5 3.2 %collective-permute-done.12 = f32[274,128]{1,0:T(8,128)S(1)} collective-permute-done((f32[274,128]{1,0:T(8,128)S(1)}, f32[274,128]{1,0:T(8,128)S(1)}, u32[]{:S(2)}, u32[]{:S(2)}) %collective-permute-start.12) | collective-permute-done | bytes 140320 | tf_op jit(solution)/shard_map/ppermute | solution.py:109
  72.0 4.9 %collective-permute-done.13 = f32[274,128]{1,0:T(8,128)S(1)} collective-permute-done((f32[274,128]{1,0:T(8,128)S(1)}, f32[274,128]{1,0:T(8,128)S(1)}, u32[]{:S(2)}, u32[]{:S(2)}) %collective-permute-start.13) | collective-permute-done | bytes 140320 | tf_op jit(solution)/shard_map/ppermute | solution.py:109
  77.0 1.4 %collective-permute-start.14 = (f32[274,128]{1,0:T(8,128)S(1)}, f32[274,128]{1,0:T(8,128)S(1)}, u32[]{:S(2)}, u32[]{:S(2)}) collective-permute-start(f32[274,128]{1,0:T(8,128)S(1)} %add.190), channel_id=1, source_target_pairs={{0,4},{1,5},{2,6},{3,7},{4,0},{5,1},{6,2},{7,3},{8,12},{9,13},{10,... | collective-permute-start | bytes 420872 | tf_op jit(solution)/shard_map/ppermute | solution.py:109
  78.9 0.7 collective-permute-start.10
  79.7 4.1 %collective-permute-start.11 = (bf16[2,128,1,128]{3,0,1,2:T(2,128)(2,1)S(1)}, bf16[2,128,1,128]{3,0,1,2:T(2,128)(2,1)S(1)}, u32[]{:S(2)}, u32[]{:S(2)}) collective-permute-start(bf16[2,128,1,128]{3,0,1,2:T(2,128)(2,1)S(1)} %copy.135), channel_id=1, source_target_pairs={{4,0},{8,4},{12,8},{16,12},{20,16},{24,20},{28,24},{0,28},{5,1},{9... | collective-permute-start | bytes 196616 | tf_op jit(solution)/shard_map/ppermute | solution.py:147
  83.8 1.7 %collective-permute-start.15 = (f32[274,128]{1,0:T(8,128)S(1)}, f32[274,128]{1,0:T(8,128)S(1)}, u32[]{:S(2)}, u32[]{:S(2)}) collective-permute-start(f32[274,128]{1,0:T(8,128)S(1)} %add.191), channel_id=1, source_target_pairs={{0,2},{1,3},{2,0},{3,1},{4,6},{5,7},{6,4},{7,5},{8,10},{9,11},{10,... | collective-permute-start | bytes 420872 | tf_op jit(solution)/shard_map/ppermute | solution.py:109
  86.1 2.9 %collective-permute-done.15 = f32[274,128]{1,0:T(8,128)S(1)} collective-permute-done((f32[274,128]{1,0:T(8,128)S(1)}, f32[274,128]{1,0:T(8,128)S(1)}, u32[]{:S(2)}, u32[]{:S(2)}) %collective-permute-start.15) | collective-permute-done | bytes 140320 | tf_op jit(solution)/shard_map/ppermute | solution.py:109
  89.1 0.6 fusion.5
  89.7 1.2 %copy.143 = bf16[2,128,16,128]{3,2,1,0:T(8,128)(2,1)} copy(bf16[2,128,16,128]{3,2,0,1:T(8,128)(2,1)S(1)} %fusion.5) | data formatting | bytes 2097152
  90.9 0.7 slice_multiply_fusion.18
  91.5 0.6 slice_multiply_fusion.20
  (81 shorter events, 5.3 us)
Async XLA Ops:
  0.6 20.0 %copy-start = (bf16[128,128]{1,0:T(8,128)(2,1)S(1)}, bf16[128,128]{1,0:T(8,128)(2,1)}, u32[]{:S(2)}) copy-start(bf16[128,128]{1,0:T(8,128)(2,1)} %param.10) | copy-start | bytes 98308
  0.6 10.8 %copy-start.3 = (bf16[2,128,16,128]{3,2,1,0:T(8,128)(2,1)S(1)}, bf16[2,128,16,128]{3,2,1,0:T(8,128)(2,1)}, u32[]{:S(2)}) copy-start(bf16[2,128,16,128]{3,2,1,0:T(8,128)(2,1)} %param.7) | copy-start | bytes 3145732
  2.2 8.8 %collective-permute-start = (bf16[2,128,1,128]{3,1,0,2:T(8,128)(2,1)S(1)}, bf16[2,128,1,128]{3,1,0,2:T(8,128)(2,1)S(1)}, u32[]{:S(2)}, u32[]{:S(2)}) collective-permute-start(bf16[2,128,1,128]{3,1,0,2:T(8,128)(2,1)S(1)} %bitcast.181), channel_id=1, source_target_pairs={{0,4},{4,8},{8,12},{12,16},{16,20},{20,24},{24,28},{28,0},{1,5},{5... | collective-permute-start | bytes 196616 | tf_op jit(solution)/shard_map/ppermute | solution.py:146
  5.2 6.0 %collective-permute-start.1 = (bf16[2,128,1,128]{3,1,0,2:T(8,128)(2,1)S(1)}, bf16[2,128,1,128]{3,1,0,2:T(8,128)(2,1)S(1)}, u32[]{:S(2)}, u32[]{:S(2)}) collective-permute-start(bf16[2,128,1,128]{3,1,0,2:T(8,128)(2,1)S(1)} %bitcast.180), channel_id=1, source_target_pairs={{4,0},{8,4},{12,8},{16,12},{20,16},{24,20},{28,24},{0,28},{5,1},{9... | collective-permute-start | bytes 196616 | tf_op jit(solution)/shard_map/ppermute | solution.py:147
  11.5 2.7 %copy-start.2 = (f32[9,128]{1,0:T(8,128)S(1)}, f32[9,128]{1,0:T(8,128)}, u32[]{:S(2)}) copy-start(f32[9,128]{1,0:T(8,128)} %k_ref.3) | copy-start | bytes 13828
  12.5 3.8 %collective-permute-start.2 = (bf16[2,1,1,18,128]{4,3,1,0,2:T(8,128)(2,1)S(1)}, bf16[2,1,1,18,128]{4,3,1,0,2:T(8,128)(2,1)S(1)}, u32[]{:S(2)}, u32[]{:S(2)}) collective-permute-start(bf16[2,1,1,18,128]{4,3,1,0,2:T(8,128)(2,1)S(1)} %slice_select_fusion.1), channel_id=1, source_target_pairs={{0,2},{2,0},{1,3},{3,1},{4,6},{6,4},{5,7},{7,5},{8,10},{10,8},{9,1... | collective-permute-start | bytes 27656 | tf_op jit(solution)/shard_map/ppermute | solution.py:129
  20.7 8.8 %copy-start.5 = (bf16[2,128,16,128]{3,2,1,0:T(8,128)(2,1)}, bf16[2,128,16,128]{3,2,1,0:T(8,128)(2,1)S(1)}, u32[]{:S(2)}) copy-start(bf16[2,128,16,128]{3,2,1,0:T(8,128)(2,1)S(1)} %get-tuple-element.49) | copy-start | bytes 3145732
  20.7 1.4 %copy-start.1 = (f32[9,128]{1,0:T(8,128)S(1)}, f32[9,128]{1,0:T(8,128)}, u32[]{:S(2)}) copy-start(f32[9,128]{1,0:T(8,128)} %k_ref.2) | copy-start | bytes 13828
  21.3 7.8 %collective-permute-start.3 = (bf16[2,128,2,128]{3,2,0,1:T(2,128)(2,1)S(1)}, bf16[2,128,2,128]{3,2,0,1:T(2,128)(2,1)S(1)}, u32[]{:S(2)}, u32[]{:S(2)}) collective-permute-start(bf16[2,128,2,128]{3,2,0,1:T(2,128)(2,1)S(1)} %get-tuple-element.64), channel_id=1, source_target_pairs={{0,4},{4,8},{8,12},{12,16},{16,20},{20,24},{24,28},{28,0},{1,5},{5... | collective-permute-start | bytes 393224 | tf_op jit(solution)/shard_map/ppermute | solution.py:146
  22.1 7.2 %collective-permute-start.4 = (bf16[2,128,2,128]{3,2,0,1:T(2,128)(2,1)S(1)}, bf16[2,128,2,128]{3,2,0,1:T(2,128)(2,1)S(1)}, u32[]{:S(2)}, u32[]{:S(2)}) collective-permute-start(bf16[2,128,2,128]{3,2,0,1:T(2,128)(2,1)S(1)} %get-tuple-element.65), channel_id=1, source_target_pairs={{4,0},{8,4},{12,8},{16,12},{20,16},{24,20},{28,24},{0,28},{5,1},{9... | collective-permute-start | bytes 393224 | tf_op jit(solution)/shard_map/ppermute | solution.py:147
  31.5 3.8 %collective-permute-start.5 = (bf16[2,2,1,20,128]{4,3,0,1,2:T(8,128)(2,1)S(1)}, bf16[2,2,1,20,128]{4,3,0,1,2:T(8,128)(2,1)S(1)}, u32[]{:S(2)}, u32[]{:S(2)}) collective-permute-start(bf16[2,2,1,20,128]{4,3,0,1,2:T(8,128)(2,1)S(1)} %slice_select_fusion), channel_id=1, source_target_pairs={{0,2},{2,0},{1,3},{3,1},{4,6},{6,4},{5,7},{7,5},{8,10},{10,8},{9,1... | collective-permute-start | bytes 61448 | tf_op jit(solution)/shard_map/ppermute | solution.py:129
  36.2 2.5 %copy-start.8 = (bf16[2,128,16,128]{3,2,1,0:T(8,128)(2,1)S(1)}, bf16[2,128,16,128]{3,2,1,0:T(8,128)(2,1)}, u32[]{:S(2)}) copy-start(bf16[2,128,16,128]{3,2,1,0:T(8,128)(2,1)} %param.8) | copy-start | bytes 3145732
  36.3 2.5 %copy-start.10 = (bf16[128,128]{1,0:T(8,128)(2,1)S(1)}, bf16[128,128]{1,0:T(8,128)(2,1)}, u32[]{:S(2)}) copy-start(bf16[128,128]{1,0:T(8,128)(2,1)} %param.12) | copy-start | bytes 98308
  42.9 3.9 %collective-permute-start.6 = (bf16[2,2,1,20,128]{4,3,0,1,2:T(8,128)(2,1)S(1)}, bf16[2,2,1,20,128]{4,3,0,1,2:T(8,128)(2,1)S(1)}, u32[]{:S(2)}, u32[]{:S(2)}) collective-permute-start(bf16[2,2,1,20,128]{4,3,0,1,2:T(8,128)(2,1)S(1)} %get-tuple-element.53), channel_id=1, source_target_pairs={{0,2},{2,0},{1,3},{3,1},{4,6},{6,4},{5,7},{7,5},{8,10},{10,8},{9,1... | collective-permute-start | bytes 61448 | tf_op jit(solution)/shard_map/ppermute | solution.py:129
  46.8 5.8 %copy-start.4 = (bf16[2,128,20,128]{3,2,0,1:T(8,128)(2,1)S(1)}, bf16[2,128,20,128]{3,2,0,1:T(8,128)(2,1)}, u32[]{:S(2)}) copy-start(bf16[2,128,20,128]{3,2,0,1:T(8,128)(2,1)} %get-tuple-element.62) | copy-start | bytes 3932164
  47.4 7.7 %collective-permute-start.7 = (bf16[2,128,2,128]{3,2,0,1:T(2,128)(2,1)S(1)}, bf16[2,128,2,128]{3,2,0,1:T(2,128)(2,1)S(1)}, u32[]{:S(2)}, u32[]{:S(2)}) collective-permute-start(bf16[2,128,2,128]{3,2,0,1:T(2,128)(2,1)S(1)} %fusion.41), channel_id=1, source_target_pairs={{0,4},{4,8},{8,12},{12,16},{16,20},{20,24},{24,28},{28,0},{1,5},{5... | collective-permute-start | bytes 393224 | tf_op jit(solution)/shard_map/ppermute | solution.py:146
  47.6 7.5 %collective-permute-start.8 = (bf16[2,128,2,128]{3,2,0,1:T(2,128)(2,1)S(1)}, bf16[2,128,2,128]{3,2,0,1:T(2,128)(2,1)S(1)}, u32[]{:S(2)}, u32[]{:S(2)}) collective-permute-start(bf16[2,128,2,128]{3,2,0,1:T(2,128)(2,1)S(1)} %fusion.40), channel_id=1, source_target_pairs={{4,0},{8,4},{12,8},{16,12},{20,16},{24,20},{28,24},{0,28},{5,1},{9... | collective-permute-start | bytes 393224 | tf_op jit(solution)/shard_map/ppermute | solution.py:147
  53.2 2.9 %copy-start.9 = (bf16[2,128,16,128]{3,2,1,0:T(8,128)(2,1)S(1)}, bf16[2,128,16,128]{3,2,1,0:T(8,128)(2,1)}, u32[]{:S(2)}) copy-start(bf16[2,128,16,128]{3,2,1,0:T(8,128)(2,1)} %param.8) | copy-start | bytes 3145732
  56.1 1.2 %copy-start.6 = (bf16[2,128,16,128]{3,2,1,0:T(8,128)(2,1)S(1)}, bf16[2,128,16,128]{3,2,1,0:T(8,128)(2,1)}, u32[]{:S(2)}) copy-start(bf16[2,128,16,128]{3,2,1,0:T(8,128)(2,1)} %copy-done.5) | copy-start | bytes 3145732
  57.3 1.6 %copy-start.7 = (f32[2,128,16,128]{3,2,1,0:T(8,128)S(1)}, f32[2,128,16,128]{3,2,1,0:T(8,128)}, u32[]{:S(2)}) copy-start(f32[2,128,16,128]{3,2,1,0:T(8,128)} %get-tuple-element.50) | copy-start | bytes 6291460
  64.2 7.6 %collective-permute-start.12 = (f32[274,128]{1,0:T(8,128)S(1)}, f32[274,128]{1,0:T(8,128)S(1)}, u32[]{:S(2)}, u32[]{:S(2)}) collective-permute-start(f32[274,128]{1,0:T(8,128)S(1)} %pad_maximum_fusion.2), channel_id=1, source_target_pairs={{0,16},{1,17},{2,18},{3,19},{4,20},{5,21},{6,22},{7,23},{8,24},{9,... | collective-permute-start | bytes 420872 | tf_op jit(solution)/shard_map/ppermute | solution.py:109
  64.6 3.7 %collective-permute-start.9 = (bf16[2,1,1,18,128]{4,3,1,0,2:T(8,128)(2,1)S(1)}, bf16[2,1,1,18,128]{4,3,1,0,2:T(8,128)(2,1)S(1)}, u32[]{:S(2)}, u32[]{:S(2)}) collective-permute-start(bf16[2,1,1,18,128]{4,3,1,0,2:T(8,128)(2,1)S(1)} %bitcast_select_fusion), channel_id=1, source_target_pairs={{0,2},{2,0},{1,3},{3,1},{4,6},{6,4},{5,7},{7,5},{8,10},{10,8},{9,1... | collective-permute-start | bytes 27656 | tf_op jit(solution)/shard_map/ppermute | solution.py:129
  71.8 5.2 %collective-permute-start.13 = (f32[274,128]{1,0:T(8,128)S(1)}, f32[274,128]{1,0:T(8,128)S(1)}, u32[]{:S(2)}, u32[]{:S(2)}) collective-permute-start(f32[274,128]{1,0:T(8,128)S(1)} %fusion.63), channel_id=1, source_target_pairs={{0,8},{1,9},{2,10},{3,11},{4,12},{5,13},{6,14},{7,15},{8,0},{9,1},... | collective-permute-start | bytes 420872 | tf_op jit(solution)/shard_map/ppermute | solution.py:109
  77.0 6.9 %collective-permute-start.14 = (f32[274,128]{1,0:T(8,128)S(1)}, f32[274,128]{1,0:T(8,128)S(1)}, u32[]{:S(2)}, u32[]{:S(2)}) collective-permute-start(f32[274,128]{1,0:T(8,128)S(1)} %add.190), channel_id=1, source_target_pairs={{0,4},{1,5},{2,6},{3,7},{4,0},{5,1},{6,2},{7,3},{8,12},{9,13},{10,... | collective-permute-start | bytes 420872 | tf_op jit(solution)/shard_map/ppermute | solution.py:109
  78.9 7.0 %collective-permute-start.10 = (bf16[2,128,1,128]{3,0,1,2:T(2,128)(2,1)S(1)}, bf16[2,128,1,128]{3,0,1,2:T(2,128)(2,1)S(1)}, u32[]{:S(2)}, u32[]{:S(2)}) collective-permute-start(bf16[2,128,1,128]{3,0,1,2:T(2,128)(2,1)S(1)} %copy.132), channel_id=1, source_target_pairs={{0,4},{4,8},{8,12},{12,16},{16,20},{20,24},{24,28},{28,0},{1,5},{5... | collective-permute-start | bytes 196616 | tf_op jit(solution)/shard_map/ppermute | solution.py:146
  79.7 6.2 %collective-permute-start.11 = (bf16[2,128,1,128]{3,0,1,2:T(2,128)(2,1)S(1)}, bf16[2,128,1,128]{3,0,1,2:T(2,128)(2,1)S(1)}, u32[]{:S(2)}, u32[]{:S(2)}) collective-permute-start(bf16[2,128,1,128]{3,0,1,2:T(2,128)(2,1)S(1)} %copy.135), channel_id=1, source_target_pairs={{4,0},{8,4},{12,8},{16,12},{20,16},{24,20},{28,24},{0,28},{5,1},{9... | collective-permute-start | bytes 196616 | tf_op jit(solution)/shard_map/ppermute | solution.py:147
  83.8 5.2 %collective-permute-start.15 = (f32[274,128]{1,0:T(8,128)S(1)}, f32[274,128]{1,0:T(8,128)S(1)}, u32[]{:S(2)}, u32[]{:S(2)}) collective-permute-start(f32[274,128]{1,0:T(8,128)S(1)} %add.191), channel_id=1, source_target_pairs={{0,2},{1,3},{2,0},{3,1},{4,6},{5,7},{6,4},{7,5},{8,10},{9,11},{10,... | collective-permute-start | bytes 420872 | tf_op jit(solution)/shard_map/ppermute | solution.py:109
  89.0 1.8 %collective-permute-start.16 = (f32[274,128]{1,0:T(8,128)S(1)}, f32[274,128]{1,0:T(8,128)S(1)}, u32[]{:S(2)}, u32[]{:S(2)}) collective-permute-start(f32[274,128]{1,0:T(8,128)S(1)} %add.192), channel_id=1, source_target_pairs={{0,1},{1,0},{2,3},{3,2},{4,5},{5,4},{6,7},{7,6},{8,9},{9,8},{10,11... | collective-permute-start | bytes 420872 | tf_op jit(solution)/shard_map/ppermute | solution.py:109

commit v6 on v5

--- a/solution.py
+++ b/solution.py
@@ -75,7 +75,7 @@
     pad_rows = grad.shape[1] + 4 * margin
     pad_cols = -(-(grad.shape[2] + 4 * margin) // 8) * 8
     vmem = pl.BlockSpec(memory_space=pltpu.VMEM)
-    params = pltpu.CompilerParams(vmem_limit_bytes=48 * 1024 * 1024)
+    params = pltpu.CompilerParams(vmem_limit_bytes=16 * 1024 * 1024)
     grad_wide = pl.pallas_call(
         functools.partial(wide_grad_body, margin),
         out_shape=jax.ShapeDtypeStruct(wide.shape, jnp.float32),

time: 92.4 us -> 88.7 us (0.960)
  other arithmetic: 17.4 us -> 15.4 us
  local copies, waits for them, and re-layouts: 7.69 us -> 5.9 us
    unnamed x25 -> x15, local copies, waits for them, and re-layouts: 2.99 us -> 1.21 us
    concatenate x2, other arithmetic: 3.08 us -> 1.95 us  [extend(): jnp.concatenate([padded_rows[:, :margin], widened, padded_rows[:, 3 * mar...]
    convert_element_type x1, other arithmetic: 3.53 us -> 2.57 us  [shards(): act_one = jax.nn.silu(pre_one).astype(jnp.bfloat16)]
where the time goes in v6:
time: 88.7 us; the launch traced here: 88.5 us
  starting transfers between devices  31.3 us (35%)
  waiting for transfers between devices  22.4 us (25%)
  other arithmetic  15.4 us (17%)
  Pallas kernels  8.09 us (9%)
  local copies, waits for them, and re-layouts  5.9 us (7%)
  matrix products  2.98 us (3%)
  between operations  2.45 us (3%)
    ppermute x4, starting transfers between devices, with_halo(): after = lax.ppermute(first, axis, down)  16.4 us
    ppermute x5, waiting for transfers between devices, tree_sum(): value = value + lax.ppermute(value, axes, pairs)  11.1 us
    ppermute x4, waiting for transfers between devices, swap_halo(): got = lax.ppermute(sent, axis, [(0, 1), (1, 0)])  7.78 us
    ppermute x4, starting transfers between devices, swap_halo(): got = lax.ppermute(sent, axis, [(0, 1), (1, 0)])  6.58 us
    pallas_call x2, Pallas kernels, conv_back_kernel(): pl.pallas_call(functools.partial(wide_grad_body, margin), out_shape=jax.S...  4.91 us
    ppermute x4, starting transfers between devices, with_halo(): before = lax.ppermute(last, axis, up)  4.57 us
    ppermute x5, starting transfers between devices, tree_sum(): value = value + lax.ppermute(value, axes, pairs)  3.7 us
    ppermute x4, waiting for transfers between devices, with_halo(): before = lax.ppermute(last, axis, up)  3.5 us
  transfers between devices with their start and end apart: 17, of which 10 were waited for; matrix products, arithmetic and copies ran while one was open for 7% of the time, Pallas kernels for 2%

profile of v6, /device:TPU:0, one launch (start us, length us, event | category | flops | bytes accessed | tf_op | source)
XLA Modules:
  0.0 88.5 jit_solution(9202579943943980818)
XLA Ops:
  0.7 1.5 %fusion.59 = (bf16[2,128,1,1,128]{4,3,1,0,2:T(2,128)(2,1)S(1)}, bf16[2,128,1,1,128]{4,3,1,0,2:T(2,128)(2,1)S(1)}) fusion(bf16[2,128,1,16,128]{4,3,1,0,2:T(8,128)(2,1)} %bitcast.169), kind=kLoop, calls=%fused_computation.169 | loop fusion | bytes 262144 | tf_op jit(solution)/shard_map/slice | solution.py:169
  2.2 3.0 %collective-permute-start = (bf16[2,128,1,128]{3,1,0,2:T(8,128)(2,1)S(1)}, bf16[2,128,1,128]{3,1,0,2:T(8,128)(2,1)S(1)}, u32[]{:S(2)}, u32[]{:S(2)}) collective-permute-start(bf16[2,128,1,128]{3,1,0,2:T(8,128)(2,1)S(1)} %bitcast.181), channel_id=1, source_target_pairs={{0,4},{4,8},{8,12},{12,16},{16,20},{20,24},{24,28},{28,0},{1,5},{5... | collective-permute-start | bytes 196616 | tf_op jit(solution)/shard_map/ppermute | solution.py:146
  5.2 3.1 %collective-permute-start.1 = (bf16[2,128,1,128]{3,1,0,2:T(8,128)(2,1)S(1)}, bf16[2,128,1,128]{3,1,0,2:T(8,128)(2,1)S(1)}, u32[]{:S(2)}, u32[]{:S(2)}) collective-permute-start(bf16[2,128,1,128]{3,1,0,2:T(8,128)(2,1)S(1)} %bitcast.180), channel_id=1, source_target_pairs={{4,0},{8,4},{12,8},{16,12},{20,16},{24,20},{28,24},{0,28},{5,1},{9... | collective-permute-start | bytes 196616 | tf_op jit(solution)/shard_map/ppermute | solution.py:147
  8.3 1.3 %fusion.60 = (s32[1,1]{1,0:T(1,128)}, s32[1,1]{1,0:T(1,128)}) fusion(s32[2,8]{1,0:T(2,128)} %param.13, s32[]{:T(128)S(6)} %clamp.1, s32[]{:T(128)} %bitcast.3, s32[]{:T(128)} %bitcast.8), kind=kLoop, calls=%fused_computation.170 | loop fusion | bytes 28 | tf_op jit(solution)/shard_map/jit(_take)/gather | solution.py:159
  11.5 1.0 %fusion.54 = (bf16[2,128,18,128]{3,2,1,0:T(8,128)(2,1)S(1)}, bf16[2,128,1,18,128]{4,3,1,0,2:T(8,128)(2,1)S(1)}) fusion(bf16[2,128,1,1,128]{4,3,1,0,2:T(2,128)(2,1)S(1)} %copy.114, bf16[2,128,1,16,128]{4,3,1,0,2:T(8,128)(2,1)S(1)} %bitcast.170, bf16[2,128,1,1,128]{4,3,1,0,2:T(2,128)(2,1)S(1)} %copy.113), kind=kLoop, calls=%fused_computation.166 | loop fusion | flops 3538944 | bytes 3538944 | tf_op jit(solution)/shard_map/concatenate | solution.py:183
  12.5 1.7 %collective-permute-start.2 = (bf16[2,1,1,18,128]{4,3,1,0,2:T(8,128)(2,1)S(1)}, bf16[2,1,1,18,128]{4,3,1,0,2:T(8,128)(2,1)S(1)}, u32[]{:S(2)}, u32[]{:S(2)}) collective-permute-start(bf16[2,1,1,18,128]{4,3,1,0,2:T(8,128)(2,1)S(1)} %slice_select_fusion.1), channel_id=1, source_target_pairs={{0,2},{2,0},{1,3},{3,1},{4,6},{6,4},{5,7},{7,5},{8,10},{10,8},{9,1... | collective-permute-start | bytes 27656 | tf_op jit(solution)/shard_map/ppermute | solution.py:129
  14.2 2.0 %collective-permute-done.2 = bf16[2,1,1,18,128]{4,3,1,0,2:T(8,128)(2,1)S(1)} collective-permute-done((bf16[2,1,1,18,128]{4,3,1,0,2:T(8,128)(2,1)S(1)}, bf16[2,1,1,18,128]{4,3,1,0,2:T(8,128)(2,1)S(1)}, u32[]{:S(2)}, u32[]{:S(2)}) %collective-permute-start.2) | collective-permute-done | bytes 9248 | tf_op jit(solution)/shard_map/ppermute | solution.py:129
  16.2 0.9 maximum_convert_fusion.2
  17.1 2.6 %multiply_convert_fusion.1 = (bf16[2,128,16,128]{3,2,1,0:T(8,128)(2,1)S(1)}, f32[2,128,16,128]{3,2,1,0:T(8,128)S(1)}) fusion(f32[128]{0:T(128)S(1)} %get-tuple-element.105, f32[2,130,1,18,128]{4,3,1,0,2:T(8,128)S(1)} %maximum_convert_fusion.2, f32[128]{0:T(128)S(1)} %get-tuple-element.98, f32[128]{0:T(128)S(1)} %get-tuple-element.99, ...), kind=kLoop, calls=%fused_computation.59 | loop fusion | flops 11534336 | bytes 22024704 | tf_op jit(solution)/shard_map/convert_element_type | solution.py:289
  19.7 0.4 fusion.28
  20.4 0.8 collective-permute-start.3
  21.1 4.3 %collective-permute-start.4 = (bf16[2,128,2,128]{3,2,0,1:T(2,128)(2,1)S(1)}, bf16[2,128,2,128]{3,2,0,1:T(2,128)(2,1)S(1)}, u32[]{:S(2)}, u32[]{:S(2)}) collective-permute-start(bf16[2,128,2,128]{3,2,0,1:T(2,128)(2,1)S(1)} %get-tuple-element.65), channel_id=1, source_target_pairs={{4,0},{8,4},{12,8},{16,12},{20,16},{24,20},{28,24},{0,28},{5,1},{9... | collective-permute-start | bytes 393224 | tf_op jit(solution)/shard_map/ppermute | solution.py:147
  25.4 2.8 %collective-permute-done.3 = bf16[2,128,2,128]{3,2,0,1:T(2,128)(2,1)S(1)} collective-permute-done((bf16[2,128,2,128]{3,2,0,1:T(2,128)(2,1)S(1)}, bf16[2,128,2,128]{3,2,0,1:T(2,128)(2,1)S(1)}, u32[]{:S(2)}, u32[]{:S(2)}) %collective-permute-start.3) | collective-permute-done | bytes 131104 | tf_op jit(solution)/shard_map/ppermute | solution.py:146
  28.5 1.0 %fusion.53 = (bf16[2,128,20,128]{3,2,0,1:T(8,128)(2,1)S(1)}, bf16[2,128,1,20,128]{4,3,0,1,2:T(8,128)(2,1)S(1)}) fusion(bf16[2,128,1,2,128]{4,3,0,1,2:T(2,128)(2,1)S(1)} %fusion.37, bf16[2,128,1,16,128]{4,3,0,1,2:T(8,128)(2,1)S(1)} %fusion.28, bf16[2,128,1,2,128]{4,3,0,1,2:T(2,128)(2,1)S(1)} %fusion.36), kind=kLoop, calls=%fused_computation.165 | loop fusion | flops 3932160 | bytes 3932160 | tf_op jit(solution)/shard_map/concatenate | solution.py:183
  29.5 1.7 %collective-permute-start.5 = (bf16[2,2,1,20,128]{4,3,0,1,2:T(8,128)(2,1)S(1)}, bf16[2,2,1,20,128]{4,3,0,1,2:T(8,128)(2,1)S(1)}, u32[]{:S(2)}, u32[]{:S(2)}) collective-permute-start(bf16[2,2,1,20,128]{4,3,0,1,2:T(8,128)(2,1)S(1)} %slice_select_fusion), channel_id=1, source_target_pairs={{0,2},{2,0},{1,3},{3,1},{4,6},{6,4},{5,7},{7,5},{8,10},{10,8},{9,1... | collective-permute-start | bytes 61448 | tf_op jit(solution)/shard_map/ppermute | solution.py:129
  31.5 1.8 %collective-permute-done.5 = bf16[2,2,1,20,128]{4,3,0,1,2:T(8,128)(2,1)S(1)} collective-permute-done((bf16[2,2,1,20,128]{4,3,0,1,2:T(8,128)(2,1)S(1)}, bf16[2,2,1,20,128]{4,3,0,1,2:T(8,128)(2,1)S(1)}, u32[]{:S(2)}, u32[]{:S(2)}) %collective-permute-start.5) | collective-permute-done | bytes 20512 | tf_op jit(solution)/shard_map/ppermute | solution.py:129
  33.4 0.9 maximum_convert_fusion
  34.3 2.5 %multiply_convert_fusion = (bf16[2,128,16,128]{3,2,0,1:T(8,128)(2,1)S(1)}, f32[2,128,16,128]{3,2,0,1:T(8,128)S(1)}) fusion(f32[128]{0:T(128)S(1)} %get-tuple-element.96, f32[2,132,1,20,128]{4,3,0,1,2:T(8,128)S(1)} %maximum_convert_fusion, f32[128]{0:T(128)S(1)} %get-tuple-element.89, f32[128]{0:T(128)S(1)} %get-tuple-element.90, ...), kind=kLoop, calls=%fused_computation.54 | loop fusion | flops 11534336 | bytes 22024704 | tf_op jit(solution)/shard_map/convert_element_type | solution.py:293
  36.8 0.7 convolution_multiply_fusion
  37.4 0.7 copy_multiply_fusion.grad_ref
  38.1 2.5 %shard_map.110 = f32[2,132,20,128]{3,2,1,0:T(8,128)S(1)} custom-call(f32[2,128,16,128]{3,2,1,0:T(8,128)S(1)} %copy_multiply_fusion.grad_ref, f32[9,128]{1,0:T(8,128)S(1)} %copy-done.1), custom_call_target="tpu_custom_call" | custom-call | flops 12165120 | bytes 5406720 | tf_op jit(solution)/shard_map/pallas_call | solution.py:79
  40.9 1.7 %collective-permute-start.6 = (bf16[2,2,1,20,128]{4,3,0,1,2:T(8,128)(2,1)S(1)}, bf16[2,2,1,20,128]{4,3,0,1,2:T(8,128)(2,1)S(1)}, u32[]{:S(2)}, u32[]{:S(2)}) collective-permute-start(bf16[2,2,1,20,128]{4,3,0,1,2:T(8,128)(2,1)S(1)} %get-tuple-element.53), channel_id=1, source_target_pairs={{0,2},{2,0},{1,3},{3,1},{4,6},{6,4},{5,7},{7,5},{8,10},{10,8},{9,1... | collective-permute-start | bytes 61448 | tf_op jit(solution)/shard_map/ppermute | solution.py:129
  42.6 0.5 convolution_bitcast_fusion
  43.1 1.7 %collective-permute-done.6 = bf16[2,2,1,20,128]{4,3,0,1,2:T(8,128)(2,1)S(1)} collective-permute-done((bf16[2,2,1,20,128]{4,3,0,1,2:T(8,128)(2,1)S(1)}, bf16[2,2,1,20,128]{4,3,0,1,2:T(8,128)(2,1)S(1)}, u32[]{:S(2)}, u32[]{:S(2)}) %collective-permute-start.6) | collective-permute-done | bytes 20512 | tf_op jit(solution)/shard_map/ppermute | solution.py:129
  45.6 5.0 %collective-permute-start.8 = (bf16[2,128,2,128]{3,2,0,1:T(2,128)(2,1)S(1)}, bf16[2,128,2,128]{3,2,0,1:T(2,128)(2,1)S(1)}, u32[]{:S(2)}, u32[]{:S(2)}) collective-permute-start(bf16[2,128,2,128]{3,2,0,1:T(2,128)(2,1)S(1)} %fusion.40), channel_id=1, source_target_pairs={{4,0},{8,4},{12,8},{16,12},{20,16},{24,20},{28,24},{0,28},{5,1},{9... | collective-permute-start | bytes 393224 | tf_op jit(solution)/shard_map/ppermute | solution.py:147
  51.2 1.6 %shard_map.113 = f32[9,128]{1,0:T(8,128)S(1)} custom-call(f32[2,132,20,128]{3,2,1,0:T(8,128)S(1)} %copy.141.wide_ref, f32[2,128,16,128]{3,2,1,0:T(8,128)S(1)} %copy_multiply_fusion.grad_ref), custom_call_target="tpu_custom_call" | custom-call | flops 12165120 | bytes 5406720 | tf_op jit(solution)/shard_map/pallas_call | solution.py:88
  53.1 1.0 %convert_bitcast_fusion = (f32[2,128,1,2,128]{4,3,0,1,2:T(2,128)S(1)}, f32[2,128,1,2,128]{4,3,0,1,2:T(2,128)S(1)}) fusion(bf16[2,128,2,128]{3,2,0,1:T(2,128)(2,1)S(1)} %collective-permute-done.8, bf16[2,128,2,128]{3,2,0,1:T(2,128)(2,1)S(1)} %fusion.41, bf16[2,128,2,128]{3,2,0,1:T(2,128)(2,1)S(1)} %fusion.40, ...), kind=kLoop, calls=%fused_computation.80 | loop fusion | flops 1048576 | bytes 1048576 | tf_op jit(solution)/shard_map/broadcast_in_dim | solution.py:235
  54.1 0.6 fusion.9
  54.7 0.5 convolution_bitcast_fusion.1
  55.2 0.9 %add_multiply_fusion.grad_ref = f32[2,128,16,128]{3,2,1,0:T(8,128)S(1)} fusion(f32[2,128,16,128]{3,2,1,0:T(8,128)S(1)} %get-tuple-element.50, bf16[2,128,16,128]{3,2,0,1:T(8,128)(2,1)S(1)} %fusion.9, bf16[128,128]{1,0:T(8,128)(2,1)S(1)} %copy-done), kind=kOutput, calls=%fused_computation.55 | convolution fusion | flops 138412032 | bytes 5275648 | tf_op jit(solution)/shard_map/dot_general | solution.py:264
  56.2 2.4 %shard_map.111 = f32[2,130,18,128]{3,2,1,0:T(8,128)S(1)} custom-call(f32[2,128,16,128]{3,2,1,0:T(8,128)S(1)} %add_multiply_fusion.grad_ref, f32[9,128]{1,0:T(8,128)S(1)} %copy-done.2), custom_call_target="tpu_custom_call" | custom-call | flops 10782720 | bytes 4792320 | tf_op jit(solution)/shard_map/pallas_call | solution.py:79
  58.9 1.5 %shard_map.112 = f32[9,128]{1,0:T(8,128)S(1)} custom-call(f32[2,130,18,128]{3,2,1,0:T(8,128)S(1)} %maximum_convert_fusion.3.wide_ref, f32[2,128,16,128]{3,2,1,0:T(8,128)S(1)} %add_multiply_fusion.grad_ref), custom_call_target="tpu_custom_call" | custom-call | flops 10782720 | bytes 4792320 | tf_op jit(solution)/shard_map/pallas_call | solution.py:88
  60.5 0.4 collective-permute-start.12
  60.9 1.5 %collective-permute-start.9 = (bf16[2,1,1,18,128]{4,3,1,0,2:T(8,128)(2,1)S(1)}, bf16[2,1,1,18,128]{4,3,1,0,2:T(8,128)(2,1)S(1)}, u32[]{:S(2)}, u32[]{:S(2)}) collective-permute-start(bf16[2,1,1,18,128]{4,3,1,0,2:T(8,128)(2,1)S(1)} %bitcast_select_fusion), channel_id=1, source_target_pairs={{0,2},{2,0},{1,3},{3,1},{4,6},{6,4},{5,7},{7,5},{8,10},{10,8},{9,1... | collective-permute-start | bytes 27656 | tf_op jit(solution)/shard_map/ppermute | solution.py:129
  62.4 2.2 %collective-permute-done.9 = bf16[2,1,1,18,128]{4,3,1,0,2:T(8,128)(2,1)S(1)} collective-permute-done((bf16[2,1,1,18,128]{4,3,1,0,2:T(8,128)(2,1)S(1)}, bf16[2,1,1,18,128]{4,3,1,0,2:T(8,128)(2,1)S(1)}, u32[]{:S(2)}, u32[]{:S(2)}) %collective-permute-start.9) | collective-permute-done | bytes 9248 | tf_op jit(solution)/shard_map/ppermute | solution.py:129
  64.8 3.2 %collective-permute-done.12 = f32[274,128]{1,0:T(8,128)S(1)} collective-permute-done((f32[274,128]{1,0:T(8,128)S(1)}, f32[274,128]{1,0:T(8,128)S(1)}, u32[]{:S(2)}, u32[]{:S(2)}) %collective-permute-start.12) | collective-permute-done | bytes 140320 | tf_op jit(solution)/shard_map/ppermute | solution.py:109
  68.3 4.9 %collective-permute-done.13 = f32[274,128]{1,0:T(8,128)S(1)} collective-permute-done((f32[274,128]{1,0:T(8,128)S(1)}, f32[274,128]{1,0:T(8,128)S(1)}, u32[]{:S(2)}, u32[]{:S(2)}) %collective-permute-start.13) | collective-permute-done | bytes 140320 | tf_op jit(solution)/shard_map/ppermute | solution.py:109
  73.3 1.4 %collective-permute-start.14 = (f32[274,128]{1,0:T(8,128)S(1)}, f32[274,128]{1,0:T(8,128)S(1)}, u32[]{:S(2)}, u32[]{:S(2)}) collective-permute-start(f32[274,128]{1,0:T(8,128)S(1)} %add.190), channel_id=1, source_target_pairs={{0,4},{1,5},{2,6},{3,7},{4,0},{5,1},{6,2},{7,3},{8,12},{9,13},{10,... | collective-permute-start | bytes 420872 | tf_op jit(solution)/shard_map/ppermute | solution.py:109
  74.7 0.4 fusion.38
  75.2 0.7 collective-permute-start.10
  76.0 4.1 %collective-permute-start.11 = (bf16[2,128,1,128]{3,0,1,2:T(2,128)(2,1)S(1)}, bf16[2,128,1,128]{3,0,1,2:T(2,128)(2,1)S(1)}, u32[]{:S(2)}, u32[]{:S(2)}) collective-permute-start(bf16[2,128,1,128]{3,0,1,2:T(2,128)(2,1)S(1)} %copy.135), channel_id=1, source_target_pairs={{4,0},{8,4},{12,8},{16,12},{20,16},{24,20},{28,24},{0,28},{5,1},{9... | collective-permute-start | bytes 196616 | tf_op jit(solution)/shard_map/ppermute | solution.py:147
  80.1 1.7 %collective-permute-start.15 = (f32[274,128]{1,0:T(8,128)S(1)}, f32[274,128]{1,0:T(8,128)S(1)}, u32[]{:S(2)}, u32[]{:S(2)}) collective-permute-start(f32[274,128]{1,0:T(8,128)S(1)} %add.191), channel_id=1, source_target_pairs={{0,2},{1,3},{2,0},{3,1},{4,6},{5,7},{6,4},{7,5},{8,10},{9,11},{10,... | collective-permute-start | bytes 420872 | tf_op jit(solution)/shard_map/ppermute | solution.py:109
  81.8 0.4 collective-permute-done.10
  82.4 2.9 %collective-permute-done.15 = f32[274,128]{1,0:T(8,128)S(1)} collective-permute-done((f32[274,128]{1,0:T(8,128)S(1)}, f32[274,128]{1,0:T(8,128)S(1)}, u32[]{:S(2)}, u32[]{:S(2)}) %collective-permute-start.15) | collective-permute-done | bytes 140320 | tf_op jit(solution)/shard_map/ppermute | solution.py:109
  85.4 0.6 fusion.5
  86.0 1.2 %copy.143 = bf16[2,128,16,128]{3,2,1,0:T(8,128)(2,1)} copy(bf16[2,128,16,128]{3,2,0,1:T(8,128)(2,1)S(1)} %fusion.5) | data formatting | bytes 2097152
  87.2 0.7 slice_multiply_fusion.18
  87.9 0.6 slice_multiply_fusion.20
  (71 shorter events, 4.5 us)
Async XLA Ops:
  0.6 19.1 %copy-start = (bf16[128,128]{1,0:T(8,128)(2,1)S(1)}, bf16[128,128]{1,0:T(8,128)(2,1)}, u32[]{:S(2)}) copy-start(bf16[128,128]{1,0:T(8,128)(2,1)} %param.10) | copy-start | bytes 98308
  0.6 10.8 %copy-start.3 = (bf16[2,128,16,128]{3,2,1,0:T(8,128)(2,1)S(1)}, bf16[2,128,16,128]{3,2,1,0:T(8,128)(2,1)}, u32[]{:S(2)}) copy-start(bf16[2,128,16,128]{3,2,1,0:T(8,128)(2,1)} %param.7) | copy-start | bytes 3145732
  2.2 8.8 %collective-permute-start = (bf16[2,128,1,128]{3,1,0,2:T(8,128)(2,1)S(1)}, bf16[2,128,1,128]{3,1,0,2:T(8,128)(2,1)S(1)}, u32[]{:S(2)}, u32[]{:S(2)}) collective-permute-start(bf16[2,128,1,128]{3,1,0,2:T(8,128)(2,1)S(1)} %bitcast.181), channel_id=1, source_target_pairs={{0,4},{4,8},{8,12},{12,16},{16,20},{20,24},{24,28},{28,0},{1,5},{5... | collective-permute-start | bytes 196616 | tf_op jit(solution)/shard_map/ppermute | solution.py:146
  5.2 6.0 %collective-permute-start.1 = (bf16[2,128,1,128]{3,1,0,2:T(8,128)(2,1)S(1)}, bf16[2,128,1,128]{3,1,0,2:T(8,128)(2,1)S(1)}, u32[]{:S(2)}, u32[]{:S(2)}) collective-permute-start(bf16[2,128,1,128]{3,1,0,2:T(8,128)(2,1)S(1)} %bitcast.180), channel_id=1, source_target_pairs={{4,0},{8,4},{12,8},{16,12},{20,16},{24,20},{28,24},{0,28},{5,1},{9... | collective-permute-start | bytes 196616 | tf_op jit(solution)/shard_map/ppermute | solution.py:147
  11.5 2.7 %copy-start.2 = (f32[9,128]{1,0:T(8,128)S(1)}, f32[9,128]{1,0:T(8,128)}, u32[]{:S(2)}) copy-start(f32[9,128]{1,0:T(8,128)} %k_ref.3) | copy-start | bytes 13828
  12.5 3.8 %collective-permute-start.2 = (bf16[2,1,1,18,128]{4,3,1,0,2:T(8,128)(2,1)S(1)}, bf16[2,1,1,18,128]{4,3,1,0,2:T(8,128)(2,1)S(1)}, u32[]{:S(2)}, u32[]{:S(2)}) collective-permute-start(bf16[2,1,1,18,128]{4,3,1,0,2:T(8,128)(2,1)S(1)} %slice_select_fusion.1), channel_id=1, source_target_pairs={{0,2},{2,0},{1,3},{3,1},{4,6},{6,4},{5,7},{7,5},{8,10},{10,8},{9,1... | collective-permute-start | bytes 27656 | tf_op jit(solution)/shard_map/ppermute | solution.py:129
  19.7 1.4 %copy-start.1 = (f32[9,128]{1,0:T(8,128)S(1)}, f32[9,128]{1,0:T(8,128)}, u32[]{:S(2)}) copy-start(f32[9,128]{1,0:T(8,128)} %k_ref.2) | copy-start | bytes 13828
  20.4 7.8 %collective-permute-start.3 = (bf16[2,128,2,128]{3,2,0,1:T(2,128)(2,1)S(1)}, bf16[2,128,2,128]{3,2,0,1:T(2,128)(2,1)S(1)}, u32[]{:S(2)}, u32[]{:S(2)}) collective-permute-start(bf16[2,128,2,128]{3,2,0,1:T(2,128)(2,1)S(1)} %get-tuple-element.64), channel_id=1, source_target_pairs={{0,4},{4,8},{8,12},{12,16},{16,20},{20,24},{24,28},{28,0},{1,5},{5... | collective-permute-start | bytes 393224 | tf_op jit(solution)/shard_map/ppermute | solution.py:146
  21.1 7.2 %collective-permute-start.4 = (bf16[2,128,2,128]{3,2,0,1:T(2,128)(2,1)S(1)}, bf16[2,128,2,128]{3,2,0,1:T(2,128)(2,1)S(1)}, u32[]{:S(2)}, u32[]{:S(2)}) collective-permute-start(bf16[2,128,2,128]{3,2,0,1:T(2,128)(2,1)S(1)} %get-tuple-element.65), channel_id=1, source_target_pairs={{4,0},{8,4},{12,8},{16,12},{20,16},{24,20},{28,24},{0,28},{5,1},{9... | collective-permute-start | bytes 393224 | tf_op jit(solution)/shard_map/ppermute | solution.py:147
  29.5 3.9 %collective-permute-start.5 = (bf16[2,2,1,20,128]{4,3,0,1,2:T(8,128)(2,1)S(1)}, bf16[2,2,1,20,128]{4,3,0,1,2:T(8,128)(2,1)S(1)}, u32[]{:S(2)}, u32[]{:S(2)}) collective-permute-start(bf16[2,2,1,20,128]{4,3,0,1,2:T(8,128)(2,1)S(1)} %slice_select_fusion), channel_id=1, source_target_pairs={{0,2},{2,0},{1,3},{3,1},{4,6},{6,4},{5,7},{7,5},{8,10},{10,8},{9,1... | collective-permute-start | bytes 61448 | tf_op jit(solution)/shard_map/ppermute | solution.py:129
  34.2 2.5 %copy-start.4 = (bf16[2,128,16,128]{3,2,1,0:T(8,128)(2,1)S(1)}, bf16[2,128,16,128]{3,2,1,0:T(8,128)(2,1)}, u32[]{:S(2)}) copy-start(bf16[2,128,16,128]{3,2,1,0:T(8,128)(2,1)} %param.8) | copy-start | bytes 3145732
  34.3 2.5 %copy-start.5 = (bf16[128,128]{1,0:T(8,128)(2,1)S(1)}, bf16[128,128]{1,0:T(8,128)(2,1)}, u32[]{:S(2)}) copy-start(bf16[128,128]{1,0:T(8,128)(2,1)} %param.12) | copy-start | bytes 98308
  40.9 3.9 %collective-permute-start.6 = (bf16[2,2,1,20,128]{4,3,0,1,2:T(8,128)(2,1)S(1)}, bf16[2,2,1,20,128]{4,3,0,1,2:T(8,128)(2,1)S(1)}, u32[]{:S(2)}, u32[]{:S(2)}) collective-permute-start(bf16[2,2,1,20,128]{4,3,0,1,2:T(8,128)(2,1)S(1)} %get-tuple-element.53), channel_id=1, source_target_pairs={{0,2},{2,0},{1,3},{3,1},{4,6},{6,4},{5,7},{7,5},{8,10},{10,8},{9,1... | collective-permute-start | bytes 61448 | tf_op jit(solution)/shard_map/ppermute | solution.py:129
  45.4 7.7 %collective-permute-start.7 = (bf16[2,128,2,128]{3,2,0,1:T(2,128)(2,1)S(1)}, bf16[2,128,2,128]{3,2,0,1:T(2,128)(2,1)S(1)}, u32[]{:S(2)}, u32[]{:S(2)}) collective-permute-start(bf16[2,128,2,128]{3,2,0,1:T(2,128)(2,1)S(1)} %fusion.41), channel_id=1, source_target_pairs={{0,4},{4,8},{8,12},{12,16},{16,20},{20,24},{24,28},{28,0},{1,5},{5... | collective-permute-start | bytes 393224 | tf_op jit(solution)/shard_map/ppermute | solution.py:146
  45.6 7.5 %collective-permute-start.8 = (bf16[2,128,2,128]{3,2,0,1:T(2,128)(2,1)S(1)}, bf16[2,128,2,128]{3,2,0,1:T(2,128)(2,1)S(1)}, u32[]{:S(2)}, u32[]{:S(2)}) collective-permute-start(bf16[2,128,2,128]{3,2,0,1:T(2,128)(2,1)S(1)} %fusion.40), channel_id=1, source_target_pairs={{4,0},{8,4},{12,8},{16,12},{20,16},{24,20},{28,24},{0,28},{5,1},{9... | collective-permute-start | bytes 393224 | tf_op jit(solution)/shard_map/ppermute | solution.py:147
  60.5 7.6 %collective-permute-start.12 = (f32[274,128]{1,0:T(8,128)S(1)}, f32[274,128]{1,0:T(8,128)S(1)}, u32[]{:S(2)}, u32[]{:S(2)}) collective-permute-start(f32[274,128]{1,0:T(8,128)S(1)} %pad_maximum_fusion.2), channel_id=1, source_target_pairs={{0,16},{1,17},{2,18},{3,19},{4,20},{5,21},{6,22},{7,23},{8,24},{9,... | collective-permute-start | bytes 420872 | tf_op jit(solution)/shard_map/ppermute | solution.py:109
  60.9 3.7 %collective-permute-start.9 = (bf16[2,1,1,18,128]{4,3,1,0,2:T(8,128)(2,1)S(1)}, bf16[2,1,1,18,128]{4,3,1,0,2:T(8,128)(2,1)S(1)}, u32[]{:S(2)}, u32[]{:S(2)}) collective-permute-start(bf16[2,1,1,18,128]{4,3,1,0,2:T(8,128)(2,1)S(1)} %bitcast_select_fusion), channel_id=1, source_target_pairs={{0,2},{2,0},{1,3},{3,1},{4,6},{6,4},{5,7},{7,5},{8,10},{10,8},{9,1... | collective-permute-start | bytes 27656 | tf_op jit(solution)/shard_map/ppermute | solution.py:129
  68.1 5.2 %collective-permute-start.13 = (f32[274,128]{1,0:T(8,128)S(1)}, f32[274,128]{1,0:T(8,128)S(1)}, u32[]{:S(2)}, u32[]{:S(2)}) collective-permute-start(f32[274,128]{1,0:T(8,128)S(1)} %fusion.63), channel_id=1, source_target_pairs={{0,8},{1,9},{2,10},{3,11},{4,12},{5,13},{6,14},{7,15},{8,0},{9,1},... | collective-permute-start | bytes 420872 | tf_op jit(solution)/shard_map/ppermute | solution.py:109
  73.3 6.8 %collective-permute-start.14 = (f32[274,128]{1,0:T(8,128)S(1)}, f32[274,128]{1,0:T(8,128)S(1)}, u32[]{:S(2)}, u32[]{:S(2)}) collective-permute-start(f32[274,128]{1,0:T(8,128)S(1)} %add.190), channel_id=1, source_target_pairs={{0,4},{1,5},{2,6},{3,7},{4,0},{5,1},{6,2},{7,3},{8,12},{9,13},{10,... | collective-permute-start | bytes 420872 | tf_op jit(solution)/shard_map/ppermute | solution.py:109
  75.2 7.0 %collective-permute-start.10 = (bf16[2,128,1,128]{3,0,1,2:T(2,128)(2,1)S(1)}, bf16[2,128,1,128]{3,0,1,2:T(2,128)(2,1)S(1)}, u32[]{:S(2)}, u32[]{:S(2)}) collective-permute-start(bf16[2,128,1,128]{3,0,1,2:T(2,128)(2,1)S(1)} %copy.132), channel_id=1, source_target_pairs={{0,4},{4,8},{8,12},{12,16},{16,20},{20,24},{24,28},{28,0},{1,5},{5... | collective-permute-start | bytes 196616 | tf_op jit(solution)/shard_map/ppermute | solution.py:146
  76.0 6.2 %collective-permute-start.11 = (bf16[2,128,1,128]{3,0,1,2:T(2,128)(2,1)S(1)}, bf16[2,128,1,128]{3,0,1,2:T(2,128)(2,1)S(1)}, u32[]{:S(2)}, u32[]{:S(2)}) collective-permute-start(bf16[2,128,1,128]{3,0,1,2:T(2,128)(2,1)S(1)} %copy.135), channel_id=1, source_target_pairs={{4,0},{8,4},{12,8},{16,12},{20,16},{24,20},{28,24},{0,28},{5,1},{9... | collective-permute-start | bytes 196616 | tf_op jit(solution)/shard_map/ppermute | solution.py:147
  80.1 5.2 %collective-permute-start.15 = (f32[274,128]{1,0:T(8,128)S(1)}, f32[274,128]{1,0:T(8,128)S(1)}, u32[]{:S(2)}, u32[]{:S(2)}) collective-permute-start(f32[274,128]{1,0:T(8,128)S(1)} %add.191), channel_id=1, source_target_pairs={{0,2},{1,3},{2,0},{3,1},{4,6},{5,7},{6,4},{7,5},{8,10},{9,11},{10,... | collective-permute-start | bytes 420872 | tf_op jit(solution)/shard_map/ppermute | solution.py:109
  85.3 1.9 %collective-permute-start.16 = (f32[274,128]{1,0:T(8,128)S(1)}, f32[274,128]{1,0:T(8,128)S(1)}, u32[]{:S(2)}, u32[]{:S(2)}) collective-permute-start(f32[274,128]{1,0:T(8,128)S(1)} %add.192), channel_id=1, source_target_pairs={{0,1},{1,0},{2,3},{3,2},{4,5},{5,4},{6,7},{7,6},{8,9},{9,8},{10,11... | collective-permute-start | bytes 420872 | tf_op jit(solution)/shard_map/ppermute | solution.py:109

commit v7 on v6

--- a/solution.py
+++ b/solution.py
@@ -7,7 +7,7 @@
 import functools
 
 COL_DEV = 16
-ROW_BLOCK = 8
+ROW_BLOCK = 16
 
 
 def tap_sum_body(margin, wide_ref, grad_ref, dk_ref):
@@ -75,7 +75,7 @@
     pad_rows = grad.shape[1] + 4 * margin
     pad_cols = -(-(grad.shape[2] + 4 * margin) // 8) * 8
     vmem = pl.BlockSpec(memory_space=pltpu.VMEM)
-    params = pltpu.CompilerParams(vmem_limit_bytes=16 * 1024 * 1024)
+    params = pltpu.CompilerParams(vmem_limit_bytes=4 * 1024 * 1024)
     grad_wide = pl.pallas_call(
         functools.partial(wide_grad_body, margin),
         out_shape=jax.ShapeDtypeStruct(wide.shape, jnp.float32),

time: 88.7 us -> 88.4 us (level)
  no operation moved by 1% of the time
where the time goes in v7:
time: 88.4 us; the launch traced here: 88.1 us
  starting transfers between devices  31.3 us (35%)
  waiting for transfers between devices  22.3 us (25%)
  other arithmetic  15.4 us (17%)
  Pallas kernels  7.81 us (9%)
  local copies, waits for them, and re-layouts  5.9 us (7%)
  matrix products  2.98 us (3%)
  between operations  2.45 us (3%)
    ppermute x4, starting transfers between devices, with_halo(): after = lax.ppermute(first, axis, down)  16.4 us
    ppermute x5, waiting for transfers between devices, tree_sum(): value = value + lax.ppermute(value, axes, pairs)  11.1 us
    ppermute x4, waiting for transfers between devices, swap_halo(): got = lax.ppermute(sent, axis, [(0, 1), (1, 0)])  7.78 us
    ppermute x4, starting transfers between devices, swap_halo(): got = lax.ppermute(sent, axis, [(0, 1), (1, 0)])  6.59 us
    ppermute x4, starting transfers between devices, with_halo(): before = lax.ppermute(last, axis, up)  4.58 us
    pallas_call x2, Pallas kernels, conv_back_kernel(): pl.pallas_call(functools.partial(wide_grad_body, margin), out_shape=jax.S...  4.55 us
    ppermute x5, starting transfers between devices, tree_sum(): value = value + lax.ppermute(value, axes, pairs)  3.69 us
    ppermute x4, waiting for transfers between devices, with_halo(): before = lax.ppermute(last, axis, up)  3.45 us
  transfers between devices with their start and end apart: 17, of which 10 were waited for; matrix products, arithmetic and copies ran while one was open for 7% of the time, Pallas kernels for 2%

profile of v7, /device:TPU:0, one launch (start us, length us, event | category | flops | bytes accessed | tf_op | source)
XLA Modules:
  0.0 88.1 jit_solution(16840471863987013652)
XLA Ops:
  0.7 1.5 %fusion.59 = (bf16[2,128,1,1,128]{4,3,1,0,2:T(2,128)(2,1)S(1)}, bf16[2,128,1,1,128]{4,3,1,0,2:T(2,128)(2,1)S(1)}) fusion(bf16[2,128,1,16,128]{4,3,1,0,2:T(8,128)(2,1)} %bitcast.169), kind=kLoop, calls=%fused_computation.169 | loop fusion | bytes 262144 | tf_op jit(solution)/shard_map/slice | solution.py:169
  2.2 3.0 %collective-permute-start = (bf16[2,128,1,128]{3,1,0,2:T(8,128)(2,1)S(1)}, bf16[2,128,1,128]{3,1,0,2:T(8,128)(2,1)S(1)}, u32[]{:S(2)}, u32[]{:S(2)}) collective-permute-start(bf16[2,128,1,128]{3,1,0,2:T(8,128)(2,1)S(1)} %bitcast.181), channel_id=1, source_target_pairs={{0,4},{4,8},{8,12},{12,16},{16,20},{20,24},{24,28},{28,0},{1,5},{5... | collective-permute-start | bytes 196616 | tf_op jit(solution)/shard_map/ppermute | solution.py:146
  5.2 3.1 %collective-permute-start.1 = (bf16[2,128,1,128]{3,1,0,2:T(8,128)(2,1)S(1)}, bf16[2,128,1,128]{3,1,0,2:T(8,128)(2,1)S(1)}, u32[]{:S(2)}, u32[]{:S(2)}) collective-permute-start(bf16[2,128,1,128]{3,1,0,2:T(8,128)(2,1)S(1)} %bitcast.180), channel_id=1, source_target_pairs={{4,0},{8,4},{12,8},{16,12},{20,16},{24,20},{28,24},{0,28},{5,1},{9... | collective-permute-start | bytes 196616 | tf_op jit(solution)/shard_map/ppermute | solution.py:147
  8.3 1.3 %fusion.60 = (s32[1,1]{1,0:T(1,128)}, s32[1,1]{1,0:T(1,128)}) fusion(s32[2,8]{1,0:T(2,128)} %param.13, s32[]{:T(128)S(6)} %clamp.1, s32[]{:T(128)} %bitcast.3, s32[]{:T(128)} %bitcast.8), kind=kLoop, calls=%fused_computation.170 | loop fusion | bytes 28 | tf_op jit(solution)/shard_map/jit(_take)/gather | solution.py:159
  11.5 1.0 %fusion.54 = (bf16[2,128,18,128]{3,2,1,0:T(8,128)(2,1)S(1)}, bf16[2,128,1,18,128]{4,3,1,0,2:T(8,128)(2,1)S(1)}) fusion(bf16[2,128,1,1,128]{4,3,1,0,2:T(2,128)(2,1)S(1)} %copy.114, bf16[2,128,1,16,128]{4,3,1,0,2:T(8,128)(2,1)S(1)} %bitcast.170, bf16[2,128,1,1,128]{4,3,1,0,2:T(2,128)(2,1)S(1)} %copy.113), kind=kLoop, calls=%fused_computation.166 | loop fusion | flops 3538944 | bytes 3538944 | tf_op jit(solution)/shard_map/concatenate | solution.py:183
  12.5 1.7 %collective-permute-start.2 = (bf16[2,1,1,18,128]{4,3,1,0,2:T(8,128)(2,1)S(1)}, bf16[2,1,1,18,128]{4,3,1,0,2:T(8,128)(2,1)S(1)}, u32[]{:S(2)}, u32[]{:S(2)}) collective-permute-start(bf16[2,1,1,18,128]{4,3,1,0,2:T(8,128)(2,1)S(1)} %slice_select_fusion.1), channel_id=1, source_target_pairs={{0,2},{2,0},{1,3},{3,1},{4,6},{6,4},{5,7},{7,5},{8,10},{10,8},{9,1... | collective-permute-start | bytes 27656 | tf_op jit(solution)/shard_map/ppermute | solution.py:129
  14.2 2.0 %collective-permute-done.2 = bf16[2,1,1,18,128]{4,3,1,0,2:T(8,128)(2,1)S(1)} collective-permute-done((bf16[2,1,1,18,128]{4,3,1,0,2:T(8,128)(2,1)S(1)}, bf16[2,1,1,18,128]{4,3,1,0,2:T(8,128)(2,1)S(1)}, u32[]{:S(2)}, u32[]{:S(2)}) %collective-permute-start.2) | collective-permute-done | bytes 9248 | tf_op jit(solution)/shard_map/ppermute | solution.py:129
  16.2 0.9 maximum_convert_fusion.2
  17.1 2.6 %multiply_convert_fusion.1 = (bf16[2,128,16,128]{3,2,1,0:T(8,128)(2,1)S(1)}, f32[2,128,16,128]{3,2,1,0:T(8,128)S(1)}) fusion(f32[128]{0:T(128)S(1)} %get-tuple-element.105, f32[2,130,1,18,128]{4,3,1,0,2:T(8,128)S(1)} %maximum_convert_fusion.2, f32[128]{0:T(128)S(1)} %get-tuple-element.98, f32[128]{0:T(128)S(1)} %get-tuple-element.99, ...), kind=kLoop, calls=%fused_computation.59 | loop fusion | flops 11534336 | bytes 22024704 | tf_op jit(solution)/shard_map/convert_element_type | solution.py:289
  19.7 0.4 fusion.28
  20.4 0.8 collective-permute-start.3
  21.1 4.3 %collective-permute-start.4 = (bf16[2,128,2,128]{3,2,0,1:T(2,128)(2,1)S(1)}, bf16[2,128,2,128]{3,2,0,1:T(2,128)(2,1)S(1)}, u32[]{:S(2)}, u32[]{:S(2)}) collective-permute-start(bf16[2,128,2,128]{3,2,0,1:T(2,128)(2,1)S(1)} %get-tuple-element.65), channel_id=1, source_target_pairs={{4,0},{8,4},{12,8},{16,12},{20,16},{24,20},{28,24},{0,28},{5,1},{9... | collective-permute-start | bytes 393224 | tf_op jit(solution)/shard_map/ppermute | solution.py:147
  25.4 2.8 %collective-permute-done.3 = bf16[2,128,2,128]{3,2,0,1:T(2,128)(2,1)S(1)} collective-permute-done((bf16[2,128,2,128]{3,2,0,1:T(2,128)(2,1)S(1)}, bf16[2,128,2,128]{3,2,0,1:T(2,128)(2,1)S(1)}, u32[]{:S(2)}, u32[]{:S(2)}) %collective-permute-start.3) | collective-permute-done | bytes 131104 | tf_op jit(solution)/shard_map/ppermute | solution.py:146
  28.5 1.0 %fusion.53 = (bf16[2,128,20,128]{3,2,0,1:T(8,128)(2,1)S(1)}, bf16[2,128,1,20,128]{4,3,0,1,2:T(8,128)(2,1)S(1)}) fusion(bf16[2,128,1,2,128]{4,3,0,1,2:T(2,128)(2,1)S(1)} %fusion.37, bf16[2,128,1,16,128]{4,3,0,1,2:T(8,128)(2,1)S(1)} %fusion.28, bf16[2,128,1,2,128]{4,3,0,1,2:T(2,128)(2,1)S(1)} %fusion.36), kind=kLoop, calls=%fused_computation.165 | loop fusion | flops 3932160 | bytes 3932160 | tf_op jit(solution)/shard_map/concatenate | solution.py:183
  29.5 1.7 %collective-permute-start.5 = (bf16[2,2,1,20,128]{4,3,0,1,2:T(8,128)(2,1)S(1)}, bf16[2,2,1,20,128]{4,3,0,1,2:T(8,128)(2,1)S(1)}, u32[]{:S(2)}, u32[]{:S(2)}) collective-permute-start(bf16[2,2,1,20,128]{4,3,0,1,2:T(8,128)(2,1)S(1)} %slice_select_fusion), channel_id=1, source_target_pairs={{0,2},{2,0},{1,3},{3,1},{4,6},{6,4},{5,7},{7,5},{8,10},{10,8},{9,1... | collective-permute-start | bytes 61448 | tf_op jit(solution)/shard_map/ppermute | solution.py:129
  31.5 1.8 %collective-permute-done.5 = bf16[2,2,1,20,128]{4,3,0,1,2:T(8,128)(2,1)S(1)} collective-permute-done((bf16[2,2,1,20,128]{4,3,0,1,2:T(8,128)(2,1)S(1)}, bf16[2,2,1,20,128]{4,3,0,1,2:T(8,128)(2,1)S(1)}, u32[]{:S(2)}, u32[]{:S(2)}) %collective-permute-start.5) | collective-permute-done | bytes 20512 | tf_op jit(solution)/shard_map/ppermute | solution.py:129
  33.4 0.9 maximum_convert_fusion
  34.3 2.5 %multiply_convert_fusion = (bf16[2,128,16,128]{3,2,0,1:T(8,128)(2,1)S(1)}, f32[2,128,16,128]{3,2,0,1:T(8,128)S(1)}) fusion(f32[128]{0:T(128)S(1)} %get-tuple-element.96, f32[2,132,1,20,128]{4,3,0,1,2:T(8,128)S(1)} %maximum_convert_fusion, f32[128]{0:T(128)S(1)} %get-tuple-element.89, f32[128]{0:T(128)S(1)} %get-tuple-element.90, ...), kind=kLoop, calls=%fused_computation.54 | loop fusion | flops 11534336 | bytes 22024704 | tf_op jit(solution)/shard_map/convert_element_type | solution.py:293
  36.8 0.7 convolution_multiply_fusion
  37.4 0.7 copy_multiply_fusion.grad_ref
  38.1 2.3 %shard_map.110 = f32[2,132,20,128]{3,2,1,0:T(8,128)S(1)} custom-call(f32[2,128,16,128]{3,2,1,0:T(8,128)S(1)} %copy_multiply_fusion.grad_ref, f32[9,128]{1,0:T(8,128)S(1)} %copy-done.1), custom_call_target="tpu_custom_call" | custom-call | flops 12165120 | bytes 5406720 | tf_op jit(solution)/shard_map/pallas_call | solution.py:79
  40.7 1.7 %collective-permute-start.6 = (bf16[2,2,1,20,128]{4,3,0,1,2:T(8,128)(2,1)S(1)}, bf16[2,2,1,20,128]{4,3,0,1,2:T(8,128)(2,1)S(1)}, u32[]{:S(2)}, u32[]{:S(2)}) collective-permute-start(bf16[2,2,1,20,128]{4,3,0,1,2:T(8,128)(2,1)S(1)} %get-tuple-element.53), channel_id=1, source_target_pairs={{0,2},{2,0},{1,3},{3,1},{4,6},{6,4},{5,7},{7,5},{8,10},{10,8},{9,1... | collective-permute-start | bytes 61448 | tf_op jit(solution)/shard_map/ppermute | solution.py:129
  42.4 0.5 convolution_bitcast_fusion
  42.9 1.7 %collective-permute-done.6 = bf16[2,2,1,20,128]{4,3,0,1,2:T(8,128)(2,1)S(1)} collective-permute-done((bf16[2,2,1,20,128]{4,3,0,1,2:T(8,128)(2,1)S(1)}, bf16[2,2,1,20,128]{4,3,0,1,2:T(8,128)(2,1)S(1)}, u32[]{:S(2)}, u32[]{:S(2)}) %collective-permute-start.6) | collective-permute-done | bytes 20512 | tf_op jit(solution)/shard_map/ppermute | solution.py:129
  45.4 5.0 %collective-permute-start.8 = (bf16[2,128,2,128]{3,2,0,1:T(2,128)(2,1)S(1)}, bf16[2,128,2,128]{3,2,0,1:T(2,128)(2,1)S(1)}, u32[]{:S(2)}, u32[]{:S(2)}) collective-permute-start(bf16[2,128,2,128]{3,2,0,1:T(2,128)(2,1)S(1)} %fusion.40), channel_id=1, source_target_pairs={{4,0},{8,4},{12,8},{16,12},{20,16},{24,20},{28,24},{0,28},{5,1},{9... | collective-permute-start | bytes 393224 | tf_op jit(solution)/shard_map/ppermute | solution.py:147
  51.0 1.7 %shard_map.113 = f32[9,128]{1,0:T(8,128)S(1)} custom-call(f32[2,132,20,128]{3,2,1,0:T(8,128)S(1)} %copy.141.wide_ref, f32[2,128,16,128]{3,2,1,0:T(8,128)S(1)} %copy_multiply_fusion.grad_ref), custom_call_target="tpu_custom_call" | custom-call | flops 12165120 | bytes 5406720 | tf_op jit(solution)/shard_map/pallas_call | solution.py:88
  52.9 1.0 %convert_bitcast_fusion = (f32[2,128,1,2,128]{4,3,0,1,2:T(2,128)S(1)}, f32[2,128,1,2,128]{4,3,0,1,2:T(2,128)S(1)}) fusion(bf16[2,128,2,128]{3,2,0,1:T(2,128)(2,1)S(1)} %collective-permute-done.8, bf16[2,128,2,128]{3,2,0,1:T(2,128)(2,1)S(1)} %fusion.41, bf16[2,128,2,128]{3,2,0,1:T(2,128)(2,1)S(1)} %fusion.40, ...), kind=kLoop, calls=%fused_computation.80 | loop fusion | flops 1048576 | bytes 1048576 | tf_op jit(solution)/shard_map/broadcast_in_dim | solution.py:235
  53.9 0.6 fusion.9
  54.6 0.5 convolution_bitcast_fusion.1
  55.1 0.9 %add_multiply_fusion.grad_ref = f32[2,128,16,128]{3,2,1,0:T(8,128)S(1)} fusion(f32[2,128,16,128]{3,2,1,0:T(8,128)S(1)} %get-tuple-element.50, bf16[2,128,16,128]{3,2,0,1:T(8,128)(2,1)S(1)} %fusion.9, bf16[128,128]{1,0:T(8,128)(2,1)S(1)} %copy-done), kind=kOutput, calls=%fused_computation.55 | convolution fusion | flops 138412032 | bytes 5275648 | tf_op jit(solution)/shard_map/dot_general | solution.py:264
  56.0 2.2 %shard_map.111 = f32[2,130,18,128]{3,2,1,0:T(8,128)S(1)} custom-call(f32[2,128,16,128]{3,2,1,0:T(8,128)S(1)} %add_multiply_fusion.grad_ref, f32[9,128]{1,0:T(8,128)S(1)} %copy-done.2), custom_call_target="tpu_custom_call" | custom-call | flops 10782720 | bytes 4792320 | tf_op jit(solution)/shard_map/pallas_call | solution.py:79
  58.5 1.6 %shard_map.112 = f32[9,128]{1,0:T(8,128)S(1)} custom-call(f32[2,130,18,128]{3,2,1,0:T(8,128)S(1)} %maximum_convert_fusion.3.wide_ref, f32[2,128,16,128]{3,2,1,0:T(8,128)S(1)} %add_multiply_fusion.grad_ref), custom_call_target="tpu_custom_call" | custom-call | flops 10782720 | bytes 4792320 | tf_op jit(solution)/shard_map/pallas_call | solution.py:88
  60.1 0.4 collective-permute-start.12
  60.6 1.5 %collective-permute-start.9 = (bf16[2,1,1,18,128]{4,3,1,0,2:T(8,128)(2,1)S(1)}, bf16[2,1,1,18,128]{4,3,1,0,2:T(8,128)(2,1)S(1)}, u32[]{:S(2)}, u32[]{:S(2)}) collective-permute-start(bf16[2,1,1,18,128]{4,3,1,0,2:T(8,128)(2,1)S(1)} %bitcast_select_fusion), channel_id=1, source_target_pairs={{0,2},{2,0},{1,3},{3,1},{4,6},{6,4},{5,7},{7,5},{8,10},{10,8},{9,1... | collective-permute-start | bytes 27656 | tf_op jit(solution)/shard_map/ppermute | solution.py:129
  62.1 2.2 %collective-permute-done.9 = bf16[2,1,1,18,128]{4,3,1,0,2:T(8,128)(2,1)S(1)} collective-permute-done((bf16[2,1,1,18,128]{4,3,1,0,2:T(8,128)(2,1)S(1)}, bf16[2,1,1,18,128]{4,3,1,0,2:T(8,128)(2,1)S(1)}, u32[]{:S(2)}, u32[]{:S(2)}) %collective-permute-start.9) | collective-permute-done | bytes 9248 | tf_op jit(solution)/shard_map/ppermute | solution.py:129
  64.5 3.2 %collective-permute-done.12 = f32[274,128]{1,0:T(8,128)S(1)} collective-permute-done((f32[274,128]{1,0:T(8,128)S(1)}, f32[274,128]{1,0:T(8,128)S(1)}, u32[]{:S(2)}, u32[]{:S(2)}) %collective-permute-start.12) | collective-permute-done | bytes 140320 | tf_op jit(solution)/shard_map/ppermute | solution.py:109
  68.0 4.9 %collective-permute-done.13 = f32[274,128]{1,0:T(8,128)S(1)} collective-permute-done((f32[274,128]{1,0:T(8,128)S(1)}, f32[274,128]{1,0:T(8,128)S(1)}, u32[]{:S(2)}, u32[]{:S(2)}) %collective-permute-start.13) | collective-permute-done | bytes 140320 | tf_op jit(solution)/shard_map/ppermute | solution.py:109
  72.9 1.4 %collective-permute-start.14 = (f32[274,128]{1,0:T(8,128)S(1)}, f32[274,128]{1,0:T(8,128)S(1)}, u32[]{:S(2)}, u32[]{:S(2)}) collective-permute-start(f32[274,128]{1,0:T(8,128)S(1)} %add.190), channel_id=1, source_target_pairs={{0,4},{1,5},{2,6},{3,7},{4,0},{5,1},{6,2},{7,3},{8,12},{9,13},{10,... | collective-permute-start | bytes 420872 | tf_op jit(solution)/shard_map/ppermute | solution.py:109
  74.3 0.4 fusion.38
  74.9 0.7 collective-permute-start.10
  75.7 4.1 %collective-permute-start.11 = (bf16[2,128,1,128]{3,0,1,2:T(2,128)(2,1)S(1)}, bf16[2,128,1,128]{3,0,1,2:T(2,128)(2,1)S(1)}, u32[]{:S(2)}, u32[]{:S(2)}) collective-permute-start(bf16[2,128,1,128]{3,0,1,2:T(2,128)(2,1)S(1)} %copy.135), channel_id=1, source_target_pairs={{4,0},{8,4},{12,8},{16,12},{20,16},{24,20},{28,24},{0,28},{5,1},{9... | collective-permute-start | bytes 196616 | tf_op jit(solution)/shard_map/ppermute | solution.py:147
  79.8 1.7 %collective-permute-start.15 = (f32[274,128]{1,0:T(8,128)S(1)}, f32[274,128]{1,0:T(8,128)S(1)}, u32[]{:S(2)}, u32[]{:S(2)}) collective-permute-start(f32[274,128]{1,0:T(8,128)S(1)} %add.191), channel_id=1, source_target_pairs={{0,2},{1,3},{2,0},{3,1},{4,6},{5,7},{6,4},{7,5},{8,10},{9,11},{10,... | collective-permute-start | bytes 420872 | tf_op jit(solution)/shard_map/ppermute | solution.py:109
  81.5 0.4 collective-permute-done.10
  82.0 2.9 %collective-permute-done.15 = f32[274,128]{1,0:T(8,128)S(1)} collective-permute-done((f32[274,128]{1,0:T(8,128)S(1)}, f32[274,128]{1,0:T(8,128)S(1)}, u32[]{:S(2)}, u32[]{:S(2)}) %collective-permute-start.15) | collective-permute-done | bytes 140320 | tf_op jit(solution)/shard_map/ppermute | solution.py:109
  85.1 0.6 fusion.5
  85.7 1.2 %copy.143 = bf16[2,128,16,128]{3,2,1,0:T(8,128)(2,1)} copy(bf16[2,128,16,128]{3,2,0,1:T(8,128)(2,1)S(1)} %fusion.5) | data formatting | bytes 2097152
  86.9 0.7 slice_multiply_fusion.18
  87.5 0.6 slice_multiply_fusion.20
  (71 shorter events, 4.5 us)
Async XLA Ops:
  0.6 19.1 %copy-start = (bf16[128,128]{1,0:T(8,128)(2,1)S(1)}, bf16[128,128]{1,0:T(8,128)(2,1)}, u32[]{:S(2)}) copy-start(bf16[128,128]{1,0:T(8,128)(2,1)} %param.10) | copy-start | bytes 98308
  0.6 10.8 %copy-start.3 = (bf16[2,128,16,128]{3,2,1,0:T(8,128)(2,1)S(1)}, bf16[2,128,16,128]{3,2,1,0:T(8,128)(2,1)}, u32[]{:S(2)}) copy-start(bf16[2,128,16,128]{3,2,1,0:T(8,128)(2,1)} %param.7) | copy-start | bytes 3145732
  2.2 8.8 %collective-permute-start = (bf16[2,128,1,128]{3,1,0,2:T(8,128)(2,1)S(1)}, bf16[2,128,1,128]{3,1,0,2:T(8,128)(2,1)S(1)}, u32[]{:S(2)}, u32[]{:S(2)}) collective-permute-start(bf16[2,128,1,128]{3,1,0,2:T(8,128)(2,1)S(1)} %bitcast.181), channel_id=1, source_target_pairs={{0,4},{4,8},{8,12},{12,16},{16,20},{20,24},{24,28},{28,0},{1,5},{5... | collective-permute-start | bytes 196616 | tf_op jit(solution)/shard_map/ppermute | solution.py:146
  5.2 6.0 %collective-permute-start.1 = (bf16[2,128,1,128]{3,1,0,2:T(8,128)(2,1)S(1)}, bf16[2,128,1,128]{3,1,0,2:T(8,128)(2,1)S(1)}, u32[]{:S(2)}, u32[]{:S(2)}) collective-permute-start(bf16[2,128,1,128]{3,1,0,2:T(8,128)(2,1)S(1)} %bitcast.180), channel_id=1, source_target_pairs={{4,0},{8,4},{12,8},{16,12},{20,16},{24,20},{28,24},{0,28},{5,1},{9... | collective-permute-start | bytes 196616 | tf_op jit(solution)/shard_map/ppermute | solution.py:147
  11.5 2.7 %copy-start.2 = (f32[9,128]{1,0:T(8,128)S(1)}, f32[9,128]{1,0:T(8,128)}, u32[]{:S(2)}) copy-start(f32[9,128]{1,0:T(8,128)} %k_ref.3) | copy-start | bytes 13828
  12.5 3.8 %collective-permute-start.2 = (bf16[2,1,1,18,128]{4,3,1,0,2:T(8,128)(2,1)S(1)}, bf16[2,1,1,18,128]{4,3,1,0,2:T(8,128)(2,1)S(1)}, u32[]{:S(2)}, u32[]{:S(2)}) collective-permute-start(bf16[2,1,1,18,128]{4,3,1,0,2:T(8,128)(2,1)S(1)} %slice_select_fusion.1), channel_id=1, source_target_pairs={{0,2},{2,0},{1,3},{3,1},{4,6},{6,4},{5,7},{7,5},{8,10},{10,8},{9,1... | collective-permute-start | bytes 27656 | tf_op jit(solution)/shard_map/ppermute | solution.py:129
  19.7 1.4 %copy-start.1 = (f32[9,128]{1,0:T(8,128)S(1)}, f32[9,128]{1,0:T(8,128)}, u32[]{:S(2)}) copy-start(f32[9,128]{1,0:T(8,128)} %k_ref.2) | copy-start | bytes 13828
  20.4 7.8 %collective-permute-start.3 = (bf16[2,128,2,128]{3,2,0,1:T(2,128)(2,1)S(1)}, bf16[2,128,2,128]{3,2,0,1:T(2,128)(2,1)S(1)}, u32[]{:S(2)}, u32[]{:S(2)}) collective-permute-start(bf16[2,128,2,128]{3,2,0,1:T(2,128)(2,1)S(1)} %get-tuple-element.64), channel_id=1, source_target_pairs={{0,4},{4,8},{8,12},{12,16},{16,20},{20,24},{24,28},{28,0},{1,5},{5... | collective-permute-start | bytes 393224 | tf_op jit(solution)/shard_map/ppermute | solution.py:146
  21.1 7.2 %collective-permute-start.4 = (bf16[2,128,2,128]{3,2,0,1:T(2,128)(2,1)S(1)}, bf16[2,128,2,128]{3,2,0,1:T(2,128)(2,1)S(1)}, u32[]{:S(2)}, u32[]{:S(2)}) collective-permute-start(bf16[2,128,2,128]{3,2,0,1:T(2,128)(2,1)S(1)} %get-tuple-element.65), channel_id=1, source_target_pairs={{4,0},{8,4},{12,8},{16,12},{20,16},{24,20},{28,24},{0,28},{5,1},{9... | collective-permute-start | bytes 393224 | tf_op jit(solution)/shard_map/ppermute | solution.py:147
  29.5 3.9 %collective-permute-start.5 = (bf16[2,2,1,20,128]{4,3,0,1,2:T(8,128)(2,1)S(1)}, bf16[2,2,1,20,128]{4,3,0,1,2:T(8,128)(2,1)S(1)}, u32[]{:S(2)}, u32[]{:S(2)}) collective-permute-start(bf16[2,2,1,20,128]{4,3,0,1,2:T(8,128)(2,1)S(1)} %slice_select_fusion), channel_id=1, source_target_pairs={{0,2},{2,0},{1,3},{3,1},{4,6},{6,4},{5,7},{7,5},{8,10},{10,8},{9,1... | collective-permute-start | bytes 61448 | tf_op jit(solution)/shard_map/ppermute | solution.py:129
  34.2 2.5 %copy-start.4 = (bf16[2,128,16,128]{3,2,1,0:T(8,128)(2,1)S(1)}, bf16[2,128,16,128]{3,2,1,0:T(8,128)(2,1)}, u32[]{:S(2)}) copy-start(bf16[2,128,16,128]{3,2,1,0:T(8,128)(2,1)} %param.8) | copy-start | bytes 3145732
  34.3 2.5 %copy-start.5 = (bf16[128,128]{1,0:T(8,128)(2,1)S(1)}, bf16[128,128]{1,0:T(8,128)(2,1)}, u32[]{:S(2)}) copy-start(bf16[128,128]{1,0:T(8,128)(2,1)} %param.12) | copy-start | bytes 98308
  40.7 3.9 %collective-permute-start.6 = (bf16[2,2,1,20,128]{4,3,0,1,2:T(8,128)(2,1)S(1)}, bf16[2,2,1,20,128]{4,3,0,1,2:T(8,128)(2,1)S(1)}, u32[]{:S(2)}, u32[]{:S(2)}) collective-permute-start(bf16[2,2,1,20,128]{4,3,0,1,2:T(8,128)(2,1)S(1)} %get-tuple-element.53), channel_id=1, source_target_pairs={{0,2},{2,0},{1,3},{3,1},{4,6},{6,4},{5,7},{7,5},{8,10},{10,8},{9,1... | collective-permute-start | bytes 61448 | tf_op jit(solution)/shard_map/ppermute | solution.py:129
  45.2 7.7 %collective-permute-start.7 = (bf16[2,128,2,128]{3,2,0,1:T(2,128)(2,1)S(1)}, bf16[2,128,2,128]{3,2,0,1:T(2,128)(2,1)S(1)}, u32[]{:S(2)}, u32[]{:S(2)}) collective-permute-start(bf16[2,128,2,128]{3,2,0,1:T(2,128)(2,1)S(1)} %fusion.41), channel_id=1, source_target_pairs={{0,4},{4,8},{8,12},{12,16},{16,20},{20,24},{24,28},{28,0},{1,5},{5... | collective-permute-start | bytes 393224 | tf_op jit(solution)/shard_map/ppermute | solution.py:146
  45.4 7.5 %collective-permute-start.8 = (bf16[2,128,2,128]{3,2,0,1:T(2,128)(2,1)S(1)}, bf16[2,128,2,128]{3,2,0,1:T(2,128)(2,1)S(1)}, u32[]{:S(2)}, u32[]{:S(2)}) collective-permute-start(bf16[2,128,2,128]{3,2,0,1:T(2,128)(2,1)S(1)} %fusion.40), channel_id=1, source_target_pairs={{4,0},{8,4},{12,8},{16,12},{20,16},{24,20},{28,24},{0,28},{5,1},{9... | collective-permute-start | bytes 393224 | tf_op jit(solution)/shard_map/ppermute | solution.py:147
  60.1 7.6 %collective-permute-start.12 = (f32[274,128]{1,0:T(8,128)S(1)}, f32[274,128]{1,0:T(8,128)S(1)}, u32[]{:S(2)}, u32[]{:S(2)}) collective-permute-start(f32[274,128]{1,0:T(8,128)S(1)} %pad_maximum_fusion.2), channel_id=1, source_target_pairs={{0,16},{1,17},{2,18},{3,19},{4,20},{5,21},{6,22},{7,23},{8,24},{9,... | collective-permute-start | bytes 420872 | tf_op jit(solution)/shard_map/ppermute | solution.py:109
  60.6 3.7 %collective-permute-start.9 = (bf16[2,1,1,18,128]{4,3,1,0,2:T(8,128)(2,1)S(1)}, bf16[2,1,1,18,128]{4,3,1,0,2:T(8,128)(2,1)S(1)}, u32[]{:S(2)}, u32[]{:S(2)}) collective-permute-start(bf16[2,1,1,18,128]{4,3,1,0,2:T(8,128)(2,1)S(1)} %bitcast_select_fusion), channel_id=1, source_target_pairs={{0,2},{2,0},{1,3},{3,1},{4,6},{6,4},{5,7},{7,5},{8,10},{10,8},{9,1... | collective-permute-start | bytes 27656 | tf_op jit(solution)/shard_map/ppermute | solution.py:129
  67.8 5.2 %collective-permute-start.13 = (f32[274,128]{1,0:T(8,128)S(1)}, f32[274,128]{1,0:T(8,128)S(1)}, u32[]{:S(2)}, u32[]{:S(2)}) collective-permute-start(f32[274,128]{1,0:T(8,128)S(1)} %fusion.63), channel_id=1, source_target_pairs={{0,8},{1,9},{2,10},{3,11},{4,12},{5,13},{6,14},{7,15},{8,0},{9,1},... | collective-permute-start | bytes 420872 | tf_op jit(solution)/shard_map/ppermute | solution.py:109
  72.9 6.8 %collective-permute-start.14 = (f32[274,128]{1,0:T(8,128)S(1)}, f32[274,128]{1,0:T(8,128)S(1)}, u32[]{:S(2)}, u32[]{:S(2)}) collective-permute-start(f32[274,128]{1,0:T(8,128)S(1)} %add.190), channel_id=1, source_target_pairs={{0,4},{1,5},{2,6},{3,7},{4,0},{5,1},{6,2},{7,3},{8,12},{9,13},{10,... | collective-permute-start | bytes 420872 | tf_op jit(solution)/shard_map/ppermute | solution.py:109
  74.9 7.0 %collective-permute-start.10 = (bf16[2,128,1,128]{3,0,1,2:T(2,128)(2,1)S(1)}, bf16[2,128,1,128]{3,0,1,2:T(2,128)(2,1)S(1)}, u32[]{:S(2)}, u32[]{:S(2)}) collective-permute-start(bf16[2,128,1,128]{3,0,1,2:T(2,128)(2,1)S(1)} %copy.132), channel_id=1, source_target_pairs={{0,4},{4,8},{8,12},{12,16},{16,20},{20,24},{24,28},{28,0},{1,5},{5... | collective-permute-start | bytes 196616 | tf_op jit(solution)/shard_map/ppermute | solution.py:146
  75.7 6.2 %collective-permute-start.11 = (bf16[2,128,1,128]{3,0,1,2:T(2,128)(2,1)S(1)}, bf16[2,128,1,128]{3,0,1,2:T(2,128)(2,1)S(1)}, u32[]{:S(2)}, u32[]{:S(2)}) collective-permute-start(bf16[2,128,1,128]{3,0,1,2:T(2,128)(2,1)S(1)} %copy.135), channel_id=1, source_target_pairs={{4,0},{8,4},{12,8},{16,12},{20,16},{24,20},{28,24},{0,28},{5,1},{9... | collective-permute-start | bytes 196616 | tf_op jit(solution)/shard_map/ppermute | solution.py:147
  79.8 5.2 %collective-permute-start.15 = (f32[274,128]{1,0:T(8,128)S(1)}, f32[274,128]{1,0:T(8,128)S(1)}, u32[]{:S(2)}, u32[]{:S(2)}) collective-permute-start(f32[274,128]{1,0:T(8,128)S(1)} %add.191), channel_id=1, source_target_pairs={{0,2},{1,3},{2,0},{3,1},{4,6},{5,7},{6,4},{7,5},{8,10},{9,11},{10,... | collective-permute-start | bytes 420872 | tf_op jit(solution)/shard_map/ppermute | solution.py:109
  85.0 1.9 %collective-permute-start.16 = (f32[274,128]{1,0:T(8,128)S(1)}, f32[274,128]{1,0:T(8,128)S(1)}, u32[]{:S(2)}, u32[]{:S(2)}) collective-permute-start(f32[274,128]{1,0:T(8,128)S(1)} %add.192), channel_id=1, source_target_pairs={{0,1},{1,0},{2,3},{3,2},{4,5},{5,4},{6,7},{7,6},{8,9},{9,8},{10,11... | collective-permute-start | bytes 420872 | tf_op jit(solution)/shard_map/ppermute | solution.py:109
